TPU v7x, 512 devices: a whole 4x8x8 slice. The times are simulated.
512 devices in a mesh: dp: 64 (over z, y_hi, core), seq: 8 (over y_lo, x).
Axes of the slice: x: 4, y: 8 (y_hi: 4, y_lo: 2; y = y_hi * 2 + y_lo), z: 8, core: 2. Of those that a mesh axis runs over, the one named last changes fastest.
Arguments:
- tokens: bfloat16 [1024, 4096], P('seq', 'dp'), may hold values from -6 to 6
- in_weight: bfloat16 [2, 4096, 8192], P(None, 'seq', 'dp'), may hold values from -0.09375 to 0.09375
- conv_weight: bfloat16 [4, 8192], P(None, 'dp'), may hold values from -0.5 to 0.5
- conv_bias: bfloat16 [8192], P('dp'), may hold values from -1 to 1
- out_weight: bfloat16 [8192, 4096], P('dp', 'seq'), may hold values from -0.0625 to 0.0625
- grad_out: bfloat16 [1024, 4096], P('seq', 'dp'), may hold values from -6 to 6
Outputs:
- output: bfloat16 [1024, 4096], P('seq', 'dp')
- grad_tokens: bfloat16 [1024, 4096], P('seq', 'dp')
- grad_in_weight: float32 [2, 4096, 8192], P(None, 'seq', 'dp')
- grad_out_weight: float32 [8192, 4096], P('dp', 'seq')
- grad_conv_weight: float32 [4, 8192], P(None, 'dp')
- grad_conv_bias: float32 [8192], P('dp')
All inputs are finite; a program needn't handle non-finite values.
Results may differ from a plain program's by a relative error of at most 0.012.
Values may be sent and summed in bfloat16 or wider, within the bound.
No kernel may reach another device: no remote copies, remote signals or barrier semaphores. Data moves between devices by JAX's collectives and lax.ppermute only.
A program may use at most 64 MiB of HBM per device.

v0:
```python
import jax
import jax.numpy as jnp
from jax import lax
from jax.sharding import PartitionSpec as P


def from_behind(block, axis, distance):
    devices = range(lax.axis_size(axis))
    route = [(i - distance, i) for i in devices if i - distance in devices]
    return lax.ppermute(block, axis, route)


def silu_parts(value):
    sig = jax.nn.sigmoid(value)
    return (value * sig, sig * (1.0 + value * (1.0 - sig)))


def on_device(tokens, in_weight, conv_weight, conv_bias, out_weight, grad_out):
    in_full, out_full = (
        lax.all_gather(in_weight, "seq", axis=1, tiled=True),
        lax.all_gather(out_weight, "seq", axis=1, tiled=True),
    )
    whole = lax.all_gather(tokens, "dp", axis=1, tiled=True)
    tok_rows = whole.shape[0]
    taps = conv_weight.shape[0]
    mixed = jnp.einsum("td,pde->tpe", whole, in_full, preferred_element_type=jnp.float32).astype(
        jnp.bfloat16
    )
    inner = mixed[:, 0, :]
    gate_in = mixed[:, 1, :]
    rim = from_behind(inner[tok_rows - (taps - 1) :], "seq", 1)
    padded = jnp.concatenate([rim, inner], axis=0)
    conv = jnp.broadcast_to(conv_bias.astype(jnp.float32)[None, :], inner.shape)
    for lag in range(taps):
        conv = conv + conv_weight[lag].astype(jnp.float32)[None, :] * padded[
            lag : lag + tok_rows
        ].astype(jnp.float32)
    act, act_slope = silu_parts(conv)
    gate, gate_slope = silu_parts(gate_in.astype(jnp.float32))
    hidden = (act * gate).astype(jnp.bfloat16)
    columns = lax.all_to_all(out_full, "dp", split_axis=1, concat_axis=0, tiled=True)
    output = jnp.dot(
        lax.all_gather(hidden, "dp", axis=1, tiled=True),
        columns,
        preferred_element_type=jnp.float32,
    ).astype(jnp.bfloat16)
    upstream = lax.all_gather(grad_out, "dp", axis=1, tiled=True)
    back = lax.dot_general(
        upstream, out_full, (((1,), (1,)), ((), ())), preferred_element_type=jnp.float32
    )
    grad_conv = (back * gate * act_slope).astype(jnp.bfloat16)
    grad_gate = (back * act * gate_slope).astype(jnp.bfloat16)
    ahead_rim = from_behind(grad_conv[: taps - 1], "seq", -1)
    ahead = jnp.concatenate([grad_conv, ahead_rim], axis=0)
    grad_inner = jnp.zeros(inner.shape, jnp.float32)
    for lag in range(taps):
        shift_start = taps - 1 - lag
        grad_inner = grad_inner + conv_weight[lag].astype(jnp.float32)[None, :] * ahead[
            shift_start : shift_start + tok_rows
        ].astype(jnp.float32)
    grad_inner = grad_inner.astype(jnp.bfloat16)
    conv_float = grad_conv.astype(jnp.float32)
    tap_rows = []
    for lag in range(taps):
        tap_rows.append(
            jnp.sum(conv_float * padded[lag : lag + tok_rows].astype(jnp.float32), axis=0)
        )
    tap_grads, bias_grads = lax.psum(
        (jnp.stack(tap_rows, axis=0), jnp.sum(conv_float, axis=0)), "seq"
    )
    branch_grads = jnp.stack([grad_inner, grad_gate], axis=1)
    term_in = jnp.einsum("td,tpe->pde", whole, branch_grads, preferred_element_type=jnp.float32)
    term_out = lax.dot_general(
        hidden, upstream, (((0,), (0,)), ((), ())), preferred_element_type=jnp.float32
    )
    grad_in_weight, grad_out_weight = (
        lax.psum_scatter(
            term_in.astype(jnp.bfloat16), "seq", scatter_dimension=1, tiled=True
        ).astype(jnp.float32),
        lax.psum_scatter(
            term_out.astype(jnp.bfloat16), "seq", scatter_dimension=1, tiled=True
        ).astype(jnp.float32),
    )
    feature_rows = lax.all_to_all(in_full, "dp", split_axis=1, concat_axis=2, tiled=True)
    grad_tokens = jnp.einsum(
        "tpe,pde->td",
        lax.all_gather(branch_grads, "dp", axis=2, tiled=True),
        feature_rows,
        preferred_element_type=jnp.float32,
    )
    grad_tokens = grad_tokens.astype(jnp.bfloat16)
    return (output, grad_tokens, grad_in_weight, grad_out_weight, tap_grads, bias_grads)


def solution(mesh):
    return jax.shard_map(
        on_device,
        mesh=mesh,
        in_specs=(
            P("seq", "dp"),
            P(None, "seq", "dp"),
            P(None, "dp"),
            P("dp"),
            P("dp", "seq"),
            P("seq", "dp"),
        ),
        out_specs=(
            P("seq", "dp"),
            P("seq", "dp"),
            P(None, "seq", "dp"),
            P("dp", "seq"),
            P(None, "dp"),
            P("dp"),
        ),
        check_vma=False,
    )
```

profile of v0, /device:TPU:1, one launch (start us, length us, event | category | flops | bytes accessed | tf_op | source)
XLA Modules:
  0.0 598.2 jit_solution(10952429365601624407)
XLA Ops:
  7.2 0.0 all-gather.7.cloned.1.call-start
  7.2 0.7 all-gather.7.cloned.1.call-update
  7.9 0.0 all-gather.9.cloned.1.call-start
  7.9 0.7 all-gather.9.cloned.1.call-update
  8.7 0.0 all-gather.13.cloned.1.call-start
  8.7 1.7 copy.20
  10.4 0.0 all-gather.13.cloned.1.call-update
  10.4 0.0 all-gather.15.cloned.1.call-start
  10.4 0.5 all-gather.15.cloned.1.call-update
  11.0 0.0 reduce-scatter.5.cloned.1.call-start
  11.0 0.7 convert_element_type.86
  11.7 0.8 bitcast_convert_fusion.3
  12.5 87.9 %all-gather.7.cloned.1.call-done = bf16[128,4096]{0,1:T(8,128)(2,1)} async-done(((bf16[128,64]{0,1:T(8,128)(2,1)}), bf16[128,4096]{0,1:T(8,128)(2,1)}) %all-gather.7.cloned.1.call-update) | async-done | bytes 1048592 | tf_op jit(solution)/shard_map/all_gather | solution.py:23
  100.4 40.0 %all-gather.9.cloned.1.call-done = bf16[2,4096,128]{2,1,0:T(8,128)(2,1)} async-done(((bf16[2,512,128]{2,1,0:T(8,128)(2,1)}), bf16[2,4096,128]{2,1,0:T(8,128)(2,1)}) %all-gather.9.cloned.1.call-update) | async-done | bytes 2097168 | tf_op jit(solution)/shard_map/all_gather | solution.py:20
  140.4 2.5 convolution_convert_fusion.2
  142.9 2.4 collective-permute-start
  145.3 41.1 %all-gather.13.cloned.1.call-done = bf16[128,4096]{0,1:T(8,128)(2,1)} async-done(((bf16[128,512]{0,1:T(8,128)(2,1)}), bf16[128,4096]{0,1:T(8,128)(2,1)}) %all-gather.13.cloned.1.call-update) | async-done | bytes 1048592 | tf_op jit(solution)/shard_map/all_gather | solution.py:21
  186.4 91.0 %all-gather.15.cloned.1.call-done = bf16[128,4096]{0,1:T(8,128)(2,1)} async-done(((bf16[128,64]{0,1:T(8,128)(2,1)}), bf16[128,4096]{0,1:T(8,128)(2,1)}) %all-gather.15.cloned.1.call-update) | async-done | bytes 1048592 | tf_op jit(solution)/shard_map/all_gather | solution.py:47
  277.3 0.0 copy-start.2
  277.3 0.0 collective-permute-done
  277.3 2.1 convert_reduce_fusion
  279.5 0.0 copy-start.1
  279.5 0.1 fusion.28
  279.6 0.0 copy-start.3
  279.6 0.0 copy-done.2
  279.6 1.4 convolution_convert_fusion.1
  281.0 0.0 reduce-scatter.5.cloned.1.call-update
  281.1 0.0 all-gather.11.cloned.1.call-start
  281.1 0.0 copy-done.3
  281.1 0.5 all-gather.11.cloned.1.call-update
  281.7 0.0 reduce-scatter.3.cloned.1.call-start
  281.7 1.3 collective-permute-start.1
  283.0 3.0 collective-permute-done.1
  286.1 0.0 copy-done.1
  286.1 0.0 copy-start
  286.1 2.1 fusion
  288.2 0.0 reduce-scatter.3.cloned.1.call-update
  288.2 0.0 all-gather.17.cloned.1.call-start
  288.3 0.6 pad_maximum_fusion
  288.9 0.1 all-gather.17.cloned.1.call-update
  289.0 0.0 copy-done
  289.0 17.8 %copy.22 = bf16[2,4096,128]{2,0,1:T(2,128)(2,1)S(1)} copy(bf16[2,4096,128]{2,1,0:T(8,128)(2,1)S(1)} %copy-done) | data formatting | bytes 4194304 | tf_op jit(solution)/shard_map/all_gather | solution.py:20
  306.8 62.8 %all_to_all.37 = bf16[2,4096,128]{2,0,1:T(2,128)(2,1)S(1)} all-to-all(bf16[2,4096,128]{2,0,1:T(2,128)(2,1)S(1)} %copy.22), channel_id=1, replica_groups=mesh['dp'=64,'seq'=8] {'dp'}, dimensions={1} | all-to-all | bytes 4194304 | tf_op jit(solution)/shard_map/all_to_all | solution.py:84
  369.6 13.4 %all-to-all-start = ((bf16[128,64,64]{0,2,1:T(8,128)(2,1)}), bf16[128,64,64]{0,2,1:T(8,128)(2,1)S(1)}, u32[]{:S(2)}, u32[]{:S(2)}) async-start(bf16[128,64,64]{0,2,1:T(8,128)(2,1)} %bitcast.74), calls=%async_computation | async-start | bytes 2097152 | tf_op jit(solution)/shard_map/all_to_all | solution.py:41
  383.0 33.1 %all-reduce = (f32[4,128]{1,0:T(4,128)}, f32[128]{0:T(128)}) all-reduce(f32[4,128]{1,0:T(4,128)S(1)} %pad_maximum_fusion.3, f32[128]{0:T(128)S(1)} %get-tuple-element.27), channel_id=1, replica_groups=mesh['dp'=64,'seq'=8] {'seq'}, use_global_device_ids=true, to_apply=%region_6.0 | all-reduce | flops 640 | bytes 5120 | tf_op jit(solution)/shard_map/psum | solution.py:68
  416.2 0.0 reduce-scatter.5.cloned.1.call-done
  416.2 1.6 convert_element_type.108
  417.8 2.7 copy.33
  420.5 2.8 all_to_all.34
  423.3 0.0 all-to-all-done
  423.3 25.8 %all-gather.11.cloned.1.call-done = bf16[128,8192]{1,0:T(8,128)(2,1)} async-done(((bf16[128,128]{1,0:T(8,128)(2,1)}), bf16[128,8192]{1,0:T(8,128)(2,1)}) %all-gather.11.cloned.1.call-update) | async-done | bytes 2097168 | tf_op jit(solution)/shard_map/all_gather | solution.py:43
  449.1 3.0 convolution_convert_fusion.3
  452.2 40.1 %reduce-scatter.3.cloned.1.call-done = bf16[2,512,128]{1,2,0:T(8,128)(2,1)} async-done(((bf16[2,4096,128]{1,2,0:T(8,128)(2,1)}), bf16[2,512,128]{1,2,0:T(8,128)(2,1)}) %reduce-scatter.3.cloned.1.call-update) | async-done | bytes 262160 | tf_op jit(solution)/shard_map/reduce_scatter | solution.py:77
  492.3 1.9 copy.25
  494.2 92.8 %all-gather.17.cloned.1.call-done = bf16[128,2,8192]{2,0,1:T(8,128)(2,1)} async-done(((bf16[128,2,128]{2,0,1:T(8,128)(2,1)}), bf16[128,2,8192]{2,0,1:T(8,128)(2,1)}) %all-gather.17.cloned.1.call-update) | async-done | bytes 4194320 | tf_op jit(solution)/shard_map/all_gather | solution.py:87
  587.0 4.4 fusion.1
  (5 shorter events, 0.1 us)
Async XLA Ops:
  7.2 93.2 %all-gather.7.cloned.1.call-start = ((), (), s32[]{:S(2)}) async-start(), calls=%async_computation.4 | async-start | bytes 1064960 | tf_op jit(solution)/shard_map/all_gather | solution.py:23
  7.9 132.4 %all-gather.9.cloned.1.call-start = ((), (), s32[]{:S(2)}) async-start(), calls=%async_computation.5 | async-start | bytes 2359296 | tf_op jit(solution)/shard_map/all_gather | solution.py:20
  8.7 177.7 %all-gather.13.cloned.1.call-start = ((), (), s32[]{:S(2)}) async-start(), calls=%async_computation.7 | async-start | bytes 1179648 | tf_op jit(solution)/shard_map/all_gather | solution.py:21
  10.4 267.0 %all-gather.15.cloned.1.call-start = ((), (), s32[]{:S(2)}) async-start(), calls=%async_computation.8 | async-start | bytes 1064960 | tf_op jit(solution)/shard_map/all_gather | solution.py:47
  11.0 405.2 %reduce-scatter.5.cloned.1.call-start = ((), (), s32[]{:S(2)}) async-start(), calls=%async_computation.11 | async-start | bytes 1179648 | tf_op jit(solution)/shard_map/reduce_scatter | solution.py:80
  142.9 134.5 %collective-permute-start = (bf16[3,128]{1,0:T(4,128)(2,1)S(1)}, bf16[3,128]{1,0:T(4,128)(2,1)S(1)}, u32[]{:S(2)}, u32[]{:S(2)}) collective-permute-start(bf16[3,128]{1,0:T(4,128)(2,1)S(1)} %slice_bitcast_fusion.2), channel_id=1, source_target_pairs={{0,1},{1,2},{2,3},{3,4},{4,5},{5,6},{6,7},{8,9},{9,10},{10,11},{11... | collective-permute-start | bytes 2312 | tf_op jit(solution)/shard_map/ppermute | solution.py:10
  277.3 2.2 copy-start.2
  279.5 6.6 %copy-start.1 = (bf16[128,4096]{0,1:T(8,128)(2,1)S(1)}, bf16[128,4096]{0,1:T(8,128)(2,1)}, u32[]{:S(2)}) copy-start(bf16[128,4096]{0,1:T(8,128)(2,1)} %all-gather.7.cloned.1.call-done) | copy-start | bytes 3145732
  279.6 1.5 copy-start.3
  281.1 168.0 %all-gather.11.cloned.1.call-start = ((), (), s32[]{:S(2)}) async-start(), calls=%async_computation.6 | async-start | bytes 2129920 | tf_op jit(solution)/shard_map/all_gather | solution.py:43
  281.7 210.6 %reduce-scatter.3.cloned.1.call-start = ((), (), s32[]{:S(2)}) async-start(), calls=%async_computation.10 | async-start | bytes 2359296 | tf_op jit(solution)/shard_map/reduce_scatter | solution.py:77
  281.7 4.3 collective-permute-start.1
  286.1 2.9 copy-start
  288.2 298.8 %all-gather.17.cloned.1.call-start = ((), (), s32[]{:S(2)}) async-start(), calls=%async_computation.9 | async-start | bytes 4259840 | tf_op jit(solution)/shard_map/all_gather | solution.py:87
  369.6 53.7 %all-to-all-start = ((bf16[128,64,64]{0,2,1:T(8,128)(2,1)}), bf16[128,64,64]{0,2,1:T(8,128)(2,1)S(1)}, u32[]{:S(2)}, u32[]{:S(2)}) async-start(bf16[128,64,64]{0,2,1:T(8,128)(2,1)} %bitcast.74), calls=%async_computation | async-start | bytes 2097152 | tf_op jit(solution)/shard_map/all_to_all | solution.py:41
Sparse Core Ops, SparseCore 0:
  11.4 88.9 all-gather.6
  102.4 37.8 all-gather.8
  143.0 43.3 all-gather.12
  189.6 87.7 all-gather.14
  281.2 35.2 reduce-scatter.4
  320.2 128.8 all-gather.10
  452.0 40.2 reduce-scatter.2
  495.5 91.4 all-gather.16
where the time goes:
time: 599 us; the launch traced here: 598 us
  waiting for transfers between devices  424 us (71%)
  blocking collectives  95.9 us (16%)
  local copies, waits for them, and re-layouts  26.9 us (4%)
  starting transfers between devices  17.5 us (3%)
  matrix products  15.6 us (3%)
  between operations  14.3 us (2%)
    all_gather x1, waiting for transfers between devices, on_device(): lax.all_gather(branch_grads, 'dp', axis=2, tiled=True)  92.8 us
    all_gather x1, waiting for transfers between devices, on_device(): upstream = lax.all_gather(grad_out, 'dp', axis=1, tiled=True)  91 us
    all_gather x1, waiting for transfers between devices, on_device(): whole = lax.all_gather(tokens, 'dp', axis=1, tiled=True)  87.9 us
    all_to_all x1, blocking collectives, on_device(): lax.all_to_all(in_full, 'dp', split_axis=1, concat_axis=2, tiled=True)  62.8 us
    all_gather x1, waiting for transfers between devices, on_device(): lax.all_gather(out_weight, 'seq', axis=1, tiled=True)  41.1 us
    reduce_scatter x1, waiting for transfers between devices, on_device(): lax.psum_scatter(term_in.astype(jnp.bfloat16), 'seq', scatter_dimension=1...  40.1 us
    all_gather x1, waiting for transfers between devices, on_device(): lax.all_gather(in_weight, 'seq', axis=1, tiled=True)  40 us
    psum x1, blocking collectives, on_device(): lax.psum((jnp.stack(tap_rows, axis=0), jnp.sum(conv_float, axis=0)), 'seq')  33.1 us
  transfers between devices with their start and end apart: 11, of which 8 were waited for; matrix products, arithmetic and copies ran while one was open for 6% of the time, Pallas kernels for 0%

commit v1 on v0

--- a/solution.py
+++ b/solution.py
@@ -16,11 +16,14 @@
 
 
 def on_device(tokens, in_weight, conv_weight, conv_bias, out_weight, grad_out):
-    in_full, out_full = (
-        lax.all_gather(in_weight, "seq", axis=1, tiled=True),
-        lax.all_gather(out_weight, "seq", axis=1, tiled=True),
-    )
-    whole = lax.all_gather(tokens, "dp", axis=1, tiled=True)
+    w_local = jnp.concatenate([in_weight, out_weight.T[None]], axis=0)
+    w_full = lax.all_gather(w_local, "seq", axis=1, tiled=True)
+    in_full = w_full[:2]
+    out_full_t = w_full[2]
+    acts = jnp.stack([tokens, grad_out], axis=1)
+    acts_full = lax.all_gather(acts, "dp", axis=2, tiled=True)
+    whole = acts_full[:, 0]
+    upstream = acts_full[:, 1]
     tok_rows = whole.shape[0]
     taps = conv_weight.shape[0]
     mixed = jnp.einsum("td,pde->tpe", whole, in_full, preferred_element_type=jnp.float32).astype(
@@ -38,16 +41,8 @@
     act, act_slope = silu_parts(conv)
     gate, gate_slope = silu_parts(gate_in.astype(jnp.float32))
     hidden = (act * gate).astype(jnp.bfloat16)
-    columns = lax.all_to_all(out_full, "dp", split_axis=1, concat_axis=0, tiled=True)
-    output = jnp.dot(
-        lax.all_gather(hidden, "dp", axis=1, tiled=True),
-        columns,
-        preferred_element_type=jnp.float32,
-    ).astype(jnp.bfloat16)
-    upstream = lax.all_gather(grad_out, "dp", axis=1, tiled=True)
-    back = lax.dot_general(
-        upstream, out_full, (((1,), (1,)), ((), ())), preferred_element_type=jnp.float32
-    )
+    out_part = jnp.einsum("te,de->dt", hidden, out_full_t, preferred_element_type=jnp.float32)
+    back = jnp.einsum("td,de->te", upstream, out_full_t, preferred_element_type=jnp.float32)
     grad_conv = (back * gate * act_slope).astype(jnp.bfloat16)
     grad_gate = (back * act * gate_slope).astype(jnp.bfloat16)
     ahead_rim = from_behind(grad_conv[: taps - 1], "seq", -1)
@@ -69,26 +64,19 @@
         (jnp.stack(tap_rows, axis=0), jnp.sum(conv_float, axis=0)), "seq"
     )
     branch_grads = jnp.stack([grad_inner, grad_gate], axis=1)
+    tok_part = jnp.einsum("tpe,pde->dt", branch_grads, in_full, preferred_element_type=jnp.float32)
+    reduced = lax.psum_scatter(
+        jnp.stack([out_part, tok_part], axis=1), "dp", scatter_dimension=0, tiled=True
+    )
+    reduced = lax.optimization_barrier(reduced)
+    output = reduced[:, 0].T.astype(jnp.bfloat16)
+    grad_tokens = reduced[:, 1].T.astype(jnp.bfloat16)
     term_in = jnp.einsum("td,tpe->pde", whole, branch_grads, preferred_element_type=jnp.float32)
-    term_out = lax.dot_general(
-        hidden, upstream, (((0,), (0,)), ((), ())), preferred_element_type=jnp.float32
-    )
-    grad_in_weight, grad_out_weight = (
-        lax.psum_scatter(
-            term_in.astype(jnp.bfloat16), "seq", scatter_dimension=1, tiled=True
-        ).astype(jnp.float32),
-        lax.psum_scatter(
-            term_out.astype(jnp.bfloat16), "seq", scatter_dimension=1, tiled=True
-        ).astype(jnp.float32),
-    )
-    feature_rows = lax.all_to_all(in_full, "dp", split_axis=1, concat_axis=2, tiled=True)
-    grad_tokens = jnp.einsum(
-        "tpe,pde->td",
-        lax.all_gather(branch_grads, "dp", axis=2, tiled=True),
-        feature_rows,
-        preferred_element_type=jnp.float32,
-    )
-    grad_tokens = grad_tokens.astype(jnp.bfloat16)
+    term_out_t = jnp.einsum("td,te->de", upstream, hidden, preferred_element_type=jnp.float32)
+    terms = jnp.concatenate([term_in, term_out_t[None]], axis=0).astype(jnp.bfloat16)
+    terms = lax.psum_scatter(terms, "seq", scatter_dimension=1, tiled=True).astype(jnp.float32)
+    grad_in_weight = terms[:2]
+    grad_out_weight = terms[2].T
     return (output, grad_tokens, grad_in_weight, grad_out_weight, tap_grads, bias_grads)
 
 

time: 599 us -> 389 us (0.65)
  waiting for transfers between devices: 424 us -> 315 us
  blocking collectives: 95.9 us -> 15.4 us
  starting transfers between devices: 17.5 us -> 3.91 us
  matrix products: 15.6 us -> 6.55 us
  other arithmetic: 3.89 us -> 10.1 us
  local copies, waits for them, and re-layouts: 26.9 us -> 20.7 us
    all_gather x6 -> x2, waiting for transfers between devices: 378 us -> 118 us  [the longest x1 89 us: on_device(): acts_full = lax.all_gather(acts, 'dp', axis=2, tiled=True)]
    reduce_scatter x2, waiting for transfers between devices: 40.1 us -> 193 us  [the longest x1 156 us: on_device(): lax.psum_scatter(jnp.stack([out_part, tok_part], axis=1), 'dp', scatter_d...]
    all_to_all x1 -> x0, blocking collectives: 62.8 us -> none  [on_device(): lax.all_to_all(in_full, 'dp', split_axis=1, concat_axis=2, tiled=True)]
    all_gather x1 -> x0, local copies, waits for them, and re-layouts: 17.8 us -> none  [on_device(): lax.all_gather(in_weight, 'seq', axis=1, tiled=True)]
    psum x1, blocking collectives: 33.1 us -> 15.4 us  [on_device(): lax.psum((jnp.stack(tap_rows, axis=0), jnp.sum(conv_float, axis=0)), 'seq')]
    all_to_all x1 -> x0, starting transfers between devices: 13.4 us -> none  [on_device(): lax.all_to_all(out_full, 'dp', split_axis=1, concat_axis=0, tiled=True)]
    dot_general x4, matrix products: 11 us -> 3.33 us  [the longest x1 1.68 us: on_device(): jnp.einsum('td,de->te', upstream, out_full_t, preferred_element_type=jnp....]
    unnamed x10, local copies, waits for them, and re-layouts: 3.56 us -> 11.2 us
  transfers between devices with their start and end apart: 11 -> 6, of which waited for: 8 -> 6; matrix products, arithmetic and copies ran while one was open for 6% -> 7% of each run, Pallas kernels for 0% -> 0%
where the time goes in v1:
time: 389 us; the launch traced here: 385 us
  waiting for transfers between devices  315 us (81%)
  local copies, waits for them, and re-layouts  20.7 us (5%)
  blocking collectives  15.4 us (4%)
  between operations  13.9 us (4%)
  other arithmetic  10.1 us (3%)
  matrix products  6.55 us (2%)
  starting transfers between devices  3.91 us (1%)
    reduce_scatter x1, waiting for transfers between devices, on_device(): lax.psum_scatter(jnp.stack([out_part, tok_part], axis=1), 'dp', scatter_d...  156 us
    all_gather x1, waiting for transfers between devices, on_device(): acts_full = lax.all_gather(acts, 'dp', axis=2, tiled=True)  89 us
    reduce_scatter x1, waiting for transfers between devices, on_device(): lax.psum_scatter(terms, 'seq', scatter_dimension=1, tiled=True)  37.2 us
    all_gather x1, waiting for transfers between devices, on_device(): w_full = lax.all_gather(w_local, 'seq', axis=1, tiled=True)  29.2 us
    psum x1, blocking collectives, on_device(): lax.psum((jnp.stack(tap_rows, axis=0), jnp.sum(conv_float, axis=0)), 'seq')  15.4 us
    unnamed x10, local copies, waits for them, and re-layouts  11.2 us
  transfers between devices with their start and end apart: 6, of which 6 were waited for; matrix products, arithmetic and copies ran while one was open for 7% of the time, Pallas kernels for 0%

profile of v1, /device:TPU:1, one launch (start us, length us, event | category | flops | bytes accessed | tf_op | source)
XLA Modules:
  0.0 385.1 jit_solution(3668761456211988924)
XLA Ops:
  7.2 0.0 all-gather.5.cloned.1.call-start
  7.2 0.7 pad_maximum_fusion.8
  8.0 0.6 copy.24
  8.6 0.0 all-gather.5.cloned.1.call-update
  8.6 0.0 all-gather.3.cloned.1.call-start
  8.7 1.0 copy.23
  9.7 1.7 pad_maximum_fusion.2
  11.4 0.0 all-gather.3.cloned.1.call-update
  11.5 0.0 reduce-scatter.5.cloned.1.call-start
  11.5 0.7 convert_element_type.83
  12.2 0.8 bitcast_convert_fusion.3
  13.0 89.0 %all-gather.5.cloned.1.call-done = bf16[128,2,4096]{0,1,2:T(2,128)(2,1)} async-done(((bf16[128,2,64]{0,1,2:T(2,128)(2,1)}), bf16[128,2,4096]{0,1,2:T(2,128)(2,1)}) %all-gather.5.cloned.1.call-update) | async-done | bytes 2097168 | tf_op jit(solution)/shard_map/all_gather | solution.py:24
  102.0 6.5 %fusion.39 = (bf16[128,1,4096]{0,1,2:T(2,128)(2,1)}, bf16[128,1,4096]{0,1,2:T(2,128)(2,1)S(1)}) fusion(bf16[128,2,4096]{0,1,2:T(2,128)(2,1)} %all-gather.5.cloned.1.call-done), kind=kLoop, calls=%fused_computation.79 | loop fusion | bytes 4194304 | tf_op jit(solution)/shard_map/slice | solution.py:25
  108.6 5.4 %copy.32 = bf16[128,1,4096]{2,0,1:T(8,128)(2,1)} copy(bf16[128,1,4096]{0,1,2:T(2,128)(2,1)} %get-tuple-element.36) | data formatting | bytes 2097152
  113.9 3.8 copy.33
  117.7 29.2 %all-gather.3.cloned.1.call-done = bf16[3,4096,128]{2,1,0:T(8,128)(2,1)} async-done(((bf16[3,512,128]{2,1,0:T(8,128)(2,1)}), bf16[3,4096,128]{2,1,0:T(8,128)(2,1)}) %all-gather.3.cloned.1.call-update) | async-done | bytes 3145744 | tf_op jit(solution)/shard_map/all_gather | solution.py:20
  146.9 0.0 copy-start
  146.9 0.0 copy-start.2
  146.9 2.5 fusion.4
  149.4 0.0 copy-start.1
  149.4 2.5 collective-permute-start
  151.9 0.7 collective-permute-done
  152.6 0.0 copy-done
  152.6 1.7 convert_reduce_fusion
  154.3 1.3 collective-permute-start.1
  155.6 0.1 fusion.34
  155.7 0.0 copy-done.2
  155.7 0.5 fusion.1
  156.2 2.7 collective-permute-done.1
  158.9 0.0 copy-done.1
  158.9 0.7 fusion
  159.6 2.0 pad_maximum_fusion.1
  161.6 0.0 reduce-scatter.5.cloned.1.call-update
  161.6 0.0 reduce-scatter.3.cloned.1.call-start
  161.7 0.5 convolution_bitcast_fusion.1
  162.1 0.7 convolution_bitcast_fusion
  162.8 2.2 pad_maximum_fusion
  165.0 0.0 reduce-scatter.3.cloned.1.call-update
  165.1 15.4 %all-reduce = (f32[4,128]{1,0:T(4,128)}, f32[128]{0:T(128)}) all-reduce(f32[4,128]{1,0:T(4,128)S(1)} %pad_maximum_fusion.9, f32[128]{0:T(128)S(1)} %get-tuple-element.27), channel_id=1, replica_groups=mesh['dp'=64,'seq'=8] {'seq'}, use_global_device_ids=true, to_apply=%region_6.0 | all-reduce | flops 640 | bytes 5120 | tf_op jit(solution)/shard_map/psum | solution.py:63
  180.4 37.2 %reduce-scatter.5.cloned.1.call-done = bf16[3,512,128]{1,2,0:T(8,128)(2,1)} async-done(((bf16[3,4096,128]{1,2,0:T(8,128)(2,1)}), bf16[3,512,128]{1,2,0:T(8,128)(2,1)}) %reduce-scatter.5.cloned.1.call-update) | async-done | bytes 393232 | tf_op jit(solution)/shard_map/reduce_scatter | solution.py:77
  217.6 1.0 slice.120
  218.6 1.0 copy.29
  219.6 1.1 convert_element_type.103
  220.7 0.7 slice_bitcast_fusion.3
  221.4 155.7 %reduce-scatter.3.cloned.1.call-done = f32[64,2,128]{2,0,1:T(8,128)} async-done(((f32[4096,2,128]{2,0,1:T(8,128)}), f32[64,2,128]{2,0,1:T(8,128)}) %reduce-scatter.3.cloned.1.call-update) | async-done | bytes 65552 | tf_op jit(solution)/shard_map/reduce_scatter | solution.py:68
  377.1 0.8 convert.17
  378.0 0.6 slice_bitcast_fusion.6
  (5 shorter events, 0.1 us)
Async XLA Ops:
  7.2 94.9 %all-gather.5.cloned.1.call-start = ((), (), s32[]{:S(2)}) async-start(), calls=%async_computation.3 | async-start | bytes 2129920 | tf_op jit(solution)/shard_map/all_gather | solution.py:24
  8.6 138.3 %all-gather.3.cloned.1.call-start = ((), (), s32[]{:S(2)}) async-start(), calls=%async_computation.2 | async-start | bytes 3538944 | tf_op jit(solution)/shard_map/all_gather | solution.py:20
  11.5 206.1 %reduce-scatter.5.cloned.1.call-start = ((), (), s32[]{:S(2)}) async-start(), calls=%async_computation.5 | async-start | bytes 3538944 | tf_op jit(solution)/shard_map/reduce_scatter | solution.py:77
  146.9 5.7 %copy-start = (bf16[3,4096,128]{2,1,0:T(8,128)(2,1)S(1)}, bf16[3,4096,128]{2,1,0:T(8,128)(2,1)}, u32[]{:S(2)}) copy-start(bf16[3,4096,128]{2,1,0:T(8,128)(2,1)} %all-gather.3.cloned.1.call-done) | copy-start | bytes 9437188
  146.9 8.8 %copy-start.2 = (bf16[128,1,4096]{2,0,1:T(8,128)(2,1)S(1)}, bf16[128,1,4096]{2,0,1:T(8,128)(2,1)}, u32[]{:S(2)}) copy-start(bf16[128,1,4096]{2,0,1:T(8,128)(2,1)} %copy.33) | copy-start | bytes 3145732
  149.4 9.5 %copy-start.1 = (bf16[128,1,4096]{2,0,1:T(8,128)(2,1)S(1)}, bf16[128,1,4096]{2,0,1:T(8,128)(2,1)}, u32[]{:S(2)}) copy-start(bf16[128,1,4096]{2,0,1:T(8,128)(2,1)} %copy.32) | copy-start | bytes 3145732
  149.4 3.2 collective-permute-start
  154.3 4.6 %collective-permute-start.1 = (bf16[3,128]{1,0:T(4,128)(2,1)S(1)}, bf16[3,128]{1,0:T(4,128)(2,1)S(1)}, u32[]{:S(2)}, u32[]{:S(2)}) collective-permute-start(bf16[3,128]{1,0:T(4,128)(2,1)S(1)} %slice.113), channel_id=1, source_target_pairs={{1,0},{2,1},{3,2},{4,3},{5,4},{6,5},{7,6},{9,8},{10,9},{11,10},{12... | collective-permute-start | bytes 2312 | tf_op jit(solution)/shard_map/ppermute | solution.py:10
  161.6 215.5 %reduce-scatter.3.cloned.1.call-start = ((), (), s32[]{:S(2)}) async-start(), calls=%async_computation.4 | async-start | bytes 4259840 | tf_op jit(solution)/shard_map/reduce_scatter | solution.py:68
Sparse Core Ops, SparseCore 0:
  11.9 90.0 all-gather.4
  104.7 42.1 all-gather.2
  161.7 55.8 reduce-scatter.4
  222.1 154.9 reduce-scatter.2

commit v2 on v1

--- a/solution.py
+++ b/solution.py
@@ -16,8 +16,11 @@
 
 
 def on_device(tokens, in_weight, conv_weight, conv_bias, out_weight, grad_out):
+    n_seq = lax.axis_size("seq")
+    n_dp = lax.axis_size("dp")
     w_local = jnp.concatenate([in_weight, out_weight.T[None]], axis=0)
-    w_full = lax.all_gather(w_local, "seq", axis=1, tiled=True)
+    w_rep = jnp.broadcast_to(w_local[None], (n_seq,) + w_local.shape)
+    w_full = lax.all_to_all(w_rep, "seq", 0, 2, tiled=True)[0]
     in_full = w_full[:2]
     out_full_t = w_full[2]
     acts = jnp.stack([tokens, grad_out], axis=1)
@@ -65,16 +68,17 @@
     )
     branch_grads = jnp.stack([grad_inner, grad_gate], axis=1)
     tok_part = jnp.einsum("tpe,pde->dt", branch_grads, in_full, preferred_element_type=jnp.float32)
-    reduced = lax.psum_scatter(
-        jnp.stack([out_part, tok_part], axis=1), "dp", scatter_dimension=0, tiled=True
-    )
-    reduced = lax.optimization_barrier(reduced)
-    output = reduced[:, 0].T.astype(jnp.bfloat16)
-    grad_tokens = reduced[:, 1].T.astype(jnp.bfloat16)
+    out_red = lax.psum_scatter(out_part, "dp", scatter_dimension=0, tiled=True)
+    out_red = lax.optimization_barrier(out_red)
+    output = out_red.T.astype(jnp.bfloat16)
+    tok_split = tok_part.reshape(n_dp, tok_part.shape[0] // n_dp, tok_rows)
+    tok_red = lax.all_to_all(tok_split, "dp", 0, 0, tiled=True).sum(axis=0)
+    grad_tokens = tok_red.T.astype(jnp.bfloat16)
     term_in = jnp.einsum("td,tpe->pde", whole, branch_grads, preferred_element_type=jnp.float32)
     term_out_t = jnp.einsum("td,te->de", upstream, hidden, preferred_element_type=jnp.float32)
     terms = jnp.concatenate([term_in, term_out_t[None]], axis=0).astype(jnp.bfloat16)
-    terms = lax.psum_scatter(terms, "seq", scatter_dimension=1, tiled=True).astype(jnp.float32)
+    terms = terms.reshape(terms.shape[0], n_seq, terms.shape[1] // n_seq, terms.shape[2])
+    terms = lax.all_to_all(terms, "seq", 1, 1, tiled=True).astype(jnp.float32).sum(axis=1)
     grad_in_weight = terms[:2]
     grad_out_weight = terms[2].T
     return (output, grad_tokens, grad_in_weight, grad_out_weight, tap_grads, bias_grads)

time: 389 us -> 393 us (1.010)
  waiting for transfers between devices: 315 us -> 261 us
  blocking collectives: 15.4 us -> 42.4 us
  starting transfers between devices: 3.91 us -> 30.4 us
  local copies, waits for them, and re-layouts: 20.7 us -> 25.9 us
    reduce_scatter x2 -> x1, waiting for transfers between devices: 193 us -> 114 us  [on_device(): out_red = lax.psum_scatter(out_part, 'dp', scatter_dimension=0, tiled=True)]
    all_to_all x0 -> x3, waiting for transfers between devices: none -> 51.3 us  [the longest x1 51.3 us: on_device(): tok_red = lax.all_to_all(tok_split, 'dp', 0, 0, tiled=True).sum(axis=0)]
    all_gather x1 -> x0, waiting for transfers between devices: 29.2 us -> none  [on_device(): w_full = lax.all_gather(w_local, 'seq', axis=1, tiled=True)]
    psum x1, blocking collectives: 15.4 us -> 42.4 us  [on_device(): lax.psum((jnp.stack(tap_rows, axis=0), jnp.sum(conv_float, axis=0)), 'seq')]
    all_to_all x0 -> x3, starting transfers between devices: none -> 25.9 us  [the longest x1 10.5 us: on_device(): lax.all_to_all(terms, 'seq', 1, 1, tiled=True).astype(jnp.float32)]
    all_gather x1, waiting for transfers between devices: 89 us -> 93.1 us  [on_device(): acts_full = lax.all_gather(acts, 'dp', axis=2, tiled=True)]
    slice x1 -> x4, local copies, waits for them, and re-layouts: 6.53 us -> 9.73 us  [the longest x1 6.5 us: on_device(): upstream = acts_full[:, 1]]
    unnamed x10 -> x15, local copies, waits for them, and re-layouts: 11.2 us -> 10.5 us
  transfers between devices with their start and end apart: 6 -> 7, of which waited for: 6 -> 4; matrix products, arithmetic and copies ran while one was open for 7% -> 7% of each run, Pallas kernels for 0% -> 0%
where the time goes in v2:
time: 393 us; the launch traced here: 389 us
  waiting for transfers between devices  261 us (66%)
  blocking collectives  42.4 us (11%)
  starting transfers between devices  30.4 us (8%)
  local copies, waits for them, and re-layouts  25.9 us (7%)
  between operations  14.3 us (4%)
  matrix products  7.22 us (2%)
  other arithmetic  7.21 us (2%)
    reduce_scatter x1, waiting for transfers between devices, on_device(): out_red = lax.psum_scatter(out_part, 'dp', scatter_dimension=0, tiled=True)  114 us
    all_gather x1, waiting for transfers between devices, on_device(): acts_full = lax.all_gather(acts, 'dp', axis=2, tiled=True)  93.1 us
    all_to_all x1, waiting for transfers between devices, on_device(): tok_red = lax.all_to_all(tok_split, 'dp', 0, 0, tiled=True).sum(axis=0)  51.3 us
    psum x1, blocking collectives, on_device(): lax.psum((jnp.stack(tap_rows, axis=0), jnp.sum(conv_float, axis=0)), 'seq')  42.4 us
    unnamed x15, local copies, waits for them, and re-layouts  10.5 us
    all_to_all x1, starting transfers between devices, on_device(): lax.all_to_all(terms, 'seq', 1, 1, tiled=True).astype(jnp.float32)  10.5 us
    all_to_all x1, starting transfers between devices, on_device(): tok_red = lax.all_to_all(tok_split, 'dp', 0, 0, tiled=True).sum(axis=0)  9.45 us
  transfers between devices with their start and end apart: 7, of which 4 were waited for; matrix products, arithmetic and copies ran while one was open for 7% of the time, Pallas kernels for 0%

profile of v2, /device:TPU:1, one launch (start us, length us, event | category | flops | bytes accessed | tf_op | source)
XLA Modules:
  0.0 388.6 jit_solution(3724221789689169663)
XLA Ops:
  7.2 1.0 copy.28
  8.2 1.0 pad_maximum_fusion.1
  9.2 2.4 broadcast_in_dim.7
  11.6 0.0 copy-start.2
  11.6 0.0 copy-start.3
  11.6 0.0 copy-start.5
  11.6 0.0 copy-start.4
  11.6 6.0 %all-to-all-start = ((bf16[8,3,512,128]{3,2,1,0:T(8,128)(2,1)}), bf16[8,3,512,128]{3,2,1,0:T(8,128)(2,1)}, u32[]{:S(2)}, u32[]{:S(2)}) async-start(bf16[8,3,512,128]{3,2,1,0:T(8,128)(2,1)} %broadcast_in_dim.7), calls=%async_computation | async-start | bytes 6291456 | tf_op jit(solution)/shard_map/all_to_all | solution.py:23
  17.6 0.0 all-gather.2.cloned.1.call-start
  17.6 0.0 copy-done.2
  17.6 0.0 copy-done.3
  17.7 0.6 copy.29
  18.3 0.0 all-gather.2.cloned.1.call-update
  18.3 0.0 copy-done.5
  18.4 0.0 copy-done.4
  18.4 93.1 %all-gather.2.cloned.1.call-done = bf16[128,2,4096]{0,1,2:T(2,128)(2,1)} async-done(((bf16[128,2,64]{0,1,2:T(2,128)(2,1)}), bf16[128,2,4096]{0,1,2:T(2,128)(2,1)}) %all-gather.2.cloned.1.call-update) | async-done | bytes 2097168 | tf_op jit(solution)/shard_map/all_gather | solution.py:27
  111.5 6.5 %fusion.35 = (bf16[128,1,4096]{0,1,2:T(2,128)(2,1)S(1)}, bf16[128,1,4096]{0,1,2:T(2,128)(2,1)}) fusion(bf16[128,2,4096]{0,1,2:T(2,128)(2,1)} %all-gather.2.cloned.1.call-done), kind=kLoop, calls=%fused_computation.77 | loop fusion | bytes 4194304 | tf_op jit(solution)/shard_map/slice | solution.py:29
  118.0 4.7 %copy.40 = bf16[128,1,4096]{2,0,1:T(8,128)(2,1)S(1)} copy(bf16[128,1,4096]{0,1,2:T(2,128)(2,1)} %get-tuple-element.37) | data formatting | bytes 2097152
  122.7 3.9 copy.41
  126.5 0.0 all-to-all-done
  126.5 1.7 slice.99
  128.3 0.2 copy.31
  128.5 0.0 copy-start.1
  128.5 0.5 convolution_convert_fusion.2
  129.0 3.1 collective-permute-start
  132.1 1.3 slice.97
  133.4 0.0 copy-start
  133.4 0.0 collective-permute-done
  133.4 1.0 copy-done
  134.4 0.0 copy-done.1
  134.4 0.5 convert_reduce_fusion.1
  134.9 1.3 collective-permute-start.1
  136.2 0.1 fusion.29
  136.2 3.0 collective-permute-done.1
  139.2 2.1 convolution_bitcast_fusion
  141.3 9.5 %all-to-all-start.1 = ((f32[64,64,128]{2,1,0:T(8,128)}), f32[64,64,128]{2,1,0:T(8,128)}, u32[]{:S(2)}, u32[]{:S(2)}) async-start(f32[64,64,128]{2,1,0:T(8,128)} %convolution_bitcast_fusion), calls=%async_computation.2 | async-start | bytes 4194304 | tf_op jit(solution)/shard_map/all_to_all | solution.py:75
  150.7 0.1 copy.42
  150.9 0.4 fusion
  151.3 0.5 copy.36
  151.9 0.7 convolution_convert_fusion
  152.6 0.2 copy.45
  152.8 1.9 pad_maximum_fusion
  154.8 51.3 %all-to-all-done.1 = f32[64,64,128]{2,1,0:T(8,128)} async-done(((f32[64,64,128]{2,1,0:T(8,128)}), f32[64,64,128]{2,1,0:T(8,128)}, u32[]{:S(2)}, u32[]{:S(2)}) %all-to-all-start.1) | async-done | bytes 2097184 | tf_op jit(solution)/shard_map/all_to_all | solution.py:75
  206.1 10.5 %all-to-all-start.2 = ((bf16[3,8,512,128]{2,3,0,1:T(8,128)(2,1)}), bf16[3,8,512,128]{2,3,0,1:T(8,128)(2,1)S(1)}, u32[]{:S(2)}, u32[]{:S(2)}) async-start(bf16[3,8,512,128]{2,3,0,1:T(8,128)(2,1)} %pad_maximum_fusion), calls=%async_computation.3 | async-start | bytes 6291456 | tf_op jit(solution)/shard_map/all_to_all | solution.py:81
  216.5 0.0 reduce-scatter.2.cloned.1.call-start
  216.6 3.0 fusion.33
  219.6 0.0 reduce-scatter.2.cloned.1.call-update
  219.6 42.4 %all-reduce = (f32[4,128]{1,0:T(4,128)}, f32[128]{0:T(128)}) all-reduce(f32[4,128]{1,0:T(4,128)S(1)} %pad_maximum_fusion.8, f32[128]{0:T(128)S(1)} %get-tuple-element.27), channel_id=1, replica_groups=mesh['dp'=64,'seq'=8] {'seq'}, use_global_device_ids=true, to_apply=%region_7.0 | all-reduce | flops 640 | bytes 5120 | tf_op jit(solution)/shard_map/psum | solution.py:66
  262.1 113.7 %reduce-scatter.2.cloned.1.call-done = f32[64,128]{1,0:T(8,128)} async-done(((f32[4096,128]{1,0:T(8,128)}), f32[64,128]{1,0:T(8,128)}) %reduce-scatter.2.cloned.1.call-update) | async-done | bytes 32784 | tf_op jit(solution)/shard_map/reduce_scatter | solution.py:71
  375.8 1.4 convert_bitcast_fusion.1
  377.2 2.3 reduce_sum.63
  379.5 0.0 all-to-all-done.2
  379.5 0.4 convert_reduce_fusion
  380.0 0.7 slice_bitcast_fusion
  380.7 1.0 copy.37
  (9 shorter events, 0.1 us)
Async XLA Ops:
  11.6 6.1 %copy-start.2 = (bf16[128,64]{0,1:T(8,128)(2,1)S(1)}, bf16[128,64]{0,1:T(8,128)(2,1)}, u32[]{:S(2)}) copy-start(bf16[128,64]{0,1:T(8,128)(2,1)} %param.11) | copy-start | bytes 49156
  11.6 6.1 %copy-start.3 = (bf16[128,64]{0,1:T(8,128)(2,1)S(1)}, bf16[128,64]{0,1:T(8,128)(2,1)}, u32[]{:S(2)}) copy-start(bf16[128,64]{0,1:T(8,128)(2,1)} %param.6) | copy-start | bytes 49156
  11.6 6.8 %copy-start.5 = (bf16[128]{0:T(256)(128)(2,1)S(1)}, bf16[128]{0:T(256)(128)(2,1)}, u32[]{:S(2)}) copy-start(bf16[128]{0:T(256)(128)(2,1)} %param.9) | copy-start | bytes 772
  11.6 6.8 %copy-start.4 = (bf16[4,128]{1,0:T(4,128)(2,1)S(1)}, bf16[4,128]{1,0:T(4,128)(2,1)}, u32[]{:S(2)}) copy-start(bf16[4,128]{1,0:T(4,128)(2,1)} %param.8) | copy-start | bytes 3076
  11.6 114.9 %all-to-all-start = ((bf16[8,3,512,128]{3,2,1,0:T(8,128)(2,1)}), bf16[8,3,512,128]{3,2,1,0:T(8,128)(2,1)}, u32[]{:S(2)}, u32[]{:S(2)}) async-start(bf16[8,3,512,128]{3,2,1,0:T(8,128)(2,1)} %broadcast_in_dim.7), calls=%async_computation | async-start | bytes 6291456 | tf_op jit(solution)/shard_map/all_to_all | solution.py:23
  17.6 93.9 %all-gather.2.cloned.1.call-start = ((), (), s32[]{:S(2)}) async-start(), calls=%async_computation.4 | async-start | bytes 2129920 | tf_op jit(solution)/shard_map/all_gather | solution.py:27
  128.5 5.9 %copy-start.1 = (bf16[128,1,4096]{2,0,1:T(8,128)(2,1)S(1)}, bf16[128,1,4096]{2,0,1:T(8,128)(2,1)}, u32[]{:S(2)}) copy-start(bf16[128,1,4096]{2,0,1:T(8,128)(2,1)} %copy.41) | copy-start | bytes 3145732
  129.0 4.4 %collective-permute-start = (bf16[3,128]{1,0:T(4,128)(2,1)S(1)}, bf16[3,128]{1,0:T(4,128)(2,1)S(1)}, u32[]{:S(2)}, u32[]{:S(2)}) collective-permute-start(bf16[3,128]{1,0:T(4,128)(2,1)S(1)} %slice_bitcast_fusion.3), channel_id=1, source_target_pairs={{0,1},{1,2},{2,3},{3,4},{4,5},{5,6},{6,7},{8,9},{9,10},{10,11},{11... | collective-permute-start | bytes 2312 | tf_op jit(solution)/shard_map/ppermute | solution.py:10
  133.4 1.0 copy-start
  134.9 4.3 %collective-permute-start.1 = (bf16[3,128]{1,0:T(4,128)(2,1)S(1)}, bf16[3,128]{1,0:T(4,128)(2,1)S(1)}, u32[]{:S(2)}, u32[]{:S(2)}) collective-permute-start(bf16[3,128]{1,0:T(4,128)(2,1)S(1)} %slice.108), channel_id=1, source_target_pairs={{1,0},{2,1},{3,2},{4,3},{5,4},{6,5},{7,6},{9,8},{10,9},{11,10},{12... | collective-permute-start | bytes 2312 | tf_op jit(solution)/shard_map/ppermute | solution.py:10
  141.3 64.8 %all-to-all-start.1 = ((f32[64,64,128]{2,1,0:T(8,128)}), f32[64,64,128]{2,1,0:T(8,128)}, u32[]{:S(2)}, u32[]{:S(2)}) async-start(f32[64,64,128]{2,1,0:T(8,128)} %convolution_bitcast_fusion), calls=%async_computation.2 | async-start | bytes 4194304 | tf_op jit(solution)/shard_map/all_to_all | solution.py:75
  206.1 173.5 %all-to-all-start.2 = ((bf16[3,8,512,128]{2,3,0,1:T(8,128)(2,1)}), bf16[3,8,512,128]{2,3,0,1:T(8,128)(2,1)S(1)}, u32[]{:S(2)}, u32[]{:S(2)}) async-start(bf16[3,8,512,128]{2,3,0,1:T(8,128)(2,1)} %pad_maximum_fusion), calls=%async_computation.3 | async-start | bytes 6291456 | tf_op jit(solution)/shard_map/all_to_all | solution.py:81
  216.5 159.3 %reduce-scatter.2.cloned.1.call-start = ((), (), s32[]{:S(2)}) async-start(), calls=%async_computation.5 | async-start | bytes 2129920 | tf_op jit(solution)/shard_map/reduce_scatter | solution.py:71
Sparse Core Ops, SparseCore 0:
  22.3 89.0 all-gather.1
  222.0 153.7 reduce-scatter.1

commit v3 on v2

--- a/solution.py
+++ b/solution.py
@@ -13,6 +13,12 @@
 def silu_parts(value):
     sig = jax.nn.sigmoid(value)
     return (value * sig, sig * (1.0 + value * (1.0 - sig)))
+
+
+def reduce_over_dp(part, n_dp):
+    split = part.astype(jnp.bfloat16).reshape(n_dp, part.shape[0] // n_dp, part.shape[1])
+    summed = lax.all_to_all(split, "dp", 0, 0, tiled=True).astype(jnp.float32).sum(axis=0)
+    return summed.T.astype(jnp.bfloat16)
 
 
 def on_device(tokens, in_weight, conv_weight, conv_bias, out_weight, grad_out):
@@ -63,17 +69,14 @@
         tap_rows.append(
             jnp.sum(conv_float * padded[lag : lag + tok_rows].astype(jnp.float32), axis=0)
         )
-    tap_grads, bias_grads = lax.psum(
-        (jnp.stack(tap_rows, axis=0), jnp.sum(conv_float, axis=0)), "seq"
-    )
+    conv_grads = jnp.concatenate([jnp.stack(tap_rows, axis=0), jnp.sum(conv_float, axis=0)[None]], axis=0)
+    conv_grads = lax.all_gather(conv_grads, "seq", axis=0, tiled=False).sum(axis=0)
+    tap_grads = conv_grads[:taps]
+    bias_grads = conv_grads[taps]
     branch_grads = jnp.stack([grad_inner, grad_gate], axis=1)
     tok_part = jnp.einsum("tpe,pde->dt", branch_grads, in_full, preferred_element_type=jnp.float32)
-    out_red = lax.psum_scatter(out_part, "dp", scatter_dimension=0, tiled=True)
-    out_red = lax.optimization_barrier(out_red)
-    output = out_red.T.astype(jnp.bfloat16)
-    tok_split = tok_part.reshape(n_dp, tok_part.shape[0] // n_dp, tok_rows)
-    tok_red = lax.all_to_all(tok_split, "dp", 0, 0, tiled=True).sum(axis=0)
-    grad_tokens = tok_red.T.astype(jnp.bfloat16)
+    output = reduce_over_dp(out_part, n_dp)
+    grad_tokens = reduce_over_dp(tok_part, n_dp)
     term_in = jnp.einsum("td,tpe->pde", whole, branch_grads, preferred_element_type=jnp.float32)
     term_out_t = jnp.einsum("td,te->de", upstream, hidden, preferred_element_type=jnp.float32)
     terms = jnp.concatenate([term_in, term_out_t[None]], axis=0).astype(jnp.bfloat16)

time: 393 us -> 297 us (0.76)
  waiting for transfers between devices: 261 us -> 143 us
  blocking collectives: 42.4 us -> 54.2 us
  starting transfers between devices: 30.4 us -> 40.2 us
    reduce_scatter x1 -> x0, waiting for transfers between devices: 114 us -> none  [on_device(): out_red = lax.psum_scatter(out_part, 'dp', scatter_dimension=0, tiled=True)]
    all_gather x0 -> x1, blocking collectives: none -> 54.2 us  [on_device(): lax.all_gather(conv_grads, 'seq', axis=0, tiled=False).sum(axis=0)]
    psum x1 -> x0, blocking collectives: 42.4 us -> none  [on_device(): lax.psum((jnp.stack(tap_rows, axis=0), jnp.sum(conv_float, axis=0)), 'seq')]
    all_to_all x1 -> x2, starting transfers between devices: 9.45 us -> 18.4 us  [reduce_over_dp(): lax.all_to_all(split, 'dp', 0, 0, tiled=True).astype(jnp.float32)]
    all_to_all x1 -> x2, waiting for transfers between devices: 51.3 us -> 46.1 us  [reduce_over_dp(): lax.all_to_all(split, 'dp', 0, 0, tiled=True).astype(jnp.float32)]
    unnamed x15 -> x17, local copies, waits for them, and re-layouts: 10.5 us -> 9.81 us
  transfers between devices with their start and end apart: 7 -> 7, of which waited for: 4 -> 4; matrix products, arithmetic and copies ran while one was open for 7% -> 10% of each run, Pallas kernels for 0% -> 0%
where the time goes in v3:
time: 297 us; the launch traced here: 291 us
  waiting for transfers between devices  143 us (48%)
  blocking collectives  54.2 us (18%)
  starting transfers between devices  40.2 us (14%)
  local copies, waits for them, and re-layouts  26.3 us (9%)
  between operations  14.3 us (5%)
  other arithmetic  7.52 us (3%)
  matrix products  5.25 us (2%)
    all_gather x1, waiting for transfers between devices, on_device(): acts_full = lax.all_gather(acts, 'dp', axis=2, tiled=True)  93.1 us
    all_gather x1, blocking collectives, on_device(): lax.all_gather(conv_grads, 'seq', axis=0, tiled=False).sum(axis=0)  54.2 us
    all_to_all x2, waiting for transfers between devices, reduce_over_dp(): lax.all_to_all(split, 'dp', 0, 0, tiled=True).astype(jnp.float32)  46.1 us
    all_to_all x2, starting transfers between devices, reduce_over_dp(): lax.all_to_all(split, 'dp', 0, 0, tiled=True).astype(jnp.float32)  18.4 us
    all_to_all x1, starting transfers between devices, on_device(): lax.all_to_all(terms, 'seq', 1, 1, tiled=True).astype(jnp.float32)  11.3 us
    unnamed x17, local copies, waits for them, and re-layouts  9.81 us
    slice x1, local copies, waits for them, and re-layouts, on_device(): upstream = acts_full[:, 1]  6.5 us
    all_to_all x1, starting transfers between devices, on_device(): w_full = lax.all_to_all(w_rep, 'seq', 0, 2, tiled=True)[0]  6.01 us
  transfers between devices with their start and end apart: 7, of which 4 were waited for; matrix products, arithmetic and copies ran while one was open for 10% of the time, Pallas kernels for 0%

profile of v3, /device:TPU:1, one launch (start us, length us, event | category | flops | bytes accessed | tf_op | source)
XLA Modules:
  0.0 290.9 jit_solution(17040692460913834708)
XLA Ops:
  7.2 1.0 copy.26
  8.2 1.0 pad_maximum_fusion.1
  9.2 2.4 broadcast_in_dim.9
  11.6 0.0 copy-start.3
  11.6 0.0 copy-start.4
  11.6 0.0 copy-start.6
  11.6 0.0 copy-start.5
  11.6 6.0 %all-to-all-start = ((bf16[8,3,512,128]{3,2,1,0:T(8,128)(2,1)}), bf16[8,3,512,128]{3,2,1,0:T(8,128)(2,1)}, u32[]{:S(2)}, u32[]{:S(2)}) async-start(bf16[8,3,512,128]{3,2,1,0:T(8,128)(2,1)} %broadcast_in_dim.9), calls=%async_computation | async-start | bytes 6291456 | tf_op jit(solution)/shard_map/all_to_all | solution.py:29
  17.6 0.0 all-gather.4.cloned.1.call-start
  17.6 0.0 copy-done.3
  17.6 0.0 copy-done.4
  17.7 0.6 copy.27
  18.3 0.0 all-gather.4.cloned.1.call-update
  18.3 0.0 copy-done.6
  18.4 0.0 copy-done.5
  18.4 93.1 %all-gather.4.cloned.1.call-done = bf16[128,2,4096]{0,1,2:T(2,128)(2,1)} async-done(((bf16[128,2,64]{0,1,2:T(2,128)(2,1)}), bf16[128,2,4096]{0,1,2:T(2,128)(2,1)}) %all-gather.4.cloned.1.call-update) | async-done | bytes 2097168 | tf_op jit(solution)/shard_map/all_gather | solution.py:33
  111.5 6.5 %fusion.34 = (bf16[128,1,4096]{0,1,2:T(2,128)(2,1)S(1)}, bf16[128,1,4096]{0,1,2:T(2,128)(2,1)}) fusion(bf16[128,2,4096]{0,1,2:T(2,128)(2,1)} %all-gather.4.cloned.1.call-done), kind=kLoop, calls=%fused_computation.75 | loop fusion | bytes 4194304 | tf_op jit(solution)/shard_map/slice | solution.py:35
  118.0 0.0 copy-start
  118.0 4.9 %copy.37 = bf16[128,1,4096]{2,0,1:T(8,128)(2,1)S(1)} copy(bf16[128,1,4096]{0,1,2:T(2,128)(2,1)} %get-tuple-element.32) | data formatting | bytes 2097152
  122.9 3.8 %copy.38 = bf16[128,1,4096]{2,0,1:T(8,128)(2,1)} copy(bf16[128,1,4096]{0,1,2:T(2,128)(2,1)S(1)} %get-tuple-element.31) | data formatting | bytes 2097152
  126.8 0.0 copy-done
  126.8 0.0 all-to-all-done
  126.8 1.7 slice.107
  128.5 0.1 copy.29
  128.7 0.0 copy-start.2
  128.7 0.4 convolution_convert_fusion.3
  129.2 3.1 %collective-permute-start = (bf16[3,128]{1,0:T(4,128)(2,1)S(1)}, bf16[3,128]{1,0:T(4,128)(2,1)S(1)}, u32[]{:S(2)}, u32[]{:S(2)}) collective-permute-start(bf16[3,128]{1,0:T(4,128)(2,1)S(1)} %slice_bitcast_fusion.3), channel_id=1, source_target_pairs={{0,1},{1,2},{2,3},{3,4},{4,5},{5,6},{6,7},{8,9},{9,10},{10,11},{11... | collective-permute-start | bytes 2312 | tf_op jit(solution)/shard_map/ppermute | solution.py:10
  132.3 1.3 slice.105
  133.6 0.0 collective-permute-done
  133.6 0.0 copy-done.2
  133.6 0.5 fusion.21
  134.1 1.4 convolution_convert_fusion.1
  135.5 8.3 %all-to-all-start.1 = ((bf16[64,64,128]{2,1,0:T(8,128)(2,1)}), bf16[64,64,128]{2,1,0:T(8,128)(2,1)}, u32[]{:S(2)}, u32[]{:S(2)}) async-start(bf16[64,64,128]{2,1,0:T(8,128)(2,1)} %bitcast.105), calls=%async_computation.1 | async-start | bytes 2097152 | tf_op jit(solution)/shard_map/all_to_all | solution.py:20
  143.8 1.3 collective-permute-start.1
  145.1 0.1 fusion.29
  145.2 3.8 %collective-permute-done.1 = bf16[3,128]{1,0:T(4,128)(2,1)S(1)} collective-permute-done((bf16[3,128]{1,0:T(4,128)(2,1)S(1)}, bf16[3,128]{1,0:T(4,128)(2,1)S(1)}, u32[]{:S(2)}, u32[]{:S(2)}) %collective-permute-start.1) | collective-permute-done | bytes 800 | tf_op jit(solution)/shard_map/ppermute | solution.py:10
  149.1 1.7 fusion
  150.8 0.0 copy-start.1
  150.8 23.8 %all-to-all-done.1 = bf16[64,64,128]{2,1,0:T(8,128)(2,1)} async-done(((bf16[64,64,128]{2,1,0:T(8,128)(2,1)}), bf16[64,64,128]{2,1,0:T(8,128)(2,1)}, u32[]{:S(2)}, u32[]{:S(2)}) %all-to-all-start.1) | async-done | bytes 1048608 | tf_op jit(solution)/shard_map/all_to_all | solution.py:20
  174.6 10.1 %all-to-all-start.2 = ((bf16[64,64,128]{2,1,0:T(8,128)(2,1)}), bf16[64,64,128]{2,1,0:T(8,128)(2,1)}, u32[]{:S(2)}, u32[]{:S(2)}) async-start(bf16[64,64,128]{2,1,0:T(8,128)(2,1)} %bitcast.101), calls=%async_computation.2 | async-start | bytes 2097152 | tf_op jit(solution)/shard_map/all_to_all | solution.py:20
  184.7 0.0 copy-done.1
  184.7 0.1 copy.39
  184.9 0.5 fusion.1
  185.3 0.5 copy.34
  185.9 0.7 convolution_convert_fusion
  186.6 0.2 copy.42
  186.8 1.9 pad_maximum_fusion
  188.8 22.4 %all-to-all-done.2 = bf16[64,64,128]{2,1,0:T(8,128)(2,1)} async-done(((bf16[64,64,128]{2,1,0:T(8,128)(2,1)}), bf16[64,64,128]{2,1,0:T(8,128)(2,1)}, u32[]{:S(2)}, u32[]{:S(2)}) %all-to-all-start.2) | async-done | bytes 1048608 | tf_op jit(solution)/shard_map/all_to_all | solution.py:20
  211.1 11.3 %all-to-all-start.3 = ((bf16[3,8,512,128]{2,3,0,1:T(8,128)(2,1)}), bf16[3,8,512,128]{2,3,0,1:T(8,128)(2,1)S(1)}, u32[]{:S(2)}, u32[]{:S(2)}) async-start(bf16[3,8,512,128]{2,3,0,1:T(8,128)(2,1)} %pad_maximum_fusion), calls=%async_computation.3 | async-start | bytes 6291456 | tf_op jit(solution)/shard_map/all_to_all | solution.py:84
  222.5 54.2 %all-gather.1 = f32[8,5,128]{2,1,0:T(8,128)S(1)} all-gather(f32[1,5,128]{2,1,0:T(8,128)S(1)} %bitcast.111), channel_id=2, replica_groups=mesh['dp'=64,'seq'=8] {'seq'}, dimensions={0}, use_global_device_ids=true | all-gather | bytes 23040 | tf_op jit(solution)/shard_map/all_gather | solution.py:73
  276.7 0.6 slice.103
  277.3 0.5 slice_bitcast_fusion.4
  277.8 2.0 reduce_sum.87
  279.8 2.0 reduce_sum.88
  281.9 0.0 all-to-all-done.3
  281.9 0.4 convert_reduce_fusion
  282.4 0.7 slice_bitcast_fusion
  283.1 1.0 copy.35
  (10 shorter events, 0.1 us)
Async XLA Ops:
  11.6 6.1 %copy-start.3 = (bf16[128,64]{0,1:T(8,128)(2,1)S(1)}, bf16[128,64]{0,1:T(8,128)(2,1)}, u32[]{:S(2)}) copy-start(bf16[128,64]{0,1:T(8,128)(2,1)} %param.11) | copy-start | bytes 49156
  11.6 6.1 %copy-start.4 = (bf16[128,64]{0,1:T(8,128)(2,1)S(1)}, bf16[128,64]{0,1:T(8,128)(2,1)}, u32[]{:S(2)}) copy-start(bf16[128,64]{0,1:T(8,128)(2,1)} %param.6) | copy-start | bytes 49156
  11.6 6.8 %copy-start.6 = (bf16[128]{0:T(256)(128)(2,1)S(1)}, bf16[128]{0:T(256)(128)(2,1)}, u32[]{:S(2)}) copy-start(bf16[128]{0:T(256)(128)(2,1)} %param.9) | copy-start | bytes 772
  11.6 6.8 %copy-start.5 = (bf16[4,128]{1,0:T(4,128)(2,1)S(1)}, bf16[4,128]{1,0:T(4,128)(2,1)}, u32[]{:S(2)}) copy-start(bf16[4,128]{1,0:T(4,128)(2,1)} %param.8) | copy-start | bytes 3076
  11.6 115.2 %all-to-all-start = ((bf16[8,3,512,128]{3,2,1,0:T(8,128)(2,1)}), bf16[8,3,512,128]{3,2,1,0:T(8,128)(2,1)}, u32[]{:S(2)}, u32[]{:S(2)}) async-start(bf16[8,3,512,128]{3,2,1,0:T(8,128)(2,1)} %broadcast_in_dim.9), calls=%async_computation | async-start | bytes 6291456 | tf_op jit(solution)/shard_map/all_to_all | solution.py:29
  17.6 93.9 %all-gather.4.cloned.1.call-start = ((), (), s32[]{:S(2)}) async-start(), calls=%async_computation.4 | async-start | bytes 2129920 | tf_op jit(solution)/shard_map/all_gather | solution.py:33
  118.0 8.8 %copy-start = (bf16[128,1,4096]{0,1,2:T(2,128)(2,1)}, bf16[128,1,4096]{0,1,2:T(2,128)(2,1)S(1)}, u32[]{:S(2)}) copy-start(bf16[128,1,4096]{0,1,2:T(2,128)(2,1)S(1)} %get-tuple-element.31) | copy-start | bytes 3145732
  128.7 4.9 %copy-start.2 = (bf16[128,1,4096]{2,0,1:T(8,128)(2,1)S(1)}, bf16[128,1,4096]{2,0,1:T(8,128)(2,1)}, u32[]{:S(2)}) copy-start(bf16[128,1,4096]{2,0,1:T(8,128)(2,1)} %copy.38) | copy-start | bytes 3145732
  129.2 4.4 %collective-permute-start = (bf16[3,128]{1,0:T(4,128)(2,1)S(1)}, bf16[3,128]{1,0:T(4,128)(2,1)S(1)}, u32[]{:S(2)}, u32[]{:S(2)}) collective-permute-start(bf16[3,128]{1,0:T(4,128)(2,1)S(1)} %slice_bitcast_fusion.3), channel_id=1, source_target_pairs={{0,1},{1,2},{2,3},{3,4},{4,5},{5,6},{6,7},{8,9},{9,10},{10,11},{11... | collective-permute-start | bytes 2312 | tf_op jit(solution)/shard_map/ppermute | solution.py:10
  135.5 39.0 %all-to-all-start.1 = ((bf16[64,64,128]{2,1,0:T(8,128)(2,1)}), bf16[64,64,128]{2,1,0:T(8,128)(2,1)}, u32[]{:S(2)}, u32[]{:S(2)}) async-start(bf16[64,64,128]{2,1,0:T(8,128)(2,1)} %bitcast.105), calls=%async_computation.1 | async-start | bytes 2097152 | tf_op jit(solution)/shard_map/all_to_all | solution.py:20
  143.8 5.2 %collective-permute-start.1 = (bf16[3,128]{1,0:T(4,128)(2,1)S(1)}, bf16[3,128]{1,0:T(4,128)(2,1)S(1)}, u32[]{:S(2)}, u32[]{:S(2)}) collective-permute-start(bf16[3,128]{1,0:T(4,128)(2,1)S(1)} %slice.116), channel_id=1, source_target_pairs={{1,0},{2,1},{3,2},{4,3},{5,4},{6,5},{7,6},{9,8},{10,9},{11,10},{12... | collective-permute-start | bytes 2312 | tf_op jit(solution)/shard_map/ppermute | solution.py:10
  150.8 33.9 %copy-start.1 = (bf16[128,1,4096]{0,1,2:T(2,128)(2,1)S(1)}, bf16[128,1,4096]{0,1,2:T(2,128)(2,1)}, u32[]{:S(2)}) copy-start(bf16[128,1,4096]{0,1,2:T(2,128)(2,1)} %copy-done) | copy-start | bytes 3145732
  174.6 36.6 %all-to-all-start.2 = ((bf16[64,64,128]{2,1,0:T(8,128)(2,1)}), bf16[64,64,128]{2,1,0:T(8,128)(2,1)}, u32[]{:S(2)}, u32[]{:S(2)}) async-start(bf16[64,64,128]{2,1,0:T(8,128)(2,1)} %bitcast.101), calls=%async_computation.2 | async-start | bytes 2097152 | tf_op jit(solution)/shard_map/all_to_all | solution.py:20
  211.1 70.7 %all-to-all-start.3 = ((bf16[3,8,512,128]{2,3,0,1:T(8,128)(2,1)}), bf16[3,8,512,128]{2,3,0,1:T(8,128)(2,1)S(1)}, u32[]{:S(2)}, u32[]{:S(2)}) async-start(bf16[3,8,512,128]{2,3,0,1:T(8,128)(2,1)} %pad_maximum_fusion), calls=%async_computation.3 | async-start | bytes 6291456 | tf_op jit(solution)/shard_map/all_to_all | solution.py:84
Sparse Core Ops, SparseCore 0:
  22.3 89.0 all-gather.3

commit v4 on v3

--- a/solution.py
+++ b/solution.py
@@ -15,6 +15,19 @@
     return (value * sig, sig * (1.0 + value * (1.0 - sig)))
 
 
+def gather_over(block, axis, n):
+    rep = jnp.broadcast_to(block[None], (n,) + block.shape)
+    return lax.all_to_all(rep, axis, 0, 2, tiled=True)[0]
+
+
+def split_exact(value):
+    hi = value.astype(jnp.bfloat16)
+    rest = value - hi.astype(jnp.float32)
+    mid = rest.astype(jnp.bfloat16)
+    lo = (rest - mid.astype(jnp.float32)).astype(jnp.bfloat16)
+    return jnp.concatenate([hi, mid, lo], axis=0)
+
+
 def reduce_over_dp(part, n_dp):
     split = part.astype(jnp.bfloat16).reshape(n_dp, part.shape[0] // n_dp, part.shape[1])
     summed = lax.all_to_all(split, "dp", 0, 0, tiled=True).astype(jnp.float32).sum(axis=0)
@@ -25,14 +38,11 @@
     n_seq = lax.axis_size("seq")
     n_dp = lax.axis_size("dp")
     w_local = jnp.concatenate([in_weight, out_weight.T[None]], axis=0)
-    w_rep = jnp.broadcast_to(w_local[None], (n_seq,) + w_local.shape)
-    w_full = lax.all_to_all(w_rep, "seq", 0, 2, tiled=True)[0]
+    w_full = gather_over(w_local, "seq", n_seq)
     in_full = w_full[:2]
     out_full_t = w_full[2]
-    acts = jnp.stack([tokens, grad_out], axis=1)
-    acts_full = lax.all_gather(acts, "dp", axis=2, tiled=True)
-    whole = acts_full[:, 0]
-    upstream = acts_full[:, 1]
+    whole = gather_over(tokens, "dp", n_dp)
+    upstream = gather_over(grad_out, "dp", n_dp)
     tok_rows = whole.shape[0]
     taps = conv_weight.shape[0]
     mixed = jnp.einsum("td,pde->tpe", whole, in_full, preferred_element_type=jnp.float32).astype(
@@ -70,9 +80,6 @@
             jnp.sum(conv_float * padded[lag : lag + tok_rows].astype(jnp.float32), axis=0)
         )
     conv_grads = jnp.concatenate([jnp.stack(tap_rows, axis=0), jnp.sum(conv_float, axis=0)[None]], axis=0)
-    conv_grads = lax.all_gather(conv_grads, "seq", axis=0, tiled=False).sum(axis=0)
-    tap_grads = conv_grads[:taps]
-    bias_grads = conv_grads[taps]
     branch_grads = jnp.stack([grad_inner, grad_gate], axis=1)
     tok_part = jnp.einsum("tpe,pde->dt", branch_grads, in_full, preferred_element_type=jnp.float32)
     output = reduce_over_dp(out_part, n_dp)
@@ -80,10 +87,25 @@
     term_in = jnp.einsum("td,tpe->pde", whole, branch_grads, preferred_element_type=jnp.float32)
     term_out_t = jnp.einsum("td,te->de", upstream, hidden, preferred_element_type=jnp.float32)
     terms = jnp.concatenate([term_in, term_out_t[None]], axis=0).astype(jnp.bfloat16)
-    terms = terms.reshape(terms.shape[0], n_seq, terms.shape[1] // n_seq, terms.shape[2])
-    terms = lax.all_to_all(terms, "seq", 1, 1, tiled=True).astype(jnp.float32).sum(axis=1)
-    grad_in_weight = terms[:2]
-    grad_out_weight = terms[2].T
+    n_mats, d_full, e_loc = terms.shape
+    d_loc = d_full // n_seq
+    terms = terms.reshape(n_mats, n_seq, d_loc, e_loc).transpose(1, 0, 2, 3)
+    terms = terms.reshape(n_seq, n_mats * d_loc, e_loc)
+    conv_parts = split_exact(conv_grads)
+    n_conv = conv_parts.shape[0]
+    pad_rows = (-n_conv) % 8
+    conv_parts = jnp.concatenate([conv_parts, jnp.zeros((pad_rows, e_loc), jnp.bfloat16)], axis=0)
+    conv_parts = jnp.broadcast_to(conv_parts[None], (n_seq,) + conv_parts.shape)
+    sent = jnp.concatenate([terms, conv_parts], axis=1)
+    summed = lax.all_to_all(sent, "seq", 0, 0, tiled=True).astype(jnp.float32).sum(axis=0)
+    weights = summed[: n_mats * d_loc].reshape(n_mats, d_loc, e_loc)
+    grad_in_weight = weights[:2]
+    grad_out_weight = weights[2].T
+    conv_sum = summed[n_mats * d_loc : n_mats * d_loc + n_conv]
+    n_row = taps + 1
+    conv_sum = (conv_sum[:n_row] + conv_sum[n_row : 2 * n_row]) + conv_sum[2 * n_row :]
+    tap_grads = conv_sum[:taps]
+    bias_grads = conv_sum[taps]
     return (output, grad_tokens, grad_in_weight, grad_out_weight, tap_grads, bias_grads)
 
 

time: 297 us -> 269 us (0.906); the launches traced: 291 us -> 268 us
  between operations: 14.3 us -> 0.94 us
  blocking collectives: 54.2 us -> 40.9 us
  starting transfers between devices: 40.2 us -> 53.1 us
  local copies, waits for them, and re-layouts: 26.3 us -> 18.9 us
  waiting for transfers between devices: 143 us -> 139 us
  matrix products: 5.25 us -> 8.31 us
    all_to_all x2 -> x3, waiting for transfers between devices: 0.01 us -> 93.4 us  [the longest x2 59.7 us: gather_over(): return lax.all_to_all(rep, axis, 0, 2, tiled=True)[0]]
    all_gather x1 -> x0, waiting for transfers between devices: 93.1 us -> none  [on_device(): acts_full = lax.all_gather(acts, 'dp', axis=2, tiled=True)]
    all_gather x1 -> x0, blocking collectives: 54.2 us -> none  [on_device(): lax.all_gather(conv_grads, 'seq', axis=0, tiled=False).sum(axis=0)]
    all_to_all x0 -> x1, blocking collectives: none -> 40.9 us  [gather_over(): return lax.all_to_all(rep, axis, 0, 2, tiled=True)[0]]
    all_to_all x2 -> x3, starting transfers between devices: 17.3 us -> 34.9 us  [the longest x2 26.4 us: gather_over(): return lax.all_to_all(rep, axis, 0, 2, tiled=True)[0]]
    slice x3 -> x2, local copies, waits for them, and re-layouts: 7.12 us -> 1.41 us  [the longest x1 0.83 us: on_device(): grad_in_weight = weights[:2]]
    concatenate x1 -> x2, local copies, waits for them, and re-layouts: 0.22 us -> 4.88 us  [on_device(): jnp.concatenate([term_in, term_out_t[None]], axis=0).astype(jnp.bfloat16)]
    unnamed x17 -> x22, local copies, waits for them, and re-layouts: 9.81 us -> 5.16 us
  transfers between devices with their start and end apart: 7 -> 7, of which waited for: 4 -> 6; matrix products, arithmetic and copies ran while one was open for 10% -> 8% of each run, Pallas kernels for 0% -> 0%
where the time goes in v4:
time: 269 us; the launch traced here: 268 us
  waiting for transfers between devices  139 us (52%)
  starting transfers between devices  53.1 us (20%)
  blocking collectives  40.9 us (15%)
  local copies, waits for them, and re-layouts  18.9 us (7%)
  matrix products  8.31 us (3%)
  other arithmetic  6.85 us (3%)
    all_to_all x2, waiting for transfers between devices, gather_over(): return lax.all_to_all(rep, axis, 0, 2, tiled=True)[0]  59.7 us
    all_to_all x2, waiting for transfers between devices, reduce_over_dp(): lax.all_to_all(split, 'dp', 0, 0, tiled=True).astype(jnp.float32)  42.1 us
    all_to_all x1, blocking collectives, gather_over(): return lax.all_to_all(rep, axis, 0, 2, tiled=True)[0]  40.9 us
    all_to_all x1, waiting for transfers between devices, on_device(): lax.all_to_all(sent, 'seq', 0, 0, tiled=True).astype(jnp.float32)  33.7 us
    all_to_all x2, starting transfers between devices, gather_over(): return lax.all_to_all(rep, axis, 0, 2, tiled=True)[0]  26.4 us
    all_to_all x2, starting transfers between devices, reduce_over_dp(): lax.all_to_all(split, 'dp', 0, 0, tiled=True).astype(jnp.float32)  15.1 us
    all_to_all x1, starting transfers between devices, on_device(): lax.all_to_all(sent, 'seq', 0, 0, tiled=True).astype(jnp.float32)  8.44 us
  transfers between devices with their start and end apart: 7, of which 6 were waited for; matrix products, arithmetic and copies ran while one was open for 8% of the time, Pallas kernels for 0%

profile of v4, /device:TPU:1, one launch (start us, length us, event | category | flops | bytes accessed | tf_op | source)
XLA Modules:
  0.0 268.0 jit_solution(2993400404110945042)
XLA Ops:
  0.6 0.0 copy-start.6
  0.6 0.0 copy-start.5
  0.7 2.0 broadcast_in_dim.19
  2.6 17.6 %all-to-all-start.1 = ((bf16[64,128,64]{1,2,0:T(8,128)(2,1)}), bf16[64,128,64]{1,2,0:T(8,128)(2,1)S(1)}, u32[]{:S(2)}, u32[]{:S(2)}) async-start(bf16[64,128,64]{1,2,0:T(8,128)(2,1)} %broadcast_in_dim.19), calls=%async_computation.1 | async-start | bytes 2097152 | tf_op jit(solution)/shard_map/all_to_all | solution.py:20
  20.3 0.0 copy-done.6
  20.3 0.1 copy.24
  20.4 0.0 copy-done.5
  20.5 32.7 %all-to-all-done.1 = bf16[64,128,64]{1,2,0:T(8,128)(2,1)S(1)} async-done(((bf16[64,128,64]{1,2,0:T(8,128)(2,1)}), bf16[64,128,64]{1,2,0:T(8,128)(2,1)S(1)}, u32[]{:S(2)}, u32[]{:S(2)}) %all-to-all-start.1) | async-done | bytes 1048608 | tf_op jit(solution)/shard_map/all_to_all | solution.py:20
  53.2 0.0 copy-start.1
  53.2 1.0 copy-done.1
  54.2 0.7 broadcast_in_dim.17
  54.9 0.0 copy-start.7
  54.9 40.9 %all_to_all.60 = bf16[8,3,512,128]{3,2,1,0:T(8,128)(2,1)S(1)} all-to-all(bf16[8,3,512,128]{3,2,1,0:T(8,128)(2,1)S(1)} %broadcast_in_dim.17), channel_id=1, replica_groups=mesh['dp'=64,'seq'=8] {'seq'}, dimensions={0} | all-to-all | bytes 6291456 | tf_op jit(solution)/shard_map/all_to_all | solution.py:20
  95.8 0.0 copy-done.7
  95.8 0.0 copy-start
  95.8 0.0 copy-start.9
  95.8 0.0 copy-start.8
  95.8 1.4 broadcast_in_dim.20
  97.3 8.8 %all-to-all-start.3 = ((bf16[64,128,64]{1,2,0:T(8,128)(2,1)}), bf16[64,128,64]{1,2,0:T(8,128)(2,1)}, u32[]{:S(2)}, u32[]{:S(2)}) async-start(bf16[64,128,64]{1,2,0:T(8,128)(2,1)} %broadcast_in_dim.20), calls=%async_computation.3 | async-start | bytes 2097152 | tf_op jit(solution)/shard_map/all_to_all | solution.py:20
  106.1 0.0 copy-done.9
  106.1 0.0 copy-done.8
  106.1 0.0 copy-done
  106.1 0.1 slice.122
  106.3 0.0 copy-start.2
  106.3 0.1 copy.25
  106.4 1.1 copy-done.2
  107.5 0.6 fusion.2
  108.1 1.8 collective-permute-start
  109.9 2.3 slice.121
  112.2 27.0 %all-to-all-done.3 = bf16[64,128,64]{1,2,0:T(8,128)(2,1)} async-done(((bf16[64,128,64]{1,2,0:T(8,128)(2,1)}), bf16[64,128,64]{1,2,0:T(8,128)(2,1)}, u32[]{:S(2)}, u32[]{:S(2)}) %all-to-all-start.3) | async-done | bytes 1048608 | tf_op jit(solution)/shard_map/all_to_all | solution.py:20
  139.2 0.0 copy-start.3
  139.2 0.0 collective-permute-done
  139.2 2.1 fusion.18
  141.4 0.0 copy-done.3
  141.4 1.5 convolution_convert_fusion.2
  142.8 7.3 %all-to-all-start.2 = ((bf16[64,64,128]{2,1,0:T(8,128)(2,1)}), bf16[64,64,128]{2,1,0:T(8,128)(2,1)}, u32[]{:S(2)}, u32[]{:S(2)}) async-start(bf16[64,64,128]{2,1,0:T(8,128)(2,1)} %bitcast.110), calls=%async_computation.2 | async-start | bytes 2097152 | tf_op jit(solution)/shard_map/all_to_all | solution.py:33
  150.1 1.3 collective-permute-start.1
  151.4 0.1 fusion.25
  151.5 3.4 %collective-permute-done.1 = bf16[3,128]{1,0:T(4,128)(2,1)S(1)} collective-permute-done((bf16[3,128]{1,0:T(4,128)(2,1)S(1)}, bf16[3,128]{1,0:T(4,128)(2,1)S(1)}, u32[]{:S(2)}, u32[]{:S(2)}) %collective-permute-start.1) | collective-permute-done | bytes 800 | tf_op jit(solution)/shard_map/ppermute | solution.py:10
  154.9 1.7 fusion
  156.6 23.4 %all-to-all-done.2 = bf16[64,64,128]{2,1,0:T(8,128)(2,1)} async-done(((bf16[64,64,128]{2,1,0:T(8,128)(2,1)}), bf16[64,64,128]{2,1,0:T(8,128)(2,1)}, u32[]{:S(2)}, u32[]{:S(2)}) %all-to-all-start.2) | async-done | bytes 1048608 | tf_op jit(solution)/shard_map/all_to_all | solution.py:33
  180.1 7.8 %all-to-all-start.4 = ((bf16[64,64,128]{2,1,0:T(8,128)(2,1)}), bf16[64,64,128]{2,1,0:T(8,128)(2,1)}, u32[]{:S(2)}, u32[]{:S(2)}) async-start(bf16[64,64,128]{2,1,0:T(8,128)(2,1)} %bitcast.29), calls=%async_computation.4 | async-start | bytes 2097152 | tf_op jit(solution)/shard_map/all_to_all | solution.py:33
  187.9 0.1 pad.5.clone
  188.0 1.7 fusion.1
  189.7 1.3 copy.37
  191.0 0.1 maximum_maximum_fusion
  191.1 0.7 convolution_convert_fusion
  191.9 2.2 copy.38
  194.1 0.0 copy-start.4
  194.1 3.5 %copy.29 = bf16[2,8,512,128]{3,2,0,1:T(8,128)(2,1)S(1)} copy(bf16[2,8,512,128]{2,1,3,0:T(8,128)(2,1)} %bitcast.107) | data formatting | bytes 4194304 | tf_op jit(solution)/shard_map/concatenate | solution.py:89
  197.6 0.0 copy-done.4
  197.7 0.3 pad_maximum_fusion.1
  197.9 1.9 pad_maximum_fusion
  199.8 18.7 %all-to-all-done.4 = bf16[64,64,128]{2,1,0:T(8,128)(2,1)} async-done(((bf16[64,64,128]{2,1,0:T(8,128)(2,1)}), bf16[64,64,128]{2,1,0:T(8,128)(2,1)}, u32[]{:S(2)}, u32[]{:S(2)}) %all-to-all-start.4) | async-done | bytes 1048608 | tf_op jit(solution)/shard_map/all_to_all | solution.py:33
  218.5 8.4 %all-to-all-start.5 = ((bf16[8,1552,128]{2,1,0:T(8,128)(2,1)}), bf16[8,1552,128]{2,1,0:T(8,128)(2,1)S(1)}, u32[]{:S(2)}, u32[]{:S(2)}) async-start(bf16[8,1552,128]{2,1,0:T(8,128)(2,1)} %pad_maximum_fusion), calls=%async_computation.5 | async-start | bytes 6356992 | tf_op jit(solution)/shard_map/all_to_all | solution.py:100
  227.0 2.0 reduce_sum.78
  229.0 2.0 reduce_sum.79
  231.0 33.7 %all-to-all-done.5 = bf16[8,1552,128]{2,1,0:T(8,128)(2,1)S(1)} async-done(((bf16[8,1552,128]{2,1,0:T(8,128)(2,1)}), bf16[8,1552,128]{2,1,0:T(8,128)(2,1)S(1)}, u32[]{:S(2)}, u32[]{:S(2)}) %all-to-all-start.5) | async-done | bytes 3178528 | tf_op jit(solution)/shard_map/all_to_all | solution.py:100
  264.7 0.5 convert_reduce_fusion
  265.2 0.8 slice.135
  266.0 0.6 slice.119
  266.6 0.5 slice_bitcast_fusion.4
  267.1 0.8 copy.31
  (12 shorter events, 0.2 us)
Async XLA Ops:
  0.6 19.7 %copy-start.6 = (bf16[128,512]{1,0:T(8,128)(2,1)S(1)}, bf16[128,512]{1,0:T(8,128)(2,1)}, u32[]{:S(2)}) copy-start(bf16[128,512]{1,0:T(8,128)(2,1)} %param.10) | copy-start | bytes 393220
  0.6 19.8 %copy-start.5 = (bf16[2,512,128]{2,1,0:T(8,128)(2,1)S(1)}, bf16[2,512,128]{2,1,0:T(8,128)(2,1)}, u32[]{:S(2)}) copy-start(bf16[2,512,128]{2,1,0:T(8,128)(2,1)} %param.7) | copy-start | bytes 786436
  2.6 50.6 %all-to-all-start.1 = ((bf16[64,128,64]{1,2,0:T(8,128)(2,1)}), bf16[64,128,64]{1,2,0:T(8,128)(2,1)S(1)}, u32[]{:S(2)}, u32[]{:S(2)}) async-start(bf16[64,128,64]{1,2,0:T(8,128)(2,1)} %broadcast_in_dim.19), calls=%async_computation.1 | async-start | bytes 2097152 | tf_op jit(solution)/shard_map/all_to_all | solution.py:20
  53.2 1.0 copy-start.1
  54.9 41.0 %copy-start.7 = (bf16[128,64]{0,1:T(8,128)(2,1)S(1)}, bf16[128,64]{0,1:T(8,128)(2,1)}, u32[]{:S(2)}) copy-start(bf16[128,64]{0,1:T(8,128)(2,1)} %param.11) | copy-start | bytes 49156
  95.8 10.3 %copy-start = (bf16[8,3,512,128]{3,2,1,0:T(8,128)(2,1)}, bf16[8,3,512,128]{3,2,1,0:T(8,128)(2,1)S(1)}, u32[]{:S(2)}) copy-start(bf16[8,3,512,128]{3,2,1,0:T(8,128)(2,1)S(1)} %all_to_all.60) | copy-start | bytes 9437188
  95.8 10.2 %copy-start.9 = (bf16[128]{0:T(256)(128)(2,1)S(1)}, bf16[128]{0:T(256)(128)(2,1)}, u32[]{:S(2)}) copy-start(bf16[128]{0:T(256)(128)(2,1)} %param.9) | copy-start | bytes 772
  95.8 10.2 %copy-start.8 = (bf16[4,128]{1,0:T(4,128)(2,1)S(1)}, bf16[4,128]{1,0:T(4,128)(2,1)}, u32[]{:S(2)}) copy-start(bf16[4,128]{1,0:T(4,128)(2,1)} %param.8) | copy-start | bytes 3076
  97.3 42.0 %all-to-all-start.3 = ((bf16[64,128,64]{1,2,0:T(8,128)(2,1)}), bf16[64,128,64]{1,2,0:T(8,128)(2,1)}, u32[]{:S(2)}, u32[]{:S(2)}) async-start(bf16[64,128,64]{1,2,0:T(8,128)(2,1)} %broadcast_in_dim.20), calls=%async_computation.3 | async-start | bytes 2097152 | tf_op jit(solution)/shard_map/all_to_all | solution.py:20
  106.3 1.2 copy-start.2
  108.1 31.2 %collective-permute-start = (bf16[3,128]{1,0:T(4,128)(2,1)S(1)}, bf16[3,128]{1,0:T(4,128)(2,1)S(1)}, u32[]{:S(2)}, u32[]{:S(2)}) collective-permute-start(bf16[3,128]{1,0:T(4,128)(2,1)S(1)} %slice_bitcast_fusion.3), channel_id=1, source_target_pairs={{0,1},{1,2},{2,3},{3,4},{4,5},{5,6},{6,7},{8,9},{9,10},{10,11},{11... | collective-permute-start | bytes 2312 | tf_op jit(solution)/shard_map/ppermute | solution.py:10
  139.2 2.2 copy-start.3
  142.8 37.2 %all-to-all-start.2 = ((bf16[64,64,128]{2,1,0:T(8,128)(2,1)}), bf16[64,64,128]{2,1,0:T(8,128)(2,1)}, u32[]{:S(2)}, u32[]{:S(2)}) async-start(bf16[64,64,128]{2,1,0:T(8,128)(2,1)} %bitcast.110), calls=%async_computation.2 | async-start | bytes 2097152 | tf_op jit(solution)/shard_map/all_to_all | solution.py:33
  150.1 4.7 %collective-permute-start.1 = (bf16[3,128]{1,0:T(4,128)(2,1)S(1)}, bf16[3,128]{1,0:T(4,128)(2,1)S(1)}, u32[]{:S(2)}, u32[]{:S(2)}) collective-permute-start(bf16[3,128]{1,0:T(4,128)(2,1)S(1)} %slice.130), channel_id=1, source_target_pairs={{1,0},{2,1},{3,2},{4,3},{5,4},{6,5},{7,6},{9,8},{10,9},{11,10},{12... | collective-permute-start | bytes 2312 | tf_op jit(solution)/shard_map/ppermute | solution.py:10
  180.1 38.5 %all-to-all-start.4 = ((bf16[64,64,128]{2,1,0:T(8,128)(2,1)}), bf16[64,64,128]{2,1,0:T(8,128)(2,1)}, u32[]{:S(2)}, u32[]{:S(2)}) async-start(bf16[64,64,128]{2,1,0:T(8,128)(2,1)} %bitcast.29), calls=%async_computation.4 | async-start | bytes 2097152 | tf_op jit(solution)/shard_map/all_to_all | solution.py:33
  194.1 3.6 %copy-start.4 = (bf16[4096,128]{1,0:T(8,128)(2,1)S(1)}, bf16[4096,128]{1,0:T(8,128)(2,1)}, u32[]{:S(2)}) copy-start(bf16[4096,128]{1,0:T(8,128)(2,1)} %copy.37) | copy-start | bytes 3145732
  218.5 46.2 %all-to-all-start.5 = ((bf16[8,1552,128]{2,1,0:T(8,128)(2,1)}), bf16[8,1552,128]{2,1,0:T(8,128)(2,1)S(1)}, u32[]{:S(2)}, u32[]{:S(2)}) async-start(bf16[8,1552,128]{2,1,0:T(8,128)(2,1)} %pad_maximum_fusion), calls=%async_computation.5 | async-start | bytes 6356992 | tf_op jit(solution)/shard_map/all_to_all | solution.py:100

commit v5 on v4

--- a/solution.py
+++ b/solution.py
@@ -38,7 +38,7 @@
     n_seq = lax.axis_size("seq")
     n_dp = lax.axis_size("dp")
     w_local = jnp.concatenate([in_weight, out_weight.T[None]], axis=0)
-    w_full = gather_over(w_local, "seq", n_seq)
+    w_full = lax.all_gather(w_local, "seq", axis=1, tiled=True)
     in_full = w_full[:2]
     out_full_t = w_full[2]
     whole = gather_over(tokens, "dp", n_dp)
@@ -87,25 +87,19 @@
     term_in = jnp.einsum("td,tpe->pde", whole, branch_grads, preferred_element_type=jnp.float32)
     term_out_t = jnp.einsum("td,te->de", upstream, hidden, preferred_element_type=jnp.float32)
     terms = jnp.concatenate([term_in, term_out_t[None]], axis=0).astype(jnp.bfloat16)
-    n_mats, d_full, e_loc = terms.shape
-    d_loc = d_full // n_seq
-    terms = terms.reshape(n_mats, n_seq, d_loc, e_loc).transpose(1, 0, 2, 3)
-    terms = terms.reshape(n_seq, n_mats * d_loc, e_loc)
-    conv_parts = split_exact(conv_grads)
-    n_conv = conv_parts.shape[0]
-    pad_rows = (-n_conv) % 8
-    conv_parts = jnp.concatenate([conv_parts, jnp.zeros((pad_rows, e_loc), jnp.bfloat16)], axis=0)
-    conv_parts = jnp.broadcast_to(conv_parts[None], (n_seq,) + conv_parts.shape)
-    sent = jnp.concatenate([terms, conv_parts], axis=1)
-    summed = lax.all_to_all(sent, "seq", 0, 0, tiled=True).astype(jnp.float32).sum(axis=0)
-    weights = summed[: n_mats * d_loc].reshape(n_mats, d_loc, e_loc)
-    grad_in_weight = weights[:2]
-    grad_out_weight = weights[2].T
-    conv_sum = summed[n_mats * d_loc : n_mats * d_loc + n_conv]
+    terms = lax.psum_scatter(terms, "seq", scatter_dimension=1, tiled=True).astype(jnp.float32)
+    grad_in_weight = terms[:2]
+    grad_out_weight = terms[2].T
     n_row = taps + 1
-    conv_sum = (conv_sum[:n_row] + conv_sum[n_row : 2 * n_row]) + conv_sum[2 * n_row :]
-    tap_grads = conv_sum[:taps]
-    bias_grads = conv_sum[taps]
+    shift = 1
+    while shift < n_seq:
+        parts = lax.ppermute(
+            split_exact(conv_grads), "seq", [(i, (i + shift) % n_seq) for i in range(n_seq)]
+        ).astype(jnp.float32)
+        conv_grads = conv_grads + ((parts[:n_row] + parts[n_row : 2 * n_row]) + parts[2 * n_row :])
+        shift *= 2
+    tap_grads = conv_grads[:taps]
+    bias_grads = conv_grads[taps]
     return (output, grad_tokens, grad_in_weight, grad_out_weight, tap_grads, bias_grads)
 
 

time: 269 us -> 236 us (0.88)
  waiting for transfers between devices: 139 us -> 106 us
  starting transfers between devices: 53.1 us -> 29.8 us
  blocking collectives: 40.9 us -> 59.1 us
  between operations: 0.94 us -> 14.3 us
  local copies, waits for them, and re-layouts: 18.9 us -> 7.13 us
    all_to_all x2 -> x1, waiting for transfers between devices: 59.7 us -> 13.5 us  [gather_over(): return lax.all_to_all(rep, axis, 0, 2, tiled=True)[0]]
    ppermute x0 -> x3, waiting for transfers between devices: none -> 34.5 us  [on_device(): lax.ppermute(split_exact(conv_grads), 'seq', [(i, (i + shift) % n_seq) fo...]
    all_to_all x1 -> x0, waiting for transfers between devices: 33.7 us -> none  [on_device(): lax.all_to_all(sent, 'seq', 0, 0, tiled=True).astype(jnp.float32)]
    all_to_all x2 -> x1, starting transfers between devices: 26.4 us -> 5.41 us  [gather_over(): return lax.all_to_all(rep, axis, 0, 2, tiled=True)[0]]
    all_to_all x1, blocking collectives: 40.9 us -> 59.1 us  [gather_over(): return lax.all_to_all(rep, axis, 0, 2, tiled=True)[0]]
    all_gather x0 -> x1, waiting for transfers between devices: none -> 18 us  [on_device(): w_full = lax.all_gather(w_local, 'seq', axis=1, tiled=True)]
    all_to_all x1 -> x0, starting transfers between devices: 8.44 us -> none  [on_device(): lax.all_to_all(sent, 'seq', 0, 0, tiled=True).astype(jnp.float32)]
    ppermute x0 -> x3, starting transfers between devices: none -> 7.89 us  [on_device(): lax.ppermute(split_exact(conv_grads), 'seq', [(i, (i + shift) % n_seq) fo...]
  transfers between devices with their start and end apart: 7 -> 10, of which waited for: 6 -> 7; matrix products, arithmetic and copies ran while one was open for 8% -> 6% of each run, Pallas kernels for 0% -> 0%
where the time goes in v5:
time: 236 us; the launch traced here: 234 us
  waiting for transfers between devices  106 us (45%)
  blocking collectives  59.1 us (25%)
  starting transfers between devices  29.8 us (13%)
  between operations  14.3 us (6%)
  matrix products  9.98 us (4%)
  other arithmetic  7.73 us (3%)
  local copies, waits for them, and re-layouts  7.13 us (3%)
    all_to_all x1, blocking collectives, gather_over(): return lax.all_to_all(rep, axis, 0, 2, tiled=True)[0]  59.1 us
    all_to_all x2, waiting for transfers between devices, reduce_over_dp(): lax.all_to_all(split, 'dp', 0, 0, tiled=True).astype(jnp.float32)  38.7 us
    ppermute x3, waiting for transfers between devices, on_device(): lax.ppermute(split_exact(conv_grads), 'seq', [(i, (i + shift) % n_seq) fo...  34.5 us
    all_gather x1, waiting for transfers between devices, on_device(): w_full = lax.all_gather(w_local, 'seq', axis=1, tiled=True)  18 us
    all_to_all x2, starting transfers between devices, reduce_over_dp(): lax.all_to_all(split, 'dp', 0, 0, tiled=True).astype(jnp.float32)  13.9 us
    all_to_all x1, waiting for transfers between devices, gather_over(): return lax.all_to_all(rep, axis, 0, 2, tiled=True)[0]  13.5 us
    ppermute x3, starting transfers between devices, on_device(): lax.ppermute(split_exact(conv_grads), 'seq', [(i, (i + shift) % n_seq) fo...  7.89 us
    all_to_all x1, starting transfers between devices, gather_over(): return lax.all_to_all(rep, axis, 0, 2, tiled=True)[0]  5.41 us
  transfers between devices with their start and end apart: 10, of which 7 were waited for; matrix products, arithmetic and copies ran while one was open for 6% of the time, Pallas kernels for 0%

profile of v5, /device:TPU:1, one launch (start us, length us, event | category | flops | bytes accessed | tf_op | source)
XLA Modules:
  0.0 234.0 jit_solution(125686010640678960)
XLA Ops:
  7.2 0.0 copy-start.2
  7.2 0.0 all-gather.2.cloned.1.call-start
  7.2 1.0 copy.17
  8.2 1.7 pad_maximum_fusion.1
  10.0 0.0 all-gather.2.cloned.1.call-update
  10.0 0.0 copy-start.4
  10.0 0.0 copy-start.3
  10.0 1.0 broadcast_in_dim.15
  11.0 59.1 %all_to_all.40 = bf16[64,128,64]{1,2,0:T(8,128)(2,1)} all-to-all(bf16[64,128,64]{1,2,0:T(8,128)(2,1)S(1)} %broadcast_in_dim.15), channel_id=1, replica_groups=mesh['dp'=64,'seq'=8] {'dp'}, dimensions={0} | all-to-all | bytes 2097152 | tf_op jit(solution)/shard_map/all_to_all | solution.py:20
  70.1 0.0 copy-done.2
  70.1 1.3 broadcast_in_dim.16
  71.3 5.4 %all-to-all-start.2 = ((bf16[64,128,64]{1,2,0:T(8,128)(2,1)}), bf16[64,128,64]{1,2,0:T(8,128)(2,1)}, u32[]{:S(2)}, u32[]{:S(2)}) async-start(bf16[64,128,64]{1,2,0:T(8,128)(2,1)} %broadcast_in_dim.16), calls=%async_computation.2 | async-start | bytes 2097152 | tf_op jit(solution)/shard_map/all_to_all | solution.py:20
  76.8 0.0 reduce-scatter.2.cloned.1.call-start
  76.8 0.0 copy-done.4
  76.8 0.0 copy-done.3
  76.9 18.0 %all-gather.2.cloned.1.call-done = bf16[3,4096,128]{2,1,0:T(8,128)(2,1)} async-done(((bf16[3,512,128]{2,1,0:T(8,128)(2,1)}), bf16[3,4096,128]{2,1,0:T(8,128)(2,1)}) %all-gather.2.cloned.1.call-update) | async-done | bytes 3145744 | tf_op jit(solution)/shard_map/all_gather | solution.py:41
  94.9 0.0 copy-start
  94.9 2.6 %fusion.3 = bf16[128,2,128]{2,0,1:T(8,128)(2,1)S(1)} fusion(bf16[3,4096,128]{2,1,0:T(8,128)(2,1)} %all-gather.2.cloned.1.call-done, bf16[128,4096,1]{0,1,2:T(8,128)(2,1)} %bitcast.93), kind=kOutput, calls=%fused_computation.9 | convolution fusion | flops 268468224 | bytes 4259840 | tf_op jit(solution)/shard_map/td,pde->tpe/dot_general | solution.py:48
  97.4 1.3 collective-permute-start
  98.8 13.5 %all-to-all-done.2 = bf16[64,128,64]{1,2,0:T(8,128)(2,1)} async-done(((bf16[64,128,64]{1,2,0:T(8,128)(2,1)}), bf16[64,128,64]{1,2,0:T(8,128)(2,1)}, u32[]{:S(2)}, u32[]{:S(2)}) %all-to-all-start.2) | async-done | bytes 1048608 | tf_op jit(solution)/shard_map/all_to_all | solution.py:20
  112.2 0.0 copy-start.1
  112.2 0.0 collective-permute-done
  112.2 0.0 copy-done
  112.2 1.8 fusion.19
  114.1 1.3 collective-permute-start.1
  115.4 0.1 fusion.26
  115.4 1.7 fusion.2
  117.2 1.2 collective-permute-done.1
  118.4 0.0 copy-done.1
  118.4 0.7 fusion
  119.2 1.9 pad_maximum_fusion
  121.1 0.0 reduce-scatter.2.cloned.1.call-update
  121.1 1.4 convolution_convert_fusion.2
  122.6 7.8 %all-to-all-start.1 = ((bf16[64,64,128]{2,1,0:T(8,128)(2,1)}), bf16[64,64,128]{2,1,0:T(8,128)(2,1)}, u32[]{:S(2)}, u32[]{:S(2)}) async-start(bf16[64,64,128]{2,1,0:T(8,128)(2,1)} %bitcast.95), calls=%async_computation.1 | async-start | bytes 2097152 | tf_op jit(solution)/shard_map/all_to_all | solution.py:33
  130.4 1.7 fusion.1
  132.1 38.7 %all-to-all-done.1 = bf16[64,64,128]{2,1,0:T(8,128)(2,1)} async-done(((bf16[64,64,128]{2,1,0:T(8,128)(2,1)}), bf16[64,64,128]{2,1,0:T(8,128)(2,1)}, u32[]{:S(2)}, u32[]{:S(2)}) %all-to-all-start.1) | async-done | bytes 1048608 | tf_op jit(solution)/shard_map/all_to_all | solution.py:33
  170.8 6.1 %all-to-all-start.3 = ((bf16[64,64,128]{2,1,0:T(8,128)(2,1)}), bf16[64,64,128]{2,1,0:T(8,128)(2,1)S(1)}, u32[]{:S(2)}, u32[]{:S(2)}) async-start(bf16[64,64,128]{2,1,0:T(8,128)(2,1)} %bitcast.25), calls=%async_computation.3 | async-start | bytes 2097152 | tf_op jit(solution)/shard_map/all_to_all | solution.py:33
  176.9 1.9 collective-permute-start.2
  178.8 28.4 %collective-permute-done.2 = bf16[15,128]{1,0:T(8,128)(2,1)S(1)} collective-permute-done((bf16[15,128]{1,0:T(8,128)(2,1)S(1)}, bf16[15,128]{1,0:T(8,128)(2,1)S(1)}, u32[]{:S(2)}, u32[]{:S(2)}) %collective-permute-start.2) | collective-permute-done | bytes 3872 | tf_op jit(solution)/shard_map/ppermute | solution.py:96
  207.3 1.9 collective-permute-start.3
  209.2 5.1 %collective-permute-done.3 = bf16[15,128]{1,0:T(8,128)(2,1)S(1)} collective-permute-done((bf16[15,128]{1,0:T(8,128)(2,1)S(1)}, bf16[15,128]{1,0:T(8,128)(2,1)S(1)}, u32[]{:S(2)}, u32[]{:S(2)}) %collective-permute-start.3) | collective-permute-done | bytes 3872 | tf_op jit(solution)/shard_map/ppermute | solution.py:96
  214.4 4.1 %collective-permute-start.4 = (bf16[15,128]{1,0:T(8,128)(2,1)S(1)}, bf16[15,128]{1,0:T(8,128)(2,1)S(1)}, u32[]{:S(2)}, u32[]{:S(2)}) collective-permute-start(bf16[15,128]{1,0:T(8,128)(2,1)S(1)} %pad_maximum_fusion.9), channel_id=1, source_target_pairs={{0,4},{1,5},{2,6},{3,7},{4,0},{5,1},{6,2},{7,3},{8,12},{9,13},{10,... | collective-permute-start | bytes 11528 | tf_op jit(solution)/shard_map/ppermute | solution.py:96
  218.4 1.0 collective-permute-done.4
  219.4 0.6 slice.126
  220.0 0.5 slice_bitcast_fusion.7
  220.5 2.0 reduce_sum.69
  222.5 0.0 all-to-all-done.3
  222.5 0.8 reduce_sum.70
  223.3 0.0 reduce-scatter.2.cloned.1.call-done
  223.3 1.0 slice.141
  224.3 1.0 copy.21
  225.3 1.1 convert_element_type.163
  226.4 0.7 slice_bitcast_fusion.3
  (19 shorter events, 0.2 us)
Async XLA Ops:
  7.2 62.9 %copy-start.2 = (bf16[128,64]{0,1:T(8,128)(2,1)S(1)}, bf16[128,64]{0,1:T(8,128)(2,1)}, u32[]{:S(2)}) copy-start(bf16[128,64]{0,1:T(8,128)(2,1)} %param.11) | copy-start | bytes 49156
  7.2 87.7 %all-gather.2.cloned.1.call-start = ((), (), s32[]{:S(2)}) async-start(), calls=%async_computation.5 | async-start | bytes 3538944 | tf_op jit(solution)/shard_map/all_gather | solution.py:41
  10.0 66.8 %copy-start.4 = (bf16[128]{0:T(256)(128)(2,1)S(1)}, bf16[128]{0:T(256)(128)(2,1)}, u32[]{:S(2)}) copy-start(bf16[128]{0:T(256)(128)(2,1)} %param.9) | copy-start | bytes 772
  10.0 66.8 %copy-start.3 = (bf16[4,128]{1,0:T(4,128)(2,1)S(1)}, bf16[4,128]{1,0:T(4,128)(2,1)}, u32[]{:S(2)}) copy-start(bf16[4,128]{1,0:T(4,128)(2,1)} %param.8) | copy-start | bytes 3076
  71.3 40.9 %all-to-all-start.2 = ((bf16[64,128,64]{1,2,0:T(8,128)(2,1)}), bf16[64,128,64]{1,2,0:T(8,128)(2,1)}, u32[]{:S(2)}, u32[]{:S(2)}) async-start(bf16[64,128,64]{1,2,0:T(8,128)(2,1)} %broadcast_in_dim.16), calls=%async_computation.2 | async-start | bytes 2097152 | tf_op jit(solution)/shard_map/all_to_all | solution.py:20
  76.8 146.6 %reduce-scatter.2.cloned.1.call-start = ((), (), s32[]{:S(2)}) async-start(), calls=%async_computation.6 | async-start | bytes 3538944 | tf_op jit(solution)/shard_map/reduce_scatter | solution.py:90
  94.9 17.4 %copy-start = (bf16[3,4096,128]{2,1,0:T(8,128)(2,1)S(1)}, bf16[3,4096,128]{2,1,0:T(8,128)(2,1)}, u32[]{:S(2)}) copy-start(bf16[3,4096,128]{2,1,0:T(8,128)(2,1)} %all-gather.2.cloned.1.call-done) | copy-start | bytes 9437188
  97.4 14.8 %collective-permute-start = (bf16[3,128]{1,0:T(4,128)(2,1)S(1)}, bf16[3,128]{1,0:T(4,128)(2,1)S(1)}, u32[]{:S(2)}, u32[]{:S(2)}) collective-permute-start(bf16[3,128]{1,0:T(4,128)(2,1)S(1)} %slice_bitcast_fusion.6), channel_id=1, source_target_pairs={{0,1},{1,2},{2,3},{3,4},{4,5},{5,6},{6,7},{8,9},{9,10},{10,11},{11... | collective-permute-start | bytes 2312 | tf_op jit(solution)/shard_map/ppermute | solution.py:10
  112.2 6.2 %copy-start.1 = (bf16[64,128,64]{1,2,0:T(8,128)(2,1)S(1)}, bf16[64,128,64]{1,2,0:T(8,128)(2,1)}, u32[]{:S(2)}) copy-start(bf16[64,128,64]{1,2,0:T(8,128)(2,1)} %all_to_all.40) | copy-start | bytes 3145732
  114.1 4.3 %collective-permute-start.1 = (bf16[3,128]{1,0:T(4,128)(2,1)S(1)}, bf16[3,128]{1,0:T(4,128)(2,1)S(1)}, u32[]{:S(2)}, u32[]{:S(2)}) collective-permute-start(bf16[3,128]{1,0:T(4,128)(2,1)S(1)} %slice.136), channel_id=1, source_target_pairs={{1,0},{2,1},{3,2},{4,3},{5,4},{6,5},{7,6},{9,8},{10,9},{11,10},{12... | collective-permute-start | bytes 2312 | tf_op jit(solution)/shard_map/ppermute | solution.py:10
  122.6 48.2 %all-to-all-start.1 = ((bf16[64,64,128]{2,1,0:T(8,128)(2,1)}), bf16[64,64,128]{2,1,0:T(8,128)(2,1)}, u32[]{:S(2)}, u32[]{:S(2)}) async-start(bf16[64,64,128]{2,1,0:T(8,128)(2,1)} %bitcast.95), calls=%async_computation.1 | async-start | bytes 2097152 | tf_op jit(solution)/shard_map/all_to_all | solution.py:33
  170.8 51.8 %all-to-all-start.3 = ((bf16[64,64,128]{2,1,0:T(8,128)(2,1)}), bf16[64,64,128]{2,1,0:T(8,128)(2,1)S(1)}, u32[]{:S(2)}, u32[]{:S(2)}) async-start(bf16[64,64,128]{2,1,0:T(8,128)(2,1)} %bitcast.25), calls=%async_computation.3 | async-start | bytes 2097152 | tf_op jit(solution)/shard_map/all_to_all | solution.py:33
  176.9 30.3 %collective-permute-start.2 = (bf16[15,128]{1,0:T(8,128)(2,1)S(1)}, bf16[15,128]{1,0:T(8,128)(2,1)S(1)}, u32[]{:S(2)}, u32[]{:S(2)}) collective-permute-start(bf16[15,128]{1,0:T(8,128)(2,1)S(1)} %pad_maximum_fusion.7), channel_id=1, source_target_pairs={{0,1},{1,2},{2,3},{3,4},{4,5},{5,6},{6,7},{7,0},{8,9},{9,10},{10,1... | collective-permute-start | bytes 11528 | tf_op jit(solution)/shard_map/ppermute | solution.py:96
  207.3 7.0 %collective-permute-start.3 = (bf16[15,128]{1,0:T(8,128)(2,1)S(1)}, bf16[15,128]{1,0:T(8,128)(2,1)S(1)}, u32[]{:S(2)}, u32[]{:S(2)}) collective-permute-start(bf16[15,128]{1,0:T(8,128)(2,1)S(1)} %pad_maximum_fusion.8), channel_id=1, source_target_pairs={{0,2},{1,3},{2,4},{3,5},{4,6},{5,7},{6,0},{7,1},{8,10},{9,11},{10,... | collective-permute-start | bytes 11528 | tf_op jit(solution)/shard_map/ppermute | solution.py:96
  214.4 5.0 %collective-permute-start.4 = (bf16[15,128]{1,0:T(8,128)(2,1)S(1)}, bf16[15,128]{1,0:T(8,128)(2,1)S(1)}, u32[]{:S(2)}, u32[]{:S(2)}) collective-permute-start(bf16[15,128]{1,0:T(8,128)(2,1)S(1)} %pad_maximum_fusion.9), channel_id=1, source_target_pairs={{0,4},{1,5},{2,6},{3,7},{4,0},{5,1},{6,2},{7,3},{8,12},{9,13},{10,... | collective-permute-start | bytes 11528 | tf_op jit(solution)/shard_map/ppermute | solution.py:96
Sparse Core Ops, SparseCore 0:
  10.7 84.1 all-gather.1
  121.3 77.0 reduce-scatter.1

commit v6 on v5

--- a/solution.py
+++ b/solution.py
@@ -15,9 +15,9 @@
     return (value * sig, sig * (1.0 + value * (1.0 - sig)))
 
 
-def gather_over(block, axis, n):
+def gather_over(block, axis, n, dim):
     rep = jnp.broadcast_to(block[None], (n,) + block.shape)
-    return lax.all_to_all(rep, axis, 0, 2, tiled=True)[0]
+    return lax.all_to_all(rep, axis, 0, dim + 1, tiled=True)[0]
 
 
 def split_exact(value):
@@ -29,9 +29,8 @@
 
 
 def reduce_over_dp(part, n_dp):
-    split = part.astype(jnp.bfloat16).reshape(n_dp, part.shape[0] // n_dp, part.shape[1])
-    summed = lax.all_to_all(split, "dp", 0, 0, tiled=True).astype(jnp.float32).sum(axis=0)
-    return summed.T.astype(jnp.bfloat16)
+    split = part.astype(jnp.bfloat16).reshape((n_dp, part.shape[0] // n_dp) + part.shape[1:])
+    return lax.all_to_all(split, "dp", 0, 0, tiled=True).astype(jnp.float32).sum(axis=0)
 
 
 def on_device(tokens, in_weight, conv_weight, conv_bias, out_weight, grad_out):
@@ -41,8 +40,9 @@
     w_full = lax.all_gather(w_local, "seq", axis=1, tiled=True)
     in_full = w_full[:2]
     out_full_t = w_full[2]
-    whole = gather_over(tokens, "dp", n_dp)
-    upstream = gather_over(grad_out, "dp", n_dp)
+    acts = gather_over(jnp.stack([tokens, grad_out], axis=1), "dp", n_dp, 2)
+    whole = acts[:, 0]
+    upstream = acts[:, 1]
     tok_rows = whole.shape[0]
     taps = conv_weight.shape[0]
     mixed = jnp.einsum("td,pde->tpe", whole, in_full, preferred_element_type=jnp.float32).astype(
@@ -82,8 +82,9 @@
     conv_grads = jnp.concatenate([jnp.stack(tap_rows, axis=0), jnp.sum(conv_float, axis=0)[None]], axis=0)
     branch_grads = jnp.stack([grad_inner, grad_gate], axis=1)
     tok_part = jnp.einsum("tpe,pde->dt", branch_grads, in_full, preferred_element_type=jnp.float32)
-    output = reduce_over_dp(out_part, n_dp)
-    grad_tokens = reduce_over_dp(tok_part, n_dp)
+    reduced = reduce_over_dp(jnp.stack([out_part, tok_part], axis=1), n_dp)
+    output = reduced[:, 0].T.astype(jnp.bfloat16)
+    grad_tokens = reduced[:, 1].T.astype(jnp.bfloat16)
     term_in = jnp.einsum("td,tpe->pde", whole, branch_grads, preferred_element_type=jnp.float32)
     term_out_t = jnp.einsum("td,te->de", upstream, hidden, preferred_element_type=jnp.float32)
     terms = jnp.concatenate([term_in, term_out_t[None]], axis=0).astype(jnp.bfloat16)

time: 236 us -> 239 us (1.013)
  blocking collectives: 59.1 us -> 0 us
  waiting for transfers between devices: 106 us -> 149 us
  starting transfers between devices: 29.8 us -> 50.2 us
  local copies, waits for them, and re-layouts: 7.13 us -> 12.5 us
  matrix products: 9.98 us -> 5.21 us
  other arithmetic: 7.73 us -> 5.27 us
    all_to_all x1, waiting for transfers between devices: 13.5 us -> 75.6 us  [gather_over(): return lax.all_to_all(rep, axis, 0, dim + 1, tiled=True)[0]]
    all_to_all x1 -> x0, blocking collectives: 59.1 us -> none  [gather_over(): return lax.all_to_all(rep, axis, 0, 2, tiled=True)[0]]
    all_to_all x2 -> x1, waiting for transfers between devices: 38.7 us -> 0.01 us  [reduce_over_dp(): lax.all_to_all(split, 'dp', 0, 0, tiled=True).astype(jnp.float32)]
    ppermute x3, waiting for transfers between devices: 34.5 us -> 69.4 us  [on_device(): lax.ppermute(split_exact(conv_grads), 'seq', [(i, (i + shift) % n_seq) fo...]
    all_gather x1, waiting for transfers between devices: 18 us -> 0.98 us  [on_device(): w_full = lax.all_gather(w_local, 'seq', axis=1, tiled=True)]
    all_to_all x1, starting transfers between devices: 5.41 us -> 18 us  [gather_over(): return lax.all_to_all(rep, axis, 0, dim + 1, tiled=True)[0]]
    ppermute x3, starting transfers between devices: 7.89 us -> 14.3 us  [on_device(): lax.ppermute(split_exact(conv_grads), 'seq', [(i, (i + shift) % n_seq) fo...]
    reduce_sum x2 -> x1, other arithmetic: 2.79 us -> 0.36 us  [reduce_over_dp(): lax.all_to_all(split, 'dp', 0, 0, tiled=True).astype(jnp.float32)]
  transfers between devices with their start and end apart: 10 -> 9, of which waited for: 7 -> 7; matrix products, arithmetic and copies ran while one was open for 6% -> 4% of each run, Pallas kernels for 0% -> 0%
where the time goes in v6:
time: 239 us; the launch traced here: 237 us
  waiting for transfers between devices  149 us (62%)
  starting transfers between devices  50.2 us (21%)
  between operations  14.3 us (6%)
  local copies, waits for them, and re-layouts  12.5 us (5%)
  other arithmetic  5.27 us (2%)
  matrix products  5.21 us (2%)
    all_to_all x1, waiting for transfers between devices, gather_over(): return lax.all_to_all(rep, axis, 0, dim + 1, tiled=True)[0]  75.6 us
    ppermute x3, waiting for transfers between devices, on_device(): lax.ppermute(split_exact(conv_grads), 'seq', [(i, (i + shift) % n_seq) fo...  69.4 us
    all_to_all x1, starting transfers between devices, gather_over(): return lax.all_to_all(rep, axis, 0, dim + 1, tiled=True)[0]  18 us
    all_to_all x1, starting transfers between devices, reduce_over_dp(): lax.all_to_all(split, 'dp', 0, 0, tiled=True).astype(jnp.float32)  15.3 us
    ppermute x3, starting transfers between devices, on_device(): lax.ppermute(split_exact(conv_grads), 'seq', [(i, (i + shift) % n_seq) fo...  14.3 us
  transfers between devices with their start and end apart: 9, of which 7 were waited for; matrix products, arithmetic and copies ran while one was open for 4% of the time, Pallas kernels for 0%

profile of v6, /device:TPU:1, one launch (start us, length us, event | category | flops | bytes accessed | tf_op | source)
XLA Modules:
  0.0 236.8 jit_solution(3404648204284872978)
XLA Ops:
  7.2 0.0 all-gather.2.cloned.1.call-start
  7.2 1.0 copy.22
  8.2 1.7 pad_maximum_fusion.2
  10.0 0.0 all-gather.2.cloned.1.call-update
  10.0 0.7 pad_maximum_fusion.8
  10.7 1.9 broadcast_in_dim.13
  12.6 0.0 copy-start.4
  12.6 0.0 copy-start.3
  12.6 18.0 %all-to-all-start = ((bf16[64,128,2,64]{1,3,2,0:T(8,128)(2,1)}), bf16[64,128,2,64]{1,3,2,0:T(8,128)(2,1)}, u32[]{:S(2)}, u32[]{:S(2)}) async-start(bf16[64,128,2,64]{1,3,2,0:T(8,128)(2,1)} %broadcast_in_dim.13), calls=%async_computation | async-start | bytes 4194304 | tf_op jit(solution)/shard_map/all_to_all | solution.py:20
  30.6 0.0 reduce-scatter.2.cloned.1.call-start
  30.6 0.0 copy-done.4
  30.6 0.0 copy-done.3
  30.7 75.6 %all-to-all-done = bf16[64,128,2,64]{1,3,2,0:T(8,128)(2,1)} async-done(((bf16[64,128,2,64]{1,3,2,0:T(8,128)(2,1)}), bf16[64,128,2,64]{1,3,2,0:T(8,128)(2,1)}, u32[]{:S(2)}, u32[]{:S(2)}) %all-to-all-start) | async-done | bytes 2097184 | tf_op jit(solution)/shard_map/all_to_all | solution.py:20
  106.3 1.8 copy.23
  108.1 1.0 all-gather.2.cloned.1.call-done
  109.1 0.0 copy-start
  109.1 2.3 fusion.6
  111.4 1.3 collective-permute-start
  112.7 0.7 collective-permute-done
  113.4 0.0 copy-done
  113.4 0.5 fusion.26
  114.0 1.3 collective-permute-start.1
  115.3 0.1 fusion.34
  115.3 0.5 fusion.2
  115.8 2.7 %collective-permute-done.1 = bf16[3,128]{1,0:T(4,128)(2,1)S(1)} collective-permute-done((bf16[3,128]{1,0:T(4,128)(2,1)S(1)}, bf16[3,128]{1,0:T(4,128)(2,1)S(1)}, u32[]{:S(2)}, u32[]{:S(2)}) %collective-permute-start.1) | collective-permute-done | bytes 800 | tf_op jit(solution)/shard_map/ppermute | solution.py:10
  118.6 0.7 fusion
  119.3 2.0 pad_maximum_fusion
  121.3 0.0 slice-start
  121.3 0.0 reduce-scatter.2.cloned.1.call-update
  121.3 0.0 copy-start.1
  121.3 1.2 slice-done
  122.5 0.4 fusion.5
  122.9 0.5 copy-done.1
  123.5 0.7 fusion.1
  124.2 0.2 pad_maximum_fusion.1
  124.4 1.5 copy.25
  125.9 15.3 %all-to-all-start.1 = ((bf16[64,64,2,128]{3,1,2,0:T(8,128)(2,1)}), bf16[64,64,2,128]{3,1,2,0:T(8,128)(2,1)S(1)}, u32[]{:S(2)}, u32[]{:S(2)}) async-start(bf16[64,64,2,128]{3,1,2,0:T(8,128)(2,1)} %copy.25), calls=%async_computation.1 | async-start | bytes 4194304 | tf_op jit(solution)/shard_map/all_to_all | solution.py:33
  141.2 3.7 %collective-permute-start.2 = (bf16[15,128]{1,0:T(8,128)(2,1)S(1)}, bf16[15,128]{1,0:T(8,128)(2,1)S(1)}, u32[]{:S(2)}, u32[]{:S(2)}) collective-permute-start(bf16[15,128]{1,0:T(8,128)(2,1)S(1)} %pad_maximum_fusion.9), channel_id=1, source_target_pairs={{0,1},{1,2},{2,3},{3,4},{4,5},{5,6},{6,7},{7,0},{8,9},{9,10},{10,1... | collective-permute-start | bytes 11528 | tf_op jit(solution)/shard_map/ppermute | solution.py:97
  144.9 63.3 %collective-permute-done.2 = bf16[15,128]{1,0:T(8,128)(2,1)S(1)} collective-permute-done((bf16[15,128]{1,0:T(8,128)(2,1)S(1)}, bf16[15,128]{1,0:T(8,128)(2,1)S(1)}, u32[]{:S(2)}, u32[]{:S(2)}) %collective-permute-start.2) | collective-permute-done | bytes 3872 | tf_op jit(solution)/shard_map/ppermute | solution.py:97
  208.2 1.9 collective-permute-start.3
  210.1 5.1 %collective-permute-done.3 = bf16[15,128]{1,0:T(8,128)(2,1)S(1)} collective-permute-done((bf16[15,128]{1,0:T(8,128)(2,1)S(1)}, bf16[15,128]{1,0:T(8,128)(2,1)S(1)}, u32[]{:S(2)}, u32[]{:S(2)}) %collective-permute-start.3) | collective-permute-done | bytes 3872 | tf_op jit(solution)/shard_map/ppermute | solution.py:97
  215.3 8.7 %collective-permute-start.4 = (bf16[15,128]{1,0:T(8,128)(2,1)S(1)}, bf16[15,128]{1,0:T(8,128)(2,1)S(1)}, u32[]{:S(2)}, u32[]{:S(2)}) collective-permute-start(bf16[15,128]{1,0:T(8,128)(2,1)S(1)} %pad_maximum_fusion.11), channel_id=1, source_target_pairs={{0,4},{1,5},{2,6},{3,7},{4,0},{5,1},{6,2},{7,3},{8,12},{9,13},{10,... | collective-permute-start | bytes 11528 | tf_op jit(solution)/shard_map/ppermute | solution.py:97
  224.0 1.0 collective-permute-done.4
  225.0 0.6 slice.144
  225.6 0.5 slice_bitcast_fusion.12
  226.1 0.0 all-to-all-done.1
  226.1 0.4 reduce
  226.5 0.6 slice_bitcast_fusion.9
  227.1 0.0 reduce-scatter.2.cloned.1.call-done
  227.1 0.0 copy-start.2
  227.1 1.1 slice.164
  228.2 1.0 copy.28
  229.2 0.0 copy-done.2
  229.2 0.1 convert_element_type.163
  229.3 0.7 slice_bitcast_fusion.6
  (19 shorter events, 0.2 us)
Async XLA Ops:
  7.2 101.9 %all-gather.2.cloned.1.call-start = ((), (), s32[]{:S(2)}) async-start(), calls=%async_computation.3 | async-start | bytes 3538944 | tf_op jit(solution)/shard_map/all_gather | solution.py:40
  12.6 18.0 %copy-start.4 = (bf16[128]{0:T(256)(128)(2,1)S(1)}, bf16[128]{0:T(256)(128)(2,1)}, u32[]{:S(2)}) copy-start(bf16[128]{0:T(256)(128)(2,1)} %param.9) | copy-start | bytes 772
  12.6 18.0 %copy-start.3 = (bf16[4,128]{1,0:T(4,128)(2,1)S(1)}, bf16[4,128]{1,0:T(4,128)(2,1)}, u32[]{:S(2)}) copy-start(bf16[4,128]{1,0:T(4,128)(2,1)} %param.8) | copy-start | bytes 3076
  12.6 93.7 %all-to-all-start = ((bf16[64,128,2,64]{1,3,2,0:T(8,128)(2,1)}), bf16[64,128,2,64]{1,3,2,0:T(8,128)(2,1)}, u32[]{:S(2)}, u32[]{:S(2)}) async-start(bf16[64,128,2,64]{1,3,2,0:T(8,128)(2,1)} %broadcast_in_dim.13), calls=%async_computation | async-start | bytes 4194304 | tf_op jit(solution)/shard_map/all_to_all | solution.py:20
  30.6 196.5 %reduce-scatter.2.cloned.1.call-start = ((), (), s32[]{:S(2)}) async-start(), calls=%async_computation.4 | async-start | bytes 3538944 | tf_op jit(solution)/shard_map/reduce_scatter | solution.py:91
  109.1 4.3 %copy-start = (bf16[3,4096,128]{2,1,0:T(8,128)(2,1)S(1)}, bf16[3,4096,128]{2,1,0:T(8,128)(2,1)}, u32[]{:S(2)}) copy-start(bf16[3,4096,128]{2,1,0:T(8,128)(2,1)} %all-gather.2.cloned.1.call-done) | copy-start | bytes 9437188
  111.4 2.0 collective-permute-start
  114.0 4.6 %collective-permute-start.1 = (bf16[3,128]{1,0:T(4,128)(2,1)S(1)}, bf16[3,128]{1,0:T(4,128)(2,1)S(1)}, u32[]{:S(2)}, u32[]{:S(2)}) collective-permute-start(bf16[3,128]{1,0:T(4,128)(2,1)S(1)} %slice.157), channel_id=1, source_target_pairs={{1,0},{2,1},{3,2},{4,3},{5,4},{6,5},{7,6},{9,8},{10,9},{11,10},{12... | collective-permute-start | bytes 2312 | tf_op jit(solution)/shard_map/ppermute | solution.py:10
  121.3 1.2 slice-start
  121.3 2.2 copy-start.1
  125.9 100.2 %all-to-all-start.1 = ((bf16[64,64,2,128]{3,1,2,0:T(8,128)(2,1)}), bf16[64,64,2,128]{3,1,2,0:T(8,128)(2,1)S(1)}, u32[]{:S(2)}, u32[]{:S(2)}) async-start(bf16[64,64,2,128]{3,1,2,0:T(8,128)(2,1)} %copy.25), calls=%async_computation.1 | async-start | bytes 4194304 | tf_op jit(solution)/shard_map/all_to_all | solution.py:33
  141.2 66.9 %collective-permute-start.2 = (bf16[15,128]{1,0:T(8,128)(2,1)S(1)}, bf16[15,128]{1,0:T(8,128)(2,1)S(1)}, u32[]{:S(2)}, u32[]{:S(2)}) collective-permute-start(bf16[15,128]{1,0:T(8,128)(2,1)S(1)} %pad_maximum_fusion.9), channel_id=1, source_target_pairs={{0,1},{1,2},{2,3},{3,4},{4,5},{5,6},{6,7},{7,0},{8,9},{9,10},{10,1... | collective-permute-start | bytes 11528 | tf_op jit(solution)/shard_map/ppermute | solution.py:97
  208.2 7.0 %collective-permute-start.3 = (bf16[15,128]{1,0:T(8,128)(2,1)S(1)}, bf16[15,128]{1,0:T(8,128)(2,1)S(1)}, u32[]{:S(2)}, u32[]{:S(2)}) collective-permute-start(bf16[15,128]{1,0:T(8,128)(2,1)S(1)} %pad_maximum_fusion.10), channel_id=1, source_target_pairs={{0,2},{1,3},{2,4},{3,5},{4,6},{5,7},{6,0},{7,1},{8,10},{9,11},{10,... | collective-permute-start | bytes 11528 | tf_op jit(solution)/shard_map/ppermute | solution.py:97
  215.3 9.7 %collective-permute-start.4 = (bf16[15,128]{1,0:T(8,128)(2,1)S(1)}, bf16[15,128]{1,0:T(8,128)(2,1)S(1)}, u32[]{:S(2)}, u32[]{:S(2)}) collective-permute-start(bf16[15,128]{1,0:T(8,128)(2,1)S(1)} %pad_maximum_fusion.11), channel_id=1, source_target_pairs={{0,4},{1,5},{2,6},{3,7},{4,0},{5,1},{6,2},{7,3},{8,12},{9,13},{10,... | collective-permute-start | bytes 11528 | tf_op jit(solution)/shard_map/ppermute | solution.py:97
  227.1 2.1 copy-start.2
Sparse Core Ops, SparseCore 0:
  10.7 98.3 all-gather.1
  121.4 97.1 reduce-scatter.1

commit v7 on v6

--- a/solution.py
+++ b/solution.py
@@ -2,6 +2,9 @@
 import jax.numpy as jnp
 from jax import lax
 from jax.sharding import PartitionSpec as P
+
+
+DP = ("chip", "core")
 
 
 def from_behind(block, axis, distance):
@@ -28,19 +31,25 @@
     return jnp.concatenate([hi, mid, lo], axis=0)
 
 
-def reduce_over_dp(part, n_dp):
-    split = part.astype(jnp.bfloat16).reshape((n_dp, part.shape[0] // n_dp) + part.shape[1:])
-    return lax.all_to_all(split, "dp", 0, 0, tiled=True).astype(jnp.float32).sum(axis=0)
+def reduce_over_dp(part, n_chip, n_core):
+    split = part.reshape((n_chip, n_core, part.shape[0] // (n_chip * n_core)) + part.shape[1:])
+    split = lax.all_to_all(split, "core", 1, 1, tiled=True).sum(axis=1)
+    split = split.astype(jnp.bfloat16)
+    return lax.all_to_all(split, "chip", 0, 0, tiled=True).astype(jnp.float32).sum(axis=0)
 
 
 def on_device(tokens, in_weight, conv_weight, conv_bias, out_weight, grad_out):
     n_seq = lax.axis_size("seq")
-    n_dp = lax.axis_size("dp")
+    n_chip = lax.axis_size("chip")
+    n_core = lax.axis_size("core")
+    n_dp = n_chip * n_core
     w_local = jnp.concatenate([in_weight, out_weight.T[None]], axis=0)
     w_full = lax.all_gather(w_local, "seq", axis=1, tiled=True)
     in_full = w_full[:2]
     out_full_t = w_full[2]
-    acts = gather_over(jnp.stack([tokens, grad_out], axis=1), "dp", n_dp, 2)
+    acts = gather_over(jnp.stack([tokens, grad_out], axis=1), "chip", n_chip, 2)
+    acts = gather_over(acts.reshape(acts.shape[:2] + (n_chip, 1, -1)), "core", n_core, 3)
+    acts = acts.reshape(acts.shape[:2] + (-1,))
     whole = acts[:, 0]
     upstream = acts[:, 1]
     tok_rows = whole.shape[0]
@@ -82,7 +91,7 @@
     conv_grads = jnp.concatenate([jnp.stack(tap_rows, axis=0), jnp.sum(conv_float, axis=0)[None]], axis=0)
     branch_grads = jnp.stack([grad_inner, grad_gate], axis=1)
     tok_part = jnp.einsum("tpe,pde->dt", branch_grads, in_full, preferred_element_type=jnp.float32)
-    reduced = reduce_over_dp(jnp.stack([out_part, tok_part], axis=1), n_dp)
+    reduced = reduce_over_dp(jnp.stack([out_part, tok_part], axis=1), n_chip, n_core)
     output = reduced[:, 0].T.astype(jnp.bfloat16)
     grad_tokens = reduced[:, 1].T.astype(jnp.bfloat16)
     term_in = jnp.einsum("td,tpe->pde", whole, branch_grads, preferred_element_type=jnp.float32)
@@ -105,24 +114,27 @@
 
 
 def solution(mesh):
+    n_core = 2
+    devices = mesh.devices.reshape(mesh.devices.shape[0] // n_core, n_core, mesh.devices.shape[1])
+    split_mesh = jax.sharding.Mesh(devices, ("chip", "core", "seq"))
     return jax.shard_map(
         on_device,
-        mesh=mesh,
+        mesh=split_mesh,
         in_specs=(
-            P("seq", "dp"),
-            P(None, "seq", "dp"),
-            P(None, "dp"),
-            P("dp"),
-            P("dp", "seq"),
-            P("seq", "dp"),
+            P("seq", DP),
+            P(None, "seq", DP),
+            P(None, DP),
+            P(DP),
+            P(DP, "seq"),
+            P("seq", DP),
         ),
         out_specs=(
-            P("seq", "dp"),
-            P("seq", "dp"),
-            P(None, "seq", "dp"),
-            P("dp", "seq"),
-            P(None, "dp"),
-            P("dp"),
+            P("seq", DP),
+            P("seq", DP),
+            P(None, "seq", DP),
+            P(DP, "seq"),
+            P(None, DP),
+            P(DP),
         ),
         check_vma=False,
     )

time: 239 us -> 192 us (0.80)
  waiting for transfers between devices: 149 us -> 86.9 us
  blocking collectives: 0 us -> 20.7 us
  starting transfers between devices: 50.2 us -> 43.4 us
  other arithmetic: 5.27 us -> 8.2 us
    all_to_all x1, waiting for transfers between devices: 75.6 us -> 36.2 us  [gather_over(): return lax.all_to_all(rep, axis, 0, dim + 1, tiled=True)[0]]
    ppermute x3, waiting for transfers between devices: 69.4 us -> 38.8 us  [on_device(): lax.ppermute(split_exact(conv_grads), 'seq', [(i, (i + shift) % n_seq) fo...]
    all_to_all x0 -> x2, blocking collectives: none -> 20.7 us  [the longest x1 10.8 us: reduce_over_dp(): split = lax.all_to_all(split, 'core', 1, 1, tiled=True).sum(axis=1)]
    all_gather x1, waiting for transfers between devices: 0.98 us -> 8.53 us  [on_device(): w_full = lax.all_gather(w_local, 'seq', axis=1, tiled=True)]
    all_to_all x1, starting transfers between devices: 15.3 us -> 11.6 us  [reduce_over_dp(): lax.all_to_all(split, 'chip', 0, 0, tiled=True).astype(jnp.float32)]
    ppermute x3, starting transfers between devices: 14.3 us -> 11.6 us  [on_device(): lax.ppermute(split_exact(conv_grads), 'seq', [(i, (i + shift) % n_seq) fo...]
    reduce_sum x1 -> x2, other arithmetic: 0.36 us -> 2.91 us  [the longest x1 2.75 us: reduce_over_dp(): split = lax.all_to_all(split, 'core', 1, 1, tiled=True).sum(axis=1)]
  transfers between devices with their start and end apart: 9 -> 9, of which waited for: 7 -> 7; matrix products, arithmetic and copies ran while one was open for 4% -> 6% of each run, Pallas kernels for 0% -> 0%
where the time goes in v7:
time: 192 us; the launch traced here: 190 us
  waiting for transfers between devices  86.9 us (45%)
  starting transfers between devices  43.4 us (23%)
  blocking collectives  20.7 us (11%)
  between operations  14.3 us (7%)
  local copies, waits for them, and re-layouts  11.1 us (6%)
  other arithmetic  8.2 us (4%)
  matrix products  5.2 us (3%)
    ppermute x3, waiting for transfers between devices, on_device(): lax.ppermute(split_exact(conv_grads), 'seq', [(i, (i + shift) % n_seq) fo...  38.8 us
    all_to_all x1, waiting for transfers between devices, gather_over(): return lax.all_to_all(rep, axis, 0, dim + 1, tiled=True)[0]  36.2 us
    all_to_all x1, starting transfers between devices, gather_over(): return lax.all_to_all(rep, axis, 0, dim + 1, tiled=True)[0]  16.5 us
    ppermute x3, starting transfers between devices, on_device(): lax.ppermute(split_exact(conv_grads), 'seq', [(i, (i + shift) % n_seq) fo...  11.6 us
    all_to_all x1, starting transfers between devices, reduce_over_dp(): lax.all_to_all(split, 'chip', 0, 0, tiled=True).astype(jnp.float32)  11.6 us
    all_to_all x1, blocking collectives, reduce_over_dp(): split = lax.all_to_all(split, 'core', 1, 1, tiled=True).sum(axis=1)  10.8 us
    all_to_all x1, blocking collectives, gather_over(): return lax.all_to_all(rep, axis, 0, dim + 1, tiled=True)[0]  9.93 us
    all_gather x1, waiting for transfers between devices, on_device(): w_full = lax.all_gather(w_local, 'seq', axis=1, tiled=True)  8.53 us
  transfers between devices with their start and end apart: 9, of which 7 were waited for; matrix products, arithmetic and copies ran while one was open for 6% of the time, Pallas kernels for 0%

profile of v7, /device:TPU:1, one launch (start us, length us, event | category | flops | bytes accessed | tf_op | source)
XLA Modules:
  0.0 189.9 jit_solution(9721975194448600780)
XLA Ops:
  7.2 0.0 all-gather.2.cloned.1.call-start
  7.2 1.0 copy.31
  8.2 0.0 copy-start.4
  8.2 0.0 copy-start.3
  8.3 1.7 pad_maximum_fusion.2
  10.0 0.0 all-gather.2.cloned.1.call-update
  10.0 0.7 pad_maximum_fusion.8
  10.8 1.2 broadcast_in_dim.17
  12.0 16.5 %all-to-all-start = ((bf16[32,128,2,64]{1,3,2,0:T(8,128)(2,1)}), bf16[32,128,2,64]{1,3,2,0:T(8,128)(2,1)S(1)}, u32[]{:S(2)}, u32[]{:S(2)}) async-start(bf16[32,128,2,64]{1,3,2,0:T(8,128)(2,1)} %broadcast_in_dim.17), calls=%async_computation | async-start | bytes 2097152 | tf_op jit(solution)/shard_map/all_to_all | solution.py:23
  28.5 0.0 reduce-scatter.2.cloned.1.call-start
  28.6 0.0 copy-done.4
  28.6 0.0 copy-done.3
  28.6 36.2 %all-to-all-done = bf16[32,128,2,64]{1,3,2,0:T(8,128)(2,1)S(1)} async-done(((bf16[32,128,2,64]{1,3,2,0:T(8,128)(2,1)}), bf16[32,128,2,64]{1,3,2,0:T(8,128)(2,1)S(1)}, u32[]{:S(2)}, u32[]{:S(2)}) %all-to-all-start) | async-done | bytes 1048608 | tf_op jit(solution)/shard_map/all_to_all | solution.py:23
  64.8 0.1 copy.32
  64.9 0.6 broadcast_in_dim.19
  65.6 9.9 %all_to_all.40 = bf16[2,128,2,32,1,64]{1,5,3,2,4,0:T(8,128)(2,1)S(1)} all-to-all(bf16[2,128,2,32,1,64]{1,5,3,2,4,0:T(8,128)(2,1)S(1)} %broadcast_in_dim.19), channel_id=1, replica_groups=mesh['chip'=32,'core'=2,'seq'=8] {'core'}, dimensions={0} | all-to-all | bytes 4194304 | tf_op jit(solution)/shard_map/all_to_all | solution.py:23
  75.5 0.2 copy.33
  75.7 8.5 %all-gather.2.cloned.1.call-done = bf16[3,4096,128]{2,1,0:T(8,128)(2,1)} async-done(((bf16[3,512,128]{2,1,0:T(8,128)(2,1)}), bf16[3,4096,128]{2,1,0:T(8,128)(2,1)}) %all-gather.2.cloned.1.call-update) | async-done | bytes 3145744 | tf_op jit(solution)/shard_map/all_gather | solution.py:47
  84.2 0.0 copy-start
  84.2 2.3 %fusion.4 = bf16[128,2,128]{2,0,1:T(8,128)(2,1)S(1)} fusion(bf16[3,4096,128]{2,1,0:T(8,128)(2,1)} %all-gather.2.cloned.1.call-done, bf16[128,2,4096]{0,2,1:T(8,128)(2,1)S(1)} %bitcast.108), kind=kOutput, calls=%fused_computation.9 | convolution fusion | flops 268468224 | bytes 3211264 | tf_op jit(solution)/shard_map/td,pde->tpe/dot_general | solution.py:57
  86.5 2.3 %collective-permute-start = (bf16[3,128]{1,0:T(4,128)(2,1)S(1)}, bf16[3,128]{1,0:T(4,128)(2,1)S(1)}, u32[]{:S(2)}, u32[]{:S(2)}) collective-permute-start(bf16[3,128]{1,0:T(4,128)(2,1)S(1)} %slice_bitcast_fusion.11), channel_id=1, source_target_pairs={{0,1},{1,2},{2,3},{3,4},{4,5},{5,6},{6,7},{8,9},{9,10},{10,11},{11... | collective-permute-start | bytes 2312 | tf_op jit(solution)/shard_map/ppermute | solution.py:13
  88.9 0.7 collective-permute-done
  89.6 0.0 copy-done
  89.6 0.5 fusion.24
  90.1 1.3 collective-permute-start.1
  91.4 0.1 fusion.33
  91.5 0.5 fusion.1
  92.0 2.7 %collective-permute-done.1 = bf16[3,128]{1,0:T(4,128)(2,1)S(1)} collective-permute-done((bf16[3,128]{1,0:T(4,128)(2,1)S(1)}, bf16[3,128]{1,0:T(4,128)(2,1)S(1)}, u32[]{:S(2)}, u32[]{:S(2)}) %collective-permute-start.1) | collective-permute-done | bytes 800 | tf_op jit(solution)/shard_map/ppermute | solution.py:13
  94.7 0.7 fusion
  95.4 2.0 %pad_maximum_fusion.1 = bf16[3,4096,128]{1,2,0:T(8,128)(2,1)} fusion(bf16[1,4096,128]{1,2,0:T(8,128)(2,1)S(1)} %fusion.1, bf16[2,4096,128]{1,2,0:T(8,128)(2,1)S(1)} %fusion), kind=kLoop, calls=%fused_computation.5 | loop fusion | flops 1572864 | bytes 6291456 | tf_op jit(solution)/shard_map/concatenate | solution.py:99
  97.4 0.0 slice-start
  97.4 0.0 reduce-scatter.2.cloned.1.call-update
  97.4 0.0 copy-start.1
  97.4 1.2 slice-done
  98.6 0.4 convolution_bitcast_fusion
  99.1 0.5 copy-done.1
  99.6 0.7 fusion.27
  100.3 0.6 pad_maximum_fusion
  100.9 0.6 copy.35
  101.5 10.8 %all_to_all.41 = f32[32,2,64,2,128]{4,2,0,3,1:T(8,128)} all-to-all(f32[32,2,64,2,128]{4,2,0,3,1:T(8,128)S(1)} %copy.35), channel_id=1, replica_groups=mesh['chip'=32,'core'=2,'seq'=8] {'core'}, dimensions={1} | all-to-all | bytes 8388608 | tf_op jit(solution)/shard_map/all_to_all | solution.py:36
  112.3 2.7 %reduce_sum.63 = bf16[32,64,2,128]{3,1,0,2:T(8,128)(2,1)S(1)} reduce(f32[32,2,64,2,128]{4,2,0,3,1:T(8,128)} %all_to_all.41, f32[]{:T(128)} %constant.1.clone.1), dimensions={1}, to_apply=%region_0.0 | reduce | flops 524288 | bytes 5242884 | tf_op jit(solution)/shard_map/reduce_sum | solution.py:36
  115.0 1.1 copy.37
  116.1 11.6 %all-to-all-start.3 = ((bf16[32,64,2,128]{3,1,2,0:T(8,128)(2,1)}), bf16[32,64,2,128]{3,1,2,0:T(8,128)(2,1)S(1)}, u32[]{:S(2)}, u32[]{:S(2)}) async-start(bf16[32,64,2,128]{3,1,2,0:T(8,128)(2,1)} %copy.37), calls=%async_computation.3 | async-start | bytes 2097152 | tf_op jit(solution)/shard_map/all_to_all | solution.py:38
  127.7 3.6 %collective-permute-start.2 = (bf16[15,128]{1,0:T(8,128)(2,1)S(1)}, bf16[15,128]{1,0:T(8,128)(2,1)S(1)}, u32[]{:S(2)}, u32[]{:S(2)}) collective-permute-start(bf16[15,128]{1,0:T(8,128)(2,1)S(1)} %pad_maximum_fusion.9), channel_id=1, source_target_pairs={{0,1},{1,2},{2,3},{3,4},{4,5},{5,6},{6,7},{7,0},{8,9},{9,10},{10,1... | collective-permute-start | bytes 11528 | tf_op jit(solution)/shard_map/ppermute | solution.py:106
  131.4 32.9 %collective-permute-done.2 = bf16[15,128]{1,0:T(8,128)(2,1)S(1)} collective-permute-done((bf16[15,128]{1,0:T(8,128)(2,1)S(1)}, bf16[15,128]{1,0:T(8,128)(2,1)S(1)}, u32[]{:S(2)}, u32[]{:S(2)}) %collective-permute-start.2) | collective-permute-done | bytes 3872 | tf_op jit(solution)/shard_map/ppermute | solution.py:106
  164.4 1.9 %collective-permute-start.3 = (bf16[15,128]{1,0:T(8,128)(2,1)S(1)}, bf16[15,128]{1,0:T(8,128)(2,1)S(1)}, u32[]{:S(2)}, u32[]{:S(2)}) collective-permute-start(bf16[15,128]{1,0:T(8,128)(2,1)S(1)} %pad_maximum_fusion.10), channel_id=1, source_target_pairs={{0,2},{1,3},{2,4},{3,5},{4,6},{5,7},{6,0},{7,1},{8,10},{9,11},{10,... | collective-permute-start | bytes 11528 | tf_op jit(solution)/shard_map/ppermute | solution.py:106
  166.3 4.9 %collective-permute-done.3 = bf16[15,128]{1,0:T(8,128)(2,1)S(1)} collective-permute-done((bf16[15,128]{1,0:T(8,128)(2,1)S(1)}, bf16[15,128]{1,0:T(8,128)(2,1)S(1)}, u32[]{:S(2)}, u32[]{:S(2)}) %collective-permute-start.3) | collective-permute-done | bytes 3872 | tf_op jit(solution)/shard_map/ppermute | solution.py:106
  171.2 6.1 %collective-permute-start.4 = (bf16[15,128]{1,0:T(8,128)(2,1)S(1)}, bf16[15,128]{1,0:T(8,128)(2,1)S(1)}, u32[]{:S(2)}, u32[]{:S(2)}) collective-permute-start(bf16[15,128]{1,0:T(8,128)(2,1)S(1)} %pad_maximum_fusion.11), channel_id=1, source_target_pairs={{0,4},{1,5},{2,6},{3,7},{4,0},{5,1},{6,2},{7,3},{8,12},{9,13},{10,... | collective-permute-start | bytes 11528 | tf_op jit(solution)/shard_map/ppermute | solution.py:106
  177.3 1.0 collective-permute-done.4
  178.3 0.6 slice.144
  178.9 0.5 slice_bitcast_fusion.12
  179.4 0.0 all-to-all-done.3
  179.4 0.2 reduce
  179.5 0.6 slice_bitcast_fusion.9
  180.2 0.0 reduce-scatter.2.cloned.1.call-done
  180.2 0.0 copy-start.2
  180.2 1.1 slice.164
  181.2 1.0 copy.40
  182.2 0.0 copy-done.2
  182.3 0.1 convert_element_type.165
  182.3 0.7 slice_bitcast_fusion.6
  (19 shorter events, 0.2 us)
Async XLA Ops:
  7.2 77.0 %all-gather.2.cloned.1.call-start = ((), (), s32[]{:S(2)}) async-start(), calls=%async_computation.5 | async-start | bytes 3538944 | tf_op jit(solution)/shard_map/all_gather | solution.py:47
  8.2 20.4 %copy-start.4 = (bf16[128]{0:T(256)(128)(2,1)S(1)}, bf16[128]{0:T(256)(128)(2,1)}, u32[]{:S(2)}) copy-start(bf16[128]{0:T(256)(128)(2,1)} %param.9) | copy-start | bytes 772
  8.2 20.4 %copy-start.3 = (bf16[4,128]{1,0:T(4,128)(2,1)S(1)}, bf16[4,128]{1,0:T(4,128)(2,1)}, u32[]{:S(2)}) copy-start(bf16[4,128]{1,0:T(4,128)(2,1)} %param.8) | copy-start | bytes 3076
  12.0 52.8 %all-to-all-start = ((bf16[32,128,2,64]{1,3,2,0:T(8,128)(2,1)}), bf16[32,128,2,64]{1,3,2,0:T(8,128)(2,1)S(1)}, u32[]{:S(2)}, u32[]{:S(2)}) async-start(bf16[32,128,2,64]{1,3,2,0:T(8,128)(2,1)} %broadcast_in_dim.17), calls=%async_computation | async-start | bytes 2097152 | tf_op jit(solution)/shard_map/all_to_all | solution.py:23
  28.5 151.6 %reduce-scatter.2.cloned.1.call-start = ((), (), s32[]{:S(2)}) async-start(), calls=%async_computation.6 | async-start | bytes 3538944 | tf_op jit(solution)/shard_map/reduce_scatter | solution.py:100
  84.2 5.4 %copy-start = (bf16[3,4096,128]{2,1,0:T(8,128)(2,1)S(1)}, bf16[3,4096,128]{2,1,0:T(8,128)(2,1)}, u32[]{:S(2)}) copy-start(bf16[3,4096,128]{2,1,0:T(8,128)(2,1)} %all-gather.2.cloned.1.call-done) | copy-start | bytes 9437188
  86.5 3.0 %collective-permute-start = (bf16[3,128]{1,0:T(4,128)(2,1)S(1)}, bf16[3,128]{1,0:T(4,128)(2,1)S(1)}, u32[]{:S(2)}, u32[]{:S(2)}) collective-permute-start(bf16[3,128]{1,0:T(4,128)(2,1)S(1)} %slice_bitcast_fusion.11), channel_id=1, source_target_pairs={{0,1},{1,2},{2,3},{3,4},{4,5},{5,6},{6,7},{8,9},{9,10},{10,11},{11... | collective-permute-start | bytes 2312 | tf_op jit(solution)/shard_map/ppermute | solution.py:13
  90.1 4.6 %collective-permute-start.1 = (bf16[3,128]{1,0:T(4,128)(2,1)S(1)}, bf16[3,128]{1,0:T(4,128)(2,1)S(1)}, u32[]{:S(2)}, u32[]{:S(2)}) collective-permute-start(bf16[3,128]{1,0:T(4,128)(2,1)S(1)} %slice.157), channel_id=1, source_target_pairs={{1,0},{2,1},{3,2},{4,3},{5,4},{6,5},{7,6},{9,8},{10,9},{11,10},{12... | collective-permute-start | bytes 2312 | tf_op jit(solution)/shard_map/ppermute | solution.py:13
  97.4 1.2 slice-start
  97.4 2.2 %copy-start.1 = (bf16[3,4096,128]{2,1,0:T(8,128)(2,1)S(1)}, bf16[3,4096,128]{2,1,0:T(8,128)(2,1)}, u32[]{:S(2)}) copy-start(bf16[3,4096,128]{2,1,0:T(8,128)(2,1)} %all-gather.2.cloned.1.call-done) | copy-start | bytes 9437188
  116.1 63.3 %all-to-all-start.3 = ((bf16[32,64,2,128]{3,1,2,0:T(8,128)(2,1)}), bf16[32,64,2,128]{3,1,2,0:T(8,128)(2,1)S(1)}, u32[]{:S(2)}, u32[]{:S(2)}) async-start(bf16[32,64,2,128]{3,1,2,0:T(8,128)(2,1)} %copy.37), calls=%async_computation.3 | async-start | bytes 2097152 | tf_op jit(solution)/shard_map/all_to_all | solution.py:38
  127.7 36.6 %collective-permute-start.2 = (bf16[15,128]{1,0:T(8,128)(2,1)S(1)}, bf16[15,128]{1,0:T(8,128)(2,1)S(1)}, u32[]{:S(2)}, u32[]{:S(2)}) collective-permute-start(bf16[15,128]{1,0:T(8,128)(2,1)S(1)} %pad_maximum_fusion.9), channel_id=1, source_target_pairs={{0,1},{1,2},{2,3},{3,4},{4,5},{5,6},{6,7},{7,0},{8,9},{9,10},{10,1... | collective-permute-start | bytes 11528 | tf_op jit(solution)/shard_map/ppermute | solution.py:106
  164.4 6.8 %collective-permute-start.3 = (bf16[15,128]{1,0:T(8,128)(2,1)S(1)}, bf16[15,128]{1,0:T(8,128)(2,1)S(1)}, u32[]{:S(2)}, u32[]{:S(2)}) collective-permute-start(bf16[15,128]{1,0:T(8,128)(2,1)S(1)} %pad_maximum_fusion.10), channel_id=1, source_target_pairs={{0,2},{1,3},{2,4},{3,5},{4,6},{5,7},{6,0},{7,1},{8,10},{9,11},{10,... | collective-permute-start | bytes 11528 | tf_op jit(solution)/shard_map/ppermute | solution.py:106
  171.2 7.1 %collective-permute-start.4 = (bf16[15,128]{1,0:T(8,128)(2,1)S(1)}, bf16[15,128]{1,0:T(8,128)(2,1)S(1)}, u32[]{:S(2)}, u32[]{:S(2)}) collective-permute-start(bf16[15,128]{1,0:T(8,128)(2,1)S(1)} %pad_maximum_fusion.11), channel_id=1, source_target_pairs={{0,4},{1,5},{2,6},{3,7},{4,0},{5,1},{6,2},{7,3},{8,12},{9,13},{10,... | collective-permute-start | bytes 11528 | tf_op jit(solution)/shard_map/ppermute | solution.py:106
  180.2 2.1 %copy-start.2 = (bf16[3,512,128]{1,2,0:T(8,128)(2,1)S(1)}, bf16[3,512,128]{1,2,0:T(8,128)(2,1)}, u32[]{:S(2)}) copy-start(bf16[3,512,128]{1,2,0:T(8,128)(2,1)} %reduce-scatter.2.cloned.1.call-done) | copy-start | bytes 1179652
Sparse Core Ops, SparseCore 0:
  10.7 73.4 all-gather.1
  97.5 76.1 reduce-scatter.1

commit v8 on v7

--- a/solution.py
+++ b/solution.py
@@ -96,20 +96,25 @@
     grad_tokens = reduced[:, 1].T.astype(jnp.bfloat16)
     term_in = jnp.einsum("td,tpe->pde", whole, branch_grads, preferred_element_type=jnp.float32)
     term_out_t = jnp.einsum("td,te->de", upstream, hidden, preferred_element_type=jnp.float32)
-    terms = jnp.concatenate([term_in, term_out_t[None]], axis=0).astype(jnp.bfloat16)
-    terms = lax.psum_scatter(terms, "seq", scatter_dimension=1, tiled=True).astype(jnp.float32)
-    grad_in_weight = terms[:2]
-    grad_out_weight = terms[2].T
+    grad_in_weight = lax.psum_scatter(
+        term_in.astype(jnp.bfloat16), "seq", scatter_dimension=1, tiled=True
+    ).astype(jnp.float32)
+    d_full, e_loc = term_out_t.shape
+    d_loc = d_full // n_seq
+    sent = term_out_t.astype(jnp.bfloat16).reshape(n_seq, d_loc, e_loc)
+    conv_parts = split_exact(conv_grads)
+    n_conv = conv_parts.shape[0]
+    pad_rows = (-n_conv) % 8
+    conv_parts = jnp.concatenate([conv_parts, jnp.zeros((pad_rows, e_loc), jnp.bfloat16)], axis=0)
+    conv_parts = jnp.broadcast_to(conv_parts[None], (n_seq,) + conv_parts.shape)
+    sent = jnp.concatenate([sent, conv_parts], axis=1)
+    summed = lax.all_to_all(sent, "seq", 0, 0, tiled=True).astype(jnp.float32).sum(axis=0)
+    grad_out_weight = summed[:d_loc].T
+    conv_sum = summed[d_loc : d_loc + n_conv]
     n_row = taps + 1
-    shift = 1
-    while shift < n_seq:
-        parts = lax.ppermute(
-            split_exact(conv_grads), "seq", [(i, (i + shift) % n_seq) for i in range(n_seq)]
-        ).astype(jnp.float32)
-        conv_grads = conv_grads + ((parts[:n_row] + parts[n_row : 2 * n_row]) + parts[2 * n_row :])
-        shift *= 2
-    tap_grads = conv_grads[:taps]
-    bias_grads = conv_grads[taps]
+    conv_sum = (conv_sum[:n_row] + conv_sum[n_row : 2 * n_row]) + conv_sum[2 * n_row :]
+    tap_grads = conv_sum[:taps]
+    bias_grads = conv_sum[taps]
     return (output, grad_tokens, grad_in_weight, grad_out_weight, tap_grads, bias_grads)
 
 

time: 192 us -> 193 us (level)
  waiting for transfers between devices: 86.9 us -> 91.8 us
  matrix products: 5.2 us -> 9.61 us
  starting transfers between devices: 43.4 us -> 39.1 us
    ppermute x3 -> x0, waiting for transfers between devices: 38.8 us -> none  [on_device(): lax.ppermute(split_exact(conv_grads), 'seq', [(i, (i + shift) % n_seq) fo...]
    all_to_all x1, waiting for transfers between devices: 0.01 us -> 27.2 us  [reduce_over_dp(): lax.all_to_all(split, 'chip', 0, 0, tiled=True).astype(jnp.float32)]
    all_to_all x0 -> x1, waiting for transfers between devices: none -> 19.2 us  [on_device(): lax.all_to_all(sent, 'seq', 0, 0, tiled=True).astype(jnp.float32)]
    ppermute x3 -> x0, starting transfers between devices: 11.6 us -> none  [on_device(): lax.ppermute(split_exact(conv_grads), 'seq', [(i, (i + shift) % n_seq) fo...]
    all_to_all x0 -> x1, starting transfers between devices: none -> 7.39 us  [on_device(): lax.all_to_all(sent, 'seq', 0, 0, tiled=True).astype(jnp.float32)]
    ppermute x2, waiting for transfers between devices: 3.38 us -> 0.7 us  [from_behind(): return lax.ppermute(block, axis, route)]
  transfers between devices with their start and end apart: 9 -> 7, of which waited for: 7 -> 5; matrix products, arithmetic and copies ran while one was open for 6% -> 9% of each run, Pallas kernels for 0% -> 0%
where the time goes in v8:
time: 193 us; the launch traced here: 192 us
  waiting for transfers between devices  91.8 us (48%)
  starting transfers between devices  39.1 us (20%)
  blocking collectives  20.5 us (11%)
  between operations  14.3 us (7%)
  matrix products  9.61 us (5%)
  local copies, waits for them, and re-layouts  9.42 us (5%)
  other arithmetic  7.35 us (4%)
    all_to_all x1, waiting for transfers between devices, gather_over(): return lax.all_to_all(rep, axis, 0, dim + 1, tiled=True)[0]  36.1 us
    all_to_all x1, waiting for transfers between devices, reduce_over_dp(): lax.all_to_all(split, 'chip', 0, 0, tiled=True).astype(jnp.float32)  27.2 us
    all_to_all x1, waiting for transfers between devices, on_device(): lax.all_to_all(sent, 'seq', 0, 0, tiled=True).astype(jnp.float32)  19.2 us
    all_to_all x1, starting transfers between devices, gather_over(): return lax.all_to_all(rep, axis, 0, dim + 1, tiled=True)[0]  16.5 us
    all_to_all x1, starting transfers between devices, reduce_over_dp(): lax.all_to_all(split, 'chip', 0, 0, tiled=True).astype(jnp.float32)  11.3 us
    all_to_all x1, blocking collectives, reduce_over_dp(): split = lax.all_to_all(split, 'core', 1, 1, tiled=True).sum(axis=1)  10.6 us
    all_to_all x1, blocking collectives, gather_over(): return lax.all_to_all(rep, axis, 0, dim + 1, tiled=True)[0]  9.93 us
    all_gather x1, waiting for transfers between devices, on_device(): w_full = lax.all_gather(w_local, 'seq', axis=1, tiled=True)  8.53 us
  transfers between devices with their start and end apart: 7, of which 5 were waited for; matrix products, arithmetic and copies ran while one was open for 9% of the time, Pallas kernels for 0%

profile of v8, /device:TPU:1, one launch (start us, length us, event | category | flops | bytes accessed | tf_op | source)
XLA Modules:
  0.0 192.0 jit_solution(7408235674912001398)
XLA Ops:
  7.2 0.0 all-gather.2.cloned.1.call-start
  7.2 1.0 copy.31
  8.2 0.0 copy-start.3
  8.2 0.0 copy-start.2
  8.3 1.7 pad_maximum_fusion.2
  10.0 0.0 all-gather.2.cloned.1.call-update
  10.0 0.7 pad_maximum_fusion.8
  10.8 1.2 broadcast_in_dim.18
  12.0 16.5 %all-to-all-start = ((bf16[32,128,2,64]{1,3,2,0:T(8,128)(2,1)}), bf16[32,128,2,64]{1,3,2,0:T(8,128)(2,1)S(1)}, u32[]{:S(2)}, u32[]{:S(2)}) async-start(bf16[32,128,2,64]{1,3,2,0:T(8,128)(2,1)} %broadcast_in_dim.18), calls=%async_computation | async-start | bytes 2097152 | tf_op jit(solution)/shard_map/all_to_all | solution.py:23
  28.5 0.0 reduce-scatter.2.cloned.1.call-start
  28.6 0.0 copy-done.3
  28.6 0.1 pad.5.clone
  28.7 0.0 copy-done.2
  28.7 36.1 %all-to-all-done = bf16[32,128,2,64]{1,3,2,0:T(8,128)(2,1)S(1)} async-done(((bf16[32,128,2,64]{1,3,2,0:T(8,128)(2,1)}), bf16[32,128,2,64]{1,3,2,0:T(8,128)(2,1)S(1)}, u32[]{:S(2)}, u32[]{:S(2)}) %all-to-all-start) | async-done | bytes 1048608 | tf_op jit(solution)/shard_map/all_to_all | solution.py:23
  64.8 0.1 copy.32
  64.9 0.6 broadcast_in_dim.20
  65.6 9.9 %all_to_all.45 = bf16[2,128,2,32,1,64]{1,5,3,2,4,0:T(8,128)(2,1)S(1)} all-to-all(bf16[2,128,2,32,1,64]{1,5,3,2,4,0:T(8,128)(2,1)S(1)} %broadcast_in_dim.20), channel_id=1, replica_groups=mesh['chip'=32,'core'=2,'seq'=8] {'core'}, dimensions={0} | all-to-all | bytes 4194304 | tf_op jit(solution)/shard_map/all_to_all | solution.py:23
  75.5 0.2 copy.33
  75.7 8.5 %all-gather.2.cloned.1.call-done = bf16[3,4096,128]{2,1,0:T(8,128)(2,1)} async-done(((bf16[3,512,128]{2,1,0:T(8,128)(2,1)}), bf16[3,4096,128]{2,1,0:T(8,128)(2,1)}) %all-gather.2.cloned.1.call-update) | async-done | bytes 3145744 | tf_op jit(solution)/shard_map/all_gather | solution.py:47
  84.2 0.0 copy-start.1
  84.2 2.3 %fusion.3 = bf16[128,2,128]{2,0,1:T(8,128)(2,1)S(1)} fusion(bf16[3,4096,128]{2,1,0:T(8,128)(2,1)} %all-gather.2.cloned.1.call-done, bf16[128,2,4096]{0,2,1:T(8,128)(2,1)S(1)} %bitcast.106), kind=kOutput, calls=%fused_computation.8 | convolution fusion | flops 268468224 | bytes 3211264 | tf_op jit(solution)/shard_map/td,pde->tpe/dot_general | solution.py:57
  86.5 2.3 %collective-permute-start = (bf16[3,128]{1,0:T(4,128)(2,1)S(1)}, bf16[3,128]{1,0:T(4,128)(2,1)S(1)}, u32[]{:S(2)}, u32[]{:S(2)}) collective-permute-start(bf16[3,128]{1,0:T(4,128)(2,1)S(1)} %slice_bitcast_fusion.11), channel_id=1, source_target_pairs={{0,1},{1,2},{2,3},{3,4},{4,5},{5,6},{6,7},{8,9},{9,10},{10,11},{11... | collective-permute-start | bytes 2312 | tf_op jit(solution)/shard_map/ppermute | solution.py:13
  88.9 0.7 collective-permute-done
  89.6 0.0 copy-done.1
  89.6 0.5 fusion.23
  90.1 0.0 slice-start
  90.2 1.4 collective-permute-start.1
  91.6 0.4 convolution_convert_fusion.1
  92.0 0.1 fusion.32
  92.1 0.0 slice-done
  92.1 1.8 convolution_bitcast_fusion
  93.9 0.1 maximum_maximum_fusion
  94.0 1.0 pad_maximum_fusion.1
  95.0 0.0 collective-permute-done.1
  95.1 2.1 %fusion = bf16[2,4096,128]{1,2,0:T(8,128)(2,1)} fusion(bf16[128,2,4096]{0,2,1:T(8,128)(2,1)S(1)} %bitcast.109, bf16[128,1,128]{2,0,1:T(8,128)(2,1)S(1)} %fusion.32, bf16[128,1,128]{2,0,1:T(8,128)(2,1)S(1)} %fusion.33), kind=kOutput, calls=%fused_computation.1 | convolution fusion | flops 269516800 | bytes 3211264 | tf_op jit(solution)/shard_map/td,tpe->pde/dot_general | solution.py:97
  97.2 0.0 reduce-scatter.2.cloned.1.call-update
  97.2 0.0 copy-start
  97.2 2.4 %fusion.26 = f32[4096,128,1]{1,0,2:T(8,128)S(1)} fusion(bf16[3,4096,128]{2,1,0:T(8,128)(2,1)} %all-gather.2.cloned.1.call-done, bf16[128,1,128]{2,0,1:T(8,128)(2,1)S(1)} %fusion.32, bf16[128,1,128]{2,0,1:T(8,128)(2,1)S(1)} %fusion.33), kind=kOutput, calls=%fused_computation.55 | convolution fusion | flops 268566528 | bytes 5308416 | tf_op jit(solution)/shard_map/tpe,pde->dt/dot_general | solution.py:93
  99.6 0.0 copy-done
  99.7 0.6 pad_maximum_fusion
  100.2 0.6 copy.35
  100.8 10.6 %all_to_all.46 = f32[32,2,64,2,128]{4,2,0,3,1:T(8,128)} all-to-all(f32[32,2,64,2,128]{4,2,0,3,1:T(8,128)S(1)} %copy.35), channel_id=1, replica_groups=mesh['chip'=32,'core'=2,'seq'=8] {'core'}, dimensions={1} | all-to-all | bytes 8388608 | tf_op jit(solution)/shard_map/all_to_all | solution.py:36
  111.4 7.4 %all-to-all-start.4 = ((bf16[8,528,128]{2,1,0:T(8,128)(2,1)}), bf16[8,528,128]{2,1,0:T(8,128)(2,1)S(1)}, u32[]{:S(2)}, u32[]{:S(2)}) async-start(bf16[8,528,128]{2,1,0:T(8,128)(2,1)} %pad_maximum_fusion.1), calls=%async_computation.5 | async-start | bytes 2162688 | tf_op jit(solution)/shard_map/all_to_all | solution.py:111
  118.8 2.7 %reduce_sum.72 = bf16[32,64,2,128]{3,1,0,2:T(8,128)(2,1)S(1)} reduce(f32[32,2,64,2,128]{4,2,0,3,1:T(8,128)} %all_to_all.46, f32[]{:T(128)} %constant.1.clone.1), dimensions={1}, to_apply=%region_0.0 | reduce | flops 524288 | bytes 5242884 | tf_op jit(solution)/shard_map/reduce_sum | solution.py:36
  121.6 1.1 copy.37
  122.7 19.2 %all-to-all-done.4 = bf16[8,528,128]{2,1,0:T(8,128)(2,1)S(1)} async-done(((bf16[8,528,128]{2,1,0:T(8,128)(2,1)}), bf16[8,528,128]{2,1,0:T(8,128)(2,1)S(1)}, u32[]{:S(2)}, u32[]{:S(2)}) %all-to-all-start.4) | async-done | bytes 1081376 | tf_op jit(solution)/shard_map/all_to_all | solution.py:111
  141.9 11.3 %all-to-all-start.3 = ((bf16[32,64,2,128]{3,1,2,0:T(8,128)(2,1)}), bf16[32,64,2,128]{3,1,2,0:T(8,128)(2,1)S(1)}, u32[]{:S(2)}, u32[]{:S(2)}) async-start(bf16[32,64,2,128]{3,1,2,0:T(8,128)(2,1)} %copy.37), calls=%async_computation.3 | async-start | bytes 2097152 | tf_op jit(solution)/shard_map/all_to_all | solution.py:38
  153.2 0.2 convert_reduce_fusion
  153.4 0.8 copy.40
  154.2 0.6 slice.120
  154.8 0.5 slice_bitcast_fusion.12
  155.3 27.2 %all-to-all-done.3 = bf16[32,64,2,128]{3,1,2,0:T(8,128)(2,1)S(1)} async-done(((bf16[32,64,2,128]{3,1,2,0:T(8,128)(2,1)}), bf16[32,64,2,128]{3,1,2,0:T(8,128)(2,1)S(1)}, u32[]{:S(2)}, u32[]{:S(2)}) %all-to-all-start.3) | async-done | bytes 1048608 | tf_op jit(solution)/shard_map/all_to_all | solution.py:38
  182.5 0.2 reduce
  182.7 0.6 slice_bitcast_fusion.9
  183.3 0.0 reduce-scatter.2.cloned.1.call-done
  183.3 1.9 copy.39
  (11 shorter events, 0.1 us)
Async XLA Ops:
  7.2 77.0 %all-gather.2.cloned.1.call-start = ((), (), s32[]{:S(2)}) async-start(), calls=%async_computation.6 | async-start | bytes 3538944 | tf_op jit(solution)/shard_map/all_gather | solution.py:47
  8.2 20.4 %copy-start.3 = (bf16[128]{0:T(256)(128)(2,1)S(1)}, bf16[128]{0:T(256)(128)(2,1)}, u32[]{:S(2)}) copy-start(bf16[128]{0:T(256)(128)(2,1)} %param.9) | copy-start | bytes 772
  8.2 20.4 %copy-start.2 = (bf16[4,128]{1,0:T(4,128)(2,1)S(1)}, bf16[4,128]{1,0:T(4,128)(2,1)}, u32[]{:S(2)}) copy-start(bf16[4,128]{1,0:T(4,128)(2,1)} %param.8) | copy-start | bytes 3076
  12.0 52.8 %all-to-all-start = ((bf16[32,128,2,64]{1,3,2,0:T(8,128)(2,1)}), bf16[32,128,2,64]{1,3,2,0:T(8,128)(2,1)S(1)}, u32[]{:S(2)}, u32[]{:S(2)}) async-start(bf16[32,128,2,64]{1,3,2,0:T(8,128)(2,1)} %broadcast_in_dim.18), calls=%async_computation | async-start | bytes 2097152 | tf_op jit(solution)/shard_map/all_to_all | solution.py:23
  28.5 154.8 %reduce-scatter.2.cloned.1.call-start = ((), (), s32[]{:S(2)}) async-start(), calls=%async_computation.7 | async-start | bytes 2359296 | tf_op jit(solution)/shard_map/reduce_scatter | solution.py:99
  84.2 5.4 %copy-start.1 = (bf16[3,4096,128]{2,1,0:T(8,128)(2,1)S(1)}, bf16[3,4096,128]{2,1,0:T(8,128)(2,1)}, u32[]{:S(2)}) copy-start(bf16[3,4096,128]{2,1,0:T(8,128)(2,1)} %all-gather.2.cloned.1.call-done) | copy-start | bytes 9437188
  86.5 3.0 %collective-permute-start = (bf16[3,128]{1,0:T(4,128)(2,1)S(1)}, bf16[3,128]{1,0:T(4,128)(2,1)S(1)}, u32[]{:S(2)}, u32[]{:S(2)}) collective-permute-start(bf16[3,128]{1,0:T(4,128)(2,1)S(1)} %slice_bitcast_fusion.11), channel_id=1, source_target_pairs={{0,1},{1,2},{2,3},{3,4},{4,5},{5,6},{6,7},{8,9},{9,10},{10,11},{11... | collective-permute-start | bytes 2312 | tf_op jit(solution)/shard_map/ppermute | solution.py:13
  90.1 2.0 %slice-start = ((bf16[3,4096,128]{2,1,0:T(8,128)(2,1)}), bf16[1,4096,128]{2,1,0:T(8,128)(2,1)S(1)}, s32[]{:S(2)}) async-start(bf16[3,4096,128]{2,1,0:T(8,128)(2,1)} %all-gather.2.cloned.1.call-done), calls=%async_computation.8 | async-start | bytes 2097152 | tf_op jit(solution)/shard_map/slice | solution.py:49
  90.2 4.9 %collective-permute-start.1 = (bf16[3,128]{1,0:T(4,128)(2,1)S(1)}, bf16[3,128]{1,0:T(4,128)(2,1)S(1)}, u32[]{:S(2)}, u32[]{:S(2)}) collective-permute-start(bf16[3,128]{1,0:T(4,128)(2,1)S(1)} %slice.133), channel_id=1, source_target_pairs={{1,0},{2,1},{3,2},{4,3},{5,4},{6,5},{7,6},{9,8},{10,9},{11,10},{12... | collective-permute-start | bytes 2312 | tf_op jit(solution)/shard_map/ppermute | solution.py:13
  97.2 2.5 %copy-start = (f32[32,2,64,1,128]{4,2,1,0,3:T(8,128)S(1)}, f32[32,2,64,1,128]{4,2,1,0,3:T(8,128)}, u32[]{:S(2)}) copy-start(f32[32,2,64,1,128]{4,2,1,0,3:T(8,128)} %convolution_bitcast_fusion) | copy-start | bytes 6291460
  111.4 30.4 %all-to-all-start.4 = ((bf16[8,528,128]{2,1,0:T(8,128)(2,1)}), bf16[8,528,128]{2,1,0:T(8,128)(2,1)S(1)}, u32[]{:S(2)}, u32[]{:S(2)}) async-start(bf16[8,528,128]{2,1,0:T(8,128)(2,1)} %pad_maximum_fusion.1), calls=%async_computation.5 | async-start | bytes 2162688 | tf_op jit(solution)/shard_map/all_to_all | solution.py:111
  141.9 40.7 %all-to-all-start.3 = ((bf16[32,64,2,128]{3,1,2,0:T(8,128)(2,1)}), bf16[32,64,2,128]{3,1,2,0:T(8,128)(2,1)S(1)}, u32[]{:S(2)}, u32[]{:S(2)}) async-start(bf16[32,64,2,128]{3,1,2,0:T(8,128)(2,1)} %copy.37), calls=%async_computation.3 | async-start | bytes 2097152 | tf_op jit(solution)/shard_map/all_to_all | solution.py:38
Sparse Core Ops, SparseCore 0:
  10.7 73.4 all-gather.1
  97.3 57.2 reduce-scatter.1

commit v9 on v8

--- a/solution.py
+++ b/solution.py
@@ -94,23 +94,27 @@
     reduced = reduce_over_dp(jnp.stack([out_part, tok_part], axis=1), n_chip, n_core)
     output = reduced[:, 0].T.astype(jnp.bfloat16)
     grad_tokens = reduced[:, 1].T.astype(jnp.bfloat16)
-    term_in = jnp.einsum("td,tpe->pde", whole, branch_grads, preferred_element_type=jnp.float32)
+    term_in = jnp.einsum("td,tpe->dpe", whole, branch_grads, preferred_element_type=jnp.float32)
     term_out_t = jnp.einsum("td,te->de", upstream, hidden, preferred_element_type=jnp.float32)
-    grad_in_weight = lax.psum_scatter(
-        term_in.astype(jnp.bfloat16), "seq", scatter_dimension=1, tiled=True
-    ).astype(jnp.float32)
     d_full, e_loc = term_out_t.shape
     d_loc = d_full // n_seq
-    sent = term_out_t.astype(jnp.bfloat16).reshape(n_seq, d_loc, e_loc)
+    half = e_loc // 2
+    on_sc = jnp.concatenate(
+        [term_in.reshape(d_full, 2 * e_loc), term_out_t[:, :half]], axis=1
+    ).astype(jnp.bfloat16)
+    on_sc = lax.psum_scatter(on_sc, "seq", scatter_dimension=0, tiled=True).astype(jnp.float32)
+    grad_in_weight = on_sc[:, : 2 * e_loc].reshape(d_loc, 2, e_loc).transpose(1, 0, 2)
+    sent = term_out_t[:, half:].astype(jnp.bfloat16).reshape(n_seq, d_loc, e_loc - half)
     conv_parts = split_exact(conv_grads)
     n_conv = conv_parts.shape[0]
     pad_rows = (-n_conv) % 8
     conv_parts = jnp.concatenate([conv_parts, jnp.zeros((pad_rows, e_loc), jnp.bfloat16)], axis=0)
+    conv_parts = conv_parts.reshape(-1, e_loc - half)
     conv_parts = jnp.broadcast_to(conv_parts[None], (n_seq,) + conv_parts.shape)
     sent = jnp.concatenate([sent, conv_parts], axis=1)
     summed = lax.all_to_all(sent, "seq", 0, 0, tiled=True).astype(jnp.float32).sum(axis=0)
-    grad_out_weight = summed[:d_loc].T
-    conv_sum = summed[d_loc : d_loc + n_conv]
+    grad_out_weight = jnp.concatenate([on_sc[:, 2 * e_loc :], summed[:d_loc]], axis=1).T
+    conv_sum = summed[d_loc:].reshape(-1, e_loc)[:n_conv]
     n_row = taps + 1
     conv_sum = (conv_sum[:n_row] + conv_sum[n_row : 2 * n_row]) + conv_sum[2 * n_row :]
     tap_grads = conv_sum[:taps]

time: 193 us -> 193 us (level)
  matrix products: 9.61 us -> 5.19 us
  other arithmetic: 7.35 us -> 9.69 us
    all_to_all x1, waiting for transfers between devices: 19.2 us -> 15.1 us  [on_device(): lax.all_to_all(sent, 'seq', 0, 0, tiled=True).astype(jnp.float32)]
    all_to_all x1, waiting for transfers between devices: 27.2 us -> 30.1 us  [reduce_over_dp(): lax.all_to_all(split, 'chip', 0, 0, tiled=True).astype(jnp.float32)]
    ppermute x2, waiting for transfers between devices: 0.7 us -> 3.31 us  [from_behind(): return lax.ppermute(block, axis, route)]
    slice x0 -> x6, local copies, waits for them, and re-layouts: none -> 2.07 us  [the longest x1 1 us: on_device(): on_sc[:, :2 * e_loc].reshape(d_loc, 2, e_loc).transpose(1, 0, 2)]
  transfers between devices with their start and end apart: 7 -> 7, of which waited for: 5 -> 6; matrix products, arithmetic and copies ran while one was open for 9% -> 7% of each run, Pallas kernels for 0% -> 0%
where the time goes in v9:
time: 193 us
  waiting for transfers between devices  93.3 us (48%)
  starting transfers between devices  38.3 us (20%)
  blocking collectives  20.7 us (11%)
  between operations  14.3 us (7%)
  local copies, waits for them, and re-layouts  11.1 us (6%)
  other arithmetic  9.69 us (5%)
  matrix products  5.19 us (3%)
    all_to_all x1, waiting for transfers between devices, gather_over(): return lax.all_to_all(rep, axis, 0, dim + 1, tiled=True)[0]  36.2 us
    all_to_all x1, waiting for transfers between devices, reduce_over_dp(): lax.all_to_all(split, 'chip', 0, 0, tiled=True).astype(jnp.float32)  30.1 us
    all_to_all x1, starting transfers between devices, gather_over(): return lax.all_to_all(rep, axis, 0, dim + 1, tiled=True)[0]  16.5 us
    all_to_all x1, waiting for transfers between devices, on_device(): lax.all_to_all(sent, 'seq', 0, 0, tiled=True).astype(jnp.float32)  15.1 us
    all_to_all x1, starting transfers between devices, reduce_over_dp(): lax.all_to_all(split, 'chip', 0, 0, tiled=True).astype(jnp.float32)  11 us
    all_to_all x1, blocking collectives, reduce_over_dp(): split = lax.all_to_all(split, 'core', 1, 1, tiled=True).sum(axis=1)  10.8 us
    all_to_all x1, blocking collectives, gather_over(): return lax.all_to_all(rep, axis, 0, dim + 1, tiled=True)[0]  9.92 us
    all_gather x1, waiting for transfers between devices, on_device(): w_full = lax.all_gather(w_local, 'seq', axis=1, tiled=True)  8.53 us
  transfers between devices with their start and end apart: 7, of which 6 were waited for; matrix products, arithmetic and copies ran while one was open for 7% of the time, Pallas kernels for 0%

profile of v9, /device:TPU:1, one launch (start us, length us, event | category | flops | bytes accessed | tf_op | source)
XLA Modules:
  0.0 192.6 jit_solution(2770524274170671723)
XLA Ops:
  7.2 0.0 all-gather.2.cloned.1.call-start
  7.2 1.0 copy.36
  8.2 0.0 copy-start.3
  8.2 0.0 copy-start.2
  8.3 1.7 pad_maximum_fusion.3
  10.0 0.0 all-gather.2.cloned.1.call-update
  10.0 0.7 pad_maximum_fusion.8
  10.8 1.2 broadcast_in_dim.20
  12.0 16.5 %all-to-all-start = ((bf16[32,128,2,64]{1,3,2,0:T(8,128)(2,1)}), bf16[32,128,2,64]{1,3,2,0:T(8,128)(2,1)S(1)}, u32[]{:S(2)}, u32[]{:S(2)}) async-start(bf16[32,128,2,64]{1,3,2,0:T(8,128)(2,1)} %broadcast_in_dim.20), calls=%async_computation | async-start | bytes 2097152 | tf_op jit(solution)/shard_map/all_to_all | solution.py:23
  28.5 0.0 reduce-scatter.2.cloned.1.call-start
  28.6 0.0 copy-done.3
  28.6 0.0 copy-done.2
  28.6 36.2 %all-to-all-done = bf16[32,128,2,64]{1,3,2,0:T(8,128)(2,1)S(1)} async-done(((bf16[32,128,2,64]{1,3,2,0:T(8,128)(2,1)}), bf16[32,128,2,64]{1,3,2,0:T(8,128)(2,1)S(1)}, u32[]{:S(2)}, u32[]{:S(2)}) %all-to-all-start) | async-done | bytes 1048608 | tf_op jit(solution)/shard_map/all_to_all | solution.py:23
  64.8 0.1 copy.37
  64.9 0.6 broadcast_in_dim.22
  65.6 9.9 %all_to_all.45 = bf16[2,128,2,32,1,64]{1,5,3,2,4,0:T(8,128)(2,1)S(1)} all-to-all(bf16[2,128,2,32,1,64]{1,5,3,2,4,0:T(8,128)(2,1)S(1)} %broadcast_in_dim.22), channel_id=1, replica_groups=mesh['chip'=32,'core'=2,'seq'=8] {'core'}, dimensions={0} | all-to-all | bytes 4194304 | tf_op jit(solution)/shard_map/all_to_all | solution.py:23
  75.5 0.2 copy.38
  75.6 8.5 %all-gather.2.cloned.1.call-done = bf16[3,4096,128]{2,1,0:T(8,128)(2,1)} async-done(((bf16[3,512,128]{2,1,0:T(8,128)(2,1)}), bf16[3,4096,128]{2,1,0:T(8,128)(2,1)}) %all-gather.2.cloned.1.call-update) | async-done | bytes 3145744 | tf_op jit(solution)/shard_map/all_gather | solution.py:47
  84.2 2.3 %fusion.2 = bf16[128,2,128]{2,0,1:T(8,128)(2,1)S(1)} fusion(bf16[3,4096,128]{2,1,0:T(8,128)(2,1)} %all-gather.2.cloned.1.call-done, bf16[128,2,4096]{0,2,1:T(8,128)(2,1)S(1)} %bitcast.113), kind=kOutput, calls=%fused_computation.8 | convolution fusion | flops 268468224 | bytes 3211264 | tf_op jit(solution)/shard_map/td,pde->tpe/dot_general | solution.py:57
  86.5 2.3 %collective-permute-start = (bf16[3,128]{1,0:T(4,128)(2,1)S(1)}, bf16[3,128]{1,0:T(4,128)(2,1)S(1)}, u32[]{:S(2)}, u32[]{:S(2)}) collective-permute-start(bf16[3,128]{1,0:T(4,128)(2,1)S(1)} %slice_bitcast_fusion.7), channel_id=1, source_target_pairs={{0,1},{1,2},{2,3},{3,4},{4,5},{5,6},{6,7},{8,9},{9,10},{10,11},{11... | collective-permute-start | bytes 2312 | tf_op jit(solution)/shard_map/ppermute | solution.py:13
  88.9 0.7 collective-permute-done
  89.5 0.0 copy-done
  89.6 0.5 fusion.26
  90.1 1.3 collective-permute-start.1
  91.4 0.5 convolution_convert_fusion.1
  91.9 0.1 fusion.42
  92.0 0.1 fusion.36
  92.0 2.6 %collective-permute-done.1 = bf16[3,128]{1,0:T(4,128)(2,1)S(1)} collective-permute-done((bf16[3,128]{1,0:T(4,128)(2,1)S(1)}, bf16[3,128]{1,0:T(4,128)(2,1)S(1)}, u32[]{:S(2)}, u32[]{:S(2)}) %collective-permute-start.1) | collective-permute-done | bytes 800 | tf_op jit(solution)/shard_map/ppermute | solution.py:13
  94.7 0.1 copy.43
  94.8 0.7 convolution_convert_fusion
  95.6 1.7 pad_maximum_fusion.1
  97.3 0.0 reduce-scatter.2.cloned.1.call-update
  97.3 0.1 pad.7.clone
  97.4 0.1 maximum_maximum_fusion
  97.5 0.1 broadcast_in_dim.50
  97.5 0.1 copy.45
  97.7 0.0 copy-start.1
  97.7 0.9 pad_maximum_fusion.2
  98.7 0.0 slice-done
  98.7 0.5 convolution_bitcast_fusion
  99.1 0.8 copy-done.1
  99.9 0.7 fusion.30
  100.6 0.6 pad_maximum_fusion
  101.2 0.6 copy.40
  101.8 10.8 %all_to_all.46 = f32[32,2,64,2,128]{4,2,0,3,1:T(8,128)} all-to-all(f32[32,2,64,2,128]{4,2,0,3,1:T(8,128)S(1)} %copy.40), channel_id=1, replica_groups=mesh['chip'=32,'core'=2,'seq'=8] {'core'}, dimensions={1} | all-to-all | bytes 8388608 | tf_op jit(solution)/shard_map/all_to_all | solution.py:36
  112.6 7.1 %all-to-all-start.4 = ((bf16[8,544,64]{1,2,0:T(8,128)(2,1)}), bf16[8,544,64]{1,2,0:T(8,128)(2,1)S(1)}, u32[]{:S(2)}, u32[]{:S(2)}) async-start(bf16[8,544,64]{1,2,0:T(8,128)(2,1)} %pad_maximum_fusion.2), calls=%async_computation.5 | async-start | bytes 1310720 | tf_op jit(solution)/shard_map/all_to_all | solution.py:115
  119.7 2.7 %reduce_sum.72 = bf16[32,64,2,128]{3,1,0,2:T(8,128)(2,1)S(1)} reduce(f32[32,2,64,2,128]{4,2,0,3,1:T(8,128)} %all_to_all.46, f32[]{:T(128)} %constant.1.clone.1), dimensions={1}, to_apply=%region_0.0 | reduce | flops 524288 | bytes 5242884 | tf_op jit(solution)/shard_map/reduce_sum | solution.py:36
  122.5 1.1 copy.42
  123.6 15.1 %all-to-all-done.4 = bf16[8,544,64]{1,2,0:T(8,128)(2,1)S(1)} async-done(((bf16[8,544,64]{1,2,0:T(8,128)(2,1)}), bf16[8,544,64]{1,2,0:T(8,128)(2,1)S(1)}, u32[]{:S(2)}, u32[]{:S(2)}) %all-to-all-start.4) | async-done | bytes 557088 | tf_op jit(solution)/shard_map/all_to_all | solution.py:115
  138.6 11.0 %all-to-all-start.3 = ((bf16[32,64,2,128]{3,1,2,0:T(8,128)(2,1)}), bf16[32,64,2,128]{3,1,2,0:T(8,128)(2,1)S(1)}, u32[]{:S(2)}, u32[]{:S(2)}) async-start(bf16[32,64,2,128]{3,1,2,0:T(8,128)(2,1)} %copy.42), calls=%async_computation.3 | async-start | bytes 2097152 | tf_op jit(solution)/shard_map/all_to_all | solution.py:38
  149.6 0.1 convert_reduce_fusion
  149.7 0.1 slice_add_fusion
  149.8 0.1 slice.178
  149.9 0.1 copy.47
  149.9 0.7 slice.149
  150.6 0.1 copy.48
  150.7 0.6 squeeze.14
  151.3 30.1 %all-to-all-done.3 = bf16[32,64,2,128]{3,1,2,0:T(8,128)(2,1)S(1)} async-done(((bf16[32,64,2,128]{3,1,2,0:T(8,128)(2,1)}), bf16[32,64,2,128]{3,1,2,0:T(8,128)(2,1)S(1)}, u32[]{:S(2)}, u32[]{:S(2)}) %all-to-all-start.3) | async-done | bytes 1048608 | tf_op jit(solution)/shard_map/all_to_all | solution.py:38
  181.4 0.2 reduce
  181.6 0.6 slice_bitcast_fusion.5
  182.2 1.0 slice.170
  183.2 1.0 copy.44
  184.2 0.8 slice.171
  185.1 0.7 maximum_bitcast_fusion
  (15 shorter events, 0.2 us)
Async XLA Ops:
  7.2 77.0 %all-gather.2.cloned.1.call-start = ((), (), s32[]{:S(2)}) async-start(), calls=%async_computation.6 | async-start | bytes 3538944 | tf_op jit(solution)/shard_map/all_gather | solution.py:47
  8.2 20.3 %copy-start.3 = (bf16[128]{0:T(256)(128)(2,1)S(1)}, bf16[128]{0:T(256)(128)(2,1)}, u32[]{:S(2)}) copy-start(bf16[128]{0:T(256)(128)(2,1)} %param.9) | copy-start | bytes 772
  8.2 20.4 %copy-start.2 = (bf16[4,128]{1,0:T(4,128)(2,1)S(1)}, bf16[4,128]{1,0:T(4,128)(2,1)}, u32[]{:S(2)}) copy-start(bf16[4,128]{1,0:T(4,128)(2,1)} %param.8) | copy-start | bytes 3076
  12.0 52.8 %all-to-all-start = ((bf16[32,128,2,64]{1,3,2,0:T(8,128)(2,1)}), bf16[32,128,2,64]{1,3,2,0:T(8,128)(2,1)S(1)}, u32[]{:S(2)}, u32[]{:S(2)}) async-start(bf16[32,128,2,64]{1,3,2,0:T(8,128)(2,1)} %broadcast_in_dim.20), calls=%async_computation | async-start | bytes 2097152 | tf_op jit(solution)/shard_map/all_to_all | solution.py:23
  28.5 153.7 %reduce-scatter.2.cloned.1.call-start = ((), (), s32[]{:S(2)}) async-start(), calls=%async_computation.7 | async-start | bytes 2949120 | tf_op jit(solution)/shard_map/reduce_scatter | solution.py:105
  84.2 5.4 %copy-start = (bf16[3,4096,128]{2,1,0:T(8,128)(2,1)S(1)}, bf16[3,4096,128]{2,1,0:T(8,128)(2,1)}, u32[]{:S(2)}) copy-start(bf16[3,4096,128]{2,1,0:T(8,128)(2,1)} %all-gather.2.cloned.1.call-done) | copy-start | bytes 9437188
  86.5 3.0 %collective-permute-start = (bf16[3,128]{1,0:T(4,128)(2,1)S(1)}, bf16[3,128]{1,0:T(4,128)(2,1)S(1)}, u32[]{:S(2)}, u32[]{:S(2)}) collective-permute-start(bf16[3,128]{1,0:T(4,128)(2,1)S(1)} %slice_bitcast_fusion.7), channel_id=1, source_target_pairs={{0,1},{1,2},{2,3},{3,4},{4,5},{5,6},{6,7},{8,9},{9,10},{10,11},{11... | collective-permute-start | bytes 2312 | tf_op jit(solution)/shard_map/ppermute | solution.py:13
  90.1 4.6 %collective-permute-start.1 = (bf16[3,128]{1,0:T(4,128)(2,1)S(1)}, bf16[3,128]{1,0:T(4,128)(2,1)S(1)}, u32[]{:S(2)}, u32[]{:S(2)}) collective-permute-start(bf16[3,128]{1,0:T(4,128)(2,1)S(1)} %slice.162), channel_id=1, source_target_pairs={{1,0},{2,1},{3,2},{4,3},{5,4},{6,5},{7,6},{9,8},{10,9},{11,10},{12... | collective-permute-start | bytes 2312 | tf_op jit(solution)/shard_map/ppermute | solution.py:13
  97.4 1.3 slice-start
  97.7 2.2 %copy-start.1 = (bf16[3,4096,128]{2,1,0:T(8,128)(2,1)S(1)}, bf16[3,4096,128]{2,1,0:T(8,128)(2,1)}, u32[]{:S(2)}) copy-start(bf16[3,4096,128]{2,1,0:T(8,128)(2,1)} %all-gather.2.cloned.1.call-done) | copy-start | bytes 9437188
  112.6 26.0 %all-to-all-start.4 = ((bf16[8,544,64]{1,2,0:T(8,128)(2,1)}), bf16[8,544,64]{1,2,0:T(8,128)(2,1)S(1)}, u32[]{:S(2)}, u32[]{:S(2)}) async-start(bf16[8,544,64]{1,2,0:T(8,128)(2,1)} %pad_maximum_fusion.2), calls=%async_computation.5 | async-start | bytes 1310720 | tf_op jit(solution)/shard_map/all_to_all | solution.py:115
  138.6 42.8 %all-to-all-start.3 = ((bf16[32,64,2,128]{3,1,2,0:T(8,128)(2,1)}), bf16[32,64,2,128]{3,1,2,0:T(8,128)(2,1)S(1)}, u32[]{:S(2)}, u32[]{:S(2)}) async-start(bf16[32,64,2,128]{3,1,2,0:T(8,128)(2,1)} %copy.42), calls=%async_computation.3 | async-start | bytes 2097152 | tf_op jit(solution)/shard_map/all_to_all | solution.py:38
Sparse Core Ops, SparseCore 0:
  10.7 73.4 all-gather.1
  97.4 64.3 reduce-scatter.1

commit v10 on v9

--- a/solution.py
+++ b/solution.py
@@ -32,8 +32,9 @@
 
 
 def reduce_over_dp(part, n_chip, n_core):
-    split = part.reshape((n_chip, n_core, part.shape[0] // (n_chip * n_core)) + part.shape[1:])
-    split = lax.all_to_all(split, "core", 1, 1, tiled=True).sum(axis=1)
+    split = part.astype(jnp.bfloat16)
+    split = split.reshape((n_chip, n_core, part.shape[0] // (n_chip * n_core)) + part.shape[1:])
+    split = lax.all_to_all(split, "core", 1, 1, tiled=True).astype(jnp.float32).sum(axis=1)
     split = split.astype(jnp.bfloat16)
     return lax.all_to_all(split, "chip", 0, 0, tiled=True).astype(jnp.float32).sum(axis=0)
 

time: 193 us -> 194 us (level)
  waiting for transfers between devices: 93.3 us -> 98.3 us
  blocking collectives: 20.7 us -> 18 us
    all_to_all x1, waiting for transfers between devices: 30.1 us -> 35 us  [reduce_over_dp(): lax.all_to_all(split, 'chip', 0, 0, tiled=True).astype(jnp.float32)]
    all_to_all x1, blocking collectives: 10.8 us -> 8.04 us  [reduce_over_dp(): lax.all_to_all(split, 'core', 1, 1, tiled=True).astype(jnp.float32)]
    reduce_sum x1, other arithmetic: 2.75 us -> 0.64 us  [reduce_over_dp(): lax.all_to_all(split, 'core', 1, 1, tiled=True).astype(jnp.float32)]
  transfers between devices with their start and end apart: 7 -> 7, of which waited for: 6 -> 6; matrix products, arithmetic and copies ran while one was open for 7% -> 6% of each run, Pallas kernels for 0% -> 0%
where the time goes in v10:
time: 194 us
  waiting for transfers between devices  98.3 us (51%)
  starting transfers between devices  38.9 us (20%)
  blocking collectives  18 us (9%)
  between operations  14.3 us (7%)
  local copies, waits for them, and re-layouts  10.7 us (6%)
  other arithmetic  8.31 us (4%)
  matrix products  5.21 us (3%)
    all_to_all x1, waiting for transfers between devices, gather_over(): return lax.all_to_all(rep, axis, 0, dim + 1, tiled=True)[0]  36.2 us
    all_to_all x1, waiting for transfers between devices, reduce_over_dp(): lax.all_to_all(split, 'chip', 0, 0, tiled=True).astype(jnp.float32)  35 us
    all_to_all x1, starting transfers between devices, gather_over(): return lax.all_to_all(rep, axis, 0, dim + 1, tiled=True)[0]  16.5 us
    all_to_all x1, waiting for transfers between devices, on_device(): lax.all_to_all(sent, 'seq', 0, 0, tiled=True).astype(jnp.float32)  15.2 us
    all_to_all x1, starting transfers between devices, reduce_over_dp(): lax.all_to_all(split, 'chip', 0, 0, tiled=True).astype(jnp.float32)  11.6 us
    all_to_all x1, blocking collectives, gather_over(): return lax.all_to_all(rep, axis, 0, dim + 1, tiled=True)[0]  9.92 us
    all_gather x1, waiting for transfers between devices, on_device(): w_full = lax.all_gather(w_local, 'seq', axis=1, tiled=True)  8.53 us
    all_to_all x1, blocking collectives, reduce_over_dp(): lax.all_to_all(split, 'core', 1, 1, tiled=True).astype(jnp.float32)  8.04 us
  transfers between devices with their start and end apart: 7, of which 6 were waited for; matrix products, arithmetic and copies ran while one was open for 6% of the time, Pallas kernels for 0%

profile of v10, /device:TPU:1, one launch (start us, length us, event | category | flops | bytes accessed | tf_op | source)
XLA Modules:
  0.0 193.6 jit_solution(13069759689500225289)
XLA Ops:
  7.2 0.0 all-gather.2.cloned.1.call-start
  7.2 1.0 copy.36
  8.2 0.0 copy-start.3
  8.2 0.0 copy-start.2
  8.3 1.7 pad_maximum_fusion.3
  10.0 0.0 all-gather.2.cloned.1.call-update
  10.0 0.7 pad_maximum_fusion.8
  10.8 1.2 broadcast_in_dim.20
  12.0 16.5 %all-to-all-start = ((bf16[32,128,2,64]{1,3,2,0:T(8,128)(2,1)}), bf16[32,128,2,64]{1,3,2,0:T(8,128)(2,1)S(1)}, u32[]{:S(2)}, u32[]{:S(2)}) async-start(bf16[32,128,2,64]{1,3,2,0:T(8,128)(2,1)} %broadcast_in_dim.20), calls=%async_computation | async-start | bytes 2097152 | tf_op jit(solution)/shard_map/all_to_all | solution.py:23
  28.5 0.0 reduce-scatter.2.cloned.1.call-start
  28.6 0.0 copy-done.3
  28.6 0.0 copy-done.2
  28.6 36.2 %all-to-all-done = bf16[32,128,2,64]{1,3,2,0:T(8,128)(2,1)S(1)} async-done(((bf16[32,128,2,64]{1,3,2,0:T(8,128)(2,1)}), bf16[32,128,2,64]{1,3,2,0:T(8,128)(2,1)S(1)}, u32[]{:S(2)}, u32[]{:S(2)}) %all-to-all-start) | async-done | bytes 1048608 | tf_op jit(solution)/shard_map/all_to_all | solution.py:23
  64.8 0.1 copy.37
  64.9 0.6 broadcast_in_dim.22
  65.6 9.9 %all_to_all.45 = bf16[2,128,2,32,1,64]{1,5,3,2,4,0:T(8,128)(2,1)S(1)} all-to-all(bf16[2,128,2,32,1,64]{1,5,3,2,4,0:T(8,128)(2,1)S(1)} %broadcast_in_dim.22), channel_id=1, replica_groups=mesh['chip'=32,'core'=2,'seq'=8] {'core'}, dimensions={0} | all-to-all | bytes 4194304 | tf_op jit(solution)/shard_map/all_to_all | solution.py:23
  75.5 0.2 copy.38
  75.6 8.5 %all-gather.2.cloned.1.call-done = bf16[3,4096,128]{2,1,0:T(8,128)(2,1)} async-done(((bf16[3,512,128]{2,1,0:T(8,128)(2,1)}), bf16[3,4096,128]{2,1,0:T(8,128)(2,1)}) %all-gather.2.cloned.1.call-update) | async-done | bytes 3145744 | tf_op jit(solution)/shard_map/all_gather | solution.py:48
  84.2 2.3 %fusion.4 = bf16[128,2,128]{2,0,1:T(8,128)(2,1)S(1)} fusion(bf16[3,4096,128]{2,1,0:T(8,128)(2,1)} %all-gather.2.cloned.1.call-done, bf16[128,2,4096]{0,2,1:T(8,128)(2,1)S(1)} %bitcast.115), kind=kOutput, calls=%fused_computation.11 | convolution fusion | flops 268468224 | bytes 3211264 | tf_op jit(solution)/shard_map/td,pde->tpe/dot_general | solution.py:58
  86.5 2.3 %collective-permute-start = (bf16[3,128]{1,0:T(4,128)(2,1)S(1)}, bf16[3,128]{1,0:T(4,128)(2,1)S(1)}, u32[]{:S(2)}, u32[]{:S(2)}) collective-permute-start(bf16[3,128]{1,0:T(4,128)(2,1)S(1)} %slice_bitcast_fusion.7), channel_id=1, source_target_pairs={{0,1},{1,2},{2,3},{3,4},{4,5},{5,6},{6,7},{8,9},{9,10},{10,11},{11... | collective-permute-start | bytes 2312 | tf_op jit(solution)/shard_map/ppermute | solution.py:13
  88.9 0.7 collective-permute-done
  89.5 0.0 copy-done
  89.6 0.5 fusion.28
  90.1 1.3 collective-permute-start.1
  91.4 0.5 convolution_convert_fusion.1
  91.9 0.1 fusion.43
  92.0 0.1 fusion.37
  92.0 2.6 %collective-permute-done.1 = bf16[3,128]{1,0:T(4,128)(2,1)S(1)} collective-permute-done((bf16[3,128]{1,0:T(4,128)(2,1)S(1)}, bf16[3,128]{1,0:T(4,128)(2,1)S(1)}, u32[]{:S(2)}, u32[]{:S(2)}) %collective-permute-start.1) | collective-permute-done | bytes 800 | tf_op jit(solution)/shard_map/ppermute | solution.py:13
  94.7 0.1 copy.43
  94.8 0.7 convolution_convert_fusion
  95.6 1.7 pad_maximum_fusion
  97.3 0.0 reduce-scatter.2.cloned.1.call-update
  97.3 0.1 pad.7.clone
  97.4 0.0 slice-start
  97.4 0.1 maximum_maximum_fusion
  97.5 0.1 broadcast_in_dim.50
  97.6 0.1 copy.45
  97.7 0.9 pad_maximum_fusion.2
  98.7 0.0 slice-done
  98.7 0.5 fusion.3
  99.1 0.8 copy-done.1
  99.9 0.7 fusion
  100.6 0.2 pad_maximum_fusion.1
  100.8 0.2 copy.40
  101.0 8.0 %all_to_all.46 = bf16[32,2,64,2,128]{4,2,0,3,1:T(8,128)(2,1)S(1)} all-to-all(bf16[32,2,64,2,128]{4,2,0,3,1:T(8,128)(2,1)S(1)} %copy.40), channel_id=1, replica_groups=mesh['chip'=32,'core'=2,'seq'=8] {'core'}, dimensions={1} | all-to-all | bytes 4194304 | tf_op jit(solution)/shard_map/all_to_all | solution.py:37
  109.1 7.1 %all-to-all-start.4 = ((bf16[8,544,64]{1,2,0:T(8,128)(2,1)}), bf16[8,544,64]{1,2,0:T(8,128)(2,1)}, u32[]{:S(2)}, u32[]{:S(2)}) async-start(bf16[8,544,64]{1,2,0:T(8,128)(2,1)} %pad_maximum_fusion.2), calls=%async_computation.5 | async-start | bytes 1310720 | tf_op jit(solution)/shard_map/all_to_all | solution.py:116
  116.2 0.6 reduce_sum.75
  116.8 1.1 copy.42
  117.9 15.2 %all-to-all-done.4 = bf16[8,544,64]{1,2,0:T(8,128)(2,1)} async-done(((bf16[8,544,64]{1,2,0:T(8,128)(2,1)}), bf16[8,544,64]{1,2,0:T(8,128)(2,1)}, u32[]{:S(2)}, u32[]{:S(2)}) %all-to-all-start.4) | async-done | bytes 557088 | tf_op jit(solution)/shard_map/all_to_all | solution.py:116
  133.1 11.6 %all-to-all-start.3 = ((bf16[32,64,2,128]{3,1,2,0:T(8,128)(2,1)}), bf16[32,64,2,128]{3,1,2,0:T(8,128)(2,1)S(1)}, u32[]{:S(2)}, u32[]{:S(2)}) async-start(bf16[32,64,2,128]{3,1,2,0:T(8,128)(2,1)} %copy.42), calls=%async_computation.3 | async-start | bytes 2097152 | tf_op jit(solution)/shard_map/all_to_all | solution.py:39
  144.7 1.2 convert_reduce_fusion
  145.9 0.1 slice_add_fusion
  146.0 0.1 slice.178
  146.1 0.1 copy.47
  146.1 0.7 slice.149
  146.8 0.1 copy.48
  146.9 0.6 squeeze.14
  147.5 35.0 %all-to-all-done.3 = bf16[32,64,2,128]{3,1,2,0:T(8,128)(2,1)S(1)} async-done(((bf16[32,64,2,128]{3,1,2,0:T(8,128)(2,1)}), bf16[32,64,2,128]{3,1,2,0:T(8,128)(2,1)S(1)}, u32[]{:S(2)}, u32[]{:S(2)}) %all-to-all-start.3) | async-done | bytes 1048608 | tf_op jit(solution)/shard_map/all_to_all | solution.py:39
  182.4 0.2 reduce.1
  182.6 0.6 slice_bitcast_fusion.5
  183.2 1.0 slice.170
  184.2 1.0 copy.44
  185.2 0.8 slice.171
  186.1 0.7 maximum_bitcast_fusion
  (15 shorter events, 0.2 us)
Async XLA Ops:
  7.2 77.0 %all-gather.2.cloned.1.call-start = ((), (), s32[]{:S(2)}) async-start(), calls=%async_computation.6 | async-start | bytes 3538944 | tf_op jit(solution)/shard_map/all_gather | solution.py:48
  8.2 20.3 %copy-start.3 = (bf16[128]{0:T(256)(128)(2,1)S(1)}, bf16[128]{0:T(256)(128)(2,1)}, u32[]{:S(2)}) copy-start(bf16[128]{0:T(256)(128)(2,1)} %param.9) | copy-start | bytes 772
  8.2 20.4 %copy-start.2 = (bf16[4,128]{1,0:T(4,128)(2,1)S(1)}, bf16[4,128]{1,0:T(4,128)(2,1)}, u32[]{:S(2)}) copy-start(bf16[4,128]{1,0:T(4,128)(2,1)} %param.8) | copy-start | bytes 3076
  12.0 52.8 %all-to-all-start = ((bf16[32,128,2,64]{1,3,2,0:T(8,128)(2,1)}), bf16[32,128,2,64]{1,3,2,0:T(8,128)(2,1)S(1)}, u32[]{:S(2)}, u32[]{:S(2)}) async-start(bf16[32,128,2,64]{1,3,2,0:T(8,128)(2,1)} %broadcast_in_dim.20), calls=%async_computation | async-start | bytes 2097152 | tf_op jit(solution)/shard_map/all_to_all | solution.py:23
  28.5 154.7 %reduce-scatter.2.cloned.1.call-start = ((), (), s32[]{:S(2)}) async-start(), calls=%async_computation.7 | async-start | bytes 2949120 | tf_op jit(solution)/shard_map/reduce_scatter | solution.py:106
  84.2 5.4 %copy-start = (bf16[3,4096,128]{2,1,0:T(8,128)(2,1)S(1)}, bf16[3,4096,128]{2,1,0:T(8,128)(2,1)}, u32[]{:S(2)}) copy-start(bf16[3,4096,128]{2,1,0:T(8,128)(2,1)} %all-gather.2.cloned.1.call-done) | copy-start | bytes 9437188
  86.5 3.0 %collective-permute-start = (bf16[3,128]{1,0:T(4,128)(2,1)S(1)}, bf16[3,128]{1,0:T(4,128)(2,1)S(1)}, u32[]{:S(2)}, u32[]{:S(2)}) collective-permute-start(bf16[3,128]{1,0:T(4,128)(2,1)S(1)} %slice_bitcast_fusion.7), channel_id=1, source_target_pairs={{0,1},{1,2},{2,3},{3,4},{4,5},{5,6},{6,7},{8,9},{9,10},{10,11},{11... | collective-permute-start | bytes 2312 | tf_op jit(solution)/shard_map/ppermute | solution.py:13
  90.1 4.6 %collective-permute-start.1 = (bf16[3,128]{1,0:T(4,128)(2,1)S(1)}, bf16[3,128]{1,0:T(4,128)(2,1)S(1)}, u32[]{:S(2)}, u32[]{:S(2)}) collective-permute-start(bf16[3,128]{1,0:T(4,128)(2,1)S(1)} %slice.162), channel_id=1, source_target_pairs={{1,0},{2,1},{3,2},{4,3},{5,4},{6,5},{7,6},{9,8},{10,9},{11,10},{12... | collective-permute-start | bytes 2312 | tf_op jit(solution)/shard_map/ppermute | solution.py:13
  97.4 1.3 slice-start
  97.7 2.2 %copy-start.1 = (bf16[3,4096,128]{2,1,0:T(8,128)(2,1)S(1)}, bf16[3,4096,128]{2,1,0:T(8,128)(2,1)}, u32[]{:S(2)}) copy-start(bf16[3,4096,128]{2,1,0:T(8,128)(2,1)} %all-gather.2.cloned.1.call-done) | copy-start | bytes 9437188
  109.1 24.1 %all-to-all-start.4 = ((bf16[8,544,64]{1,2,0:T(8,128)(2,1)}), bf16[8,544,64]{1,2,0:T(8,128)(2,1)}, u32[]{:S(2)}, u32[]{:S(2)}) async-start(bf16[8,544,64]{1,2,0:T(8,128)(2,1)} %pad_maximum_fusion.2), calls=%async_computation.5 | async-start | bytes 1310720 | tf_op jit(solution)/shard_map/all_to_all | solution.py:116
  133.1 49.3 %all-to-all-start.3 = ((bf16[32,64,2,128]{3,1,2,0:T(8,128)(2,1)}), bf16[32,64,2,128]{3,1,2,0:T(8,128)(2,1)S(1)}, u32[]{:S(2)}, u32[]{:S(2)}) async-start(bf16[32,64,2,128]{3,1,2,0:T(8,128)(2,1)} %copy.42), calls=%async_computation.3 | async-start | bytes 2097152 | tf_op jit(solution)/shard_map/all_to_all | solution.py:39
Sparse Core Ops, SparseCore 0:
  10.7 73.4 all-gather.1
  97.4 72.9 reduce-scatter.1

commit v11 on v7

--- a/solution.py
+++ b/solution.py
@@ -100,14 +100,11 @@
     terms = lax.psum_scatter(terms, "seq", scatter_dimension=1, tiled=True).astype(jnp.float32)
     grad_in_weight = terms[:2]
     grad_out_weight = terms[2].T
+    conv_parts = split_exact(conv_grads)
+    conv_parts = jnp.broadcast_to(conv_parts[None], (n_seq,) + conv_parts.shape)
+    parts = lax.all_to_all(conv_parts, "seq", 0, 0, tiled=True).astype(jnp.float32).sum(axis=0)
     n_row = taps + 1
-    shift = 1
-    while shift < n_seq:
-        parts = lax.ppermute(
-            split_exact(conv_grads), "seq", [(i, (i + shift) % n_seq) for i in range(n_seq)]
-        ).astype(jnp.float32)
-        conv_grads = conv_grads + ((parts[:n_row] + parts[n_row : 2 * n_row]) + parts[2 * n_row :])
-        shift *= 2
+    conv_grads = (parts[:n_row] + parts[n_row : 2 * n_row]) + parts[2 * n_row :]
     tap_grads = conv_grads[:taps]
     bias_grads = conv_grads[taps]
     return (output, grad_tokens, grad_in_weight, grad_out_weight, tap_grads, bias_grads)

time: 192 us -> 187 us (0.974)
  starting transfers between devices: 43.4 us -> 38.2 us
    ppermute x3 -> x0, waiting for transfers between devices: 38.8 us -> none  [on_device(): lax.ppermute(split_exact(conv_grads), 'seq', [(i, (i + shift) % n_seq) fo...]
    all_to_all x1, waiting for transfers between devices: 0.01 us -> 38.1 us  [reduce_over_dp(): lax.all_to_all(split, 'chip', 0, 0, tiled=True).astype(jnp.float32)]
    ppermute x3 -> x0, starting transfers between devices: 11.6 us -> none  [on_device(): lax.ppermute(split_exact(conv_grads), 'seq', [(i, (i + shift) % n_seq) fo...]
    all_to_all x0 -> x1, starting transfers between devices: none -> 7.13 us  [on_device(): lax.all_to_all(conv_parts, 'seq', 0, 0, tiled=True).astype(jnp.float32)]
  transfers between devices with their start and end apart: 9 -> 7, of which waited for: 7 -> 6; matrix products, arithmetic and copies ran while one was open for 6% -> 7% of each run, Pallas kernels for 0% -> 0%
where the time goes in v11:
time: 187 us; the launch traced here: 186 us
  waiting for transfers between devices  87.9 us (47%)
  starting transfers between devices  38.2 us (20%)
  blocking collectives  20.7 us (11%)
  between operations  14.3 us (8%)
  local copies, waits for them, and re-layouts  11.7 us (6%)
  other arithmetic  8.16 us (4%)
  matrix products  5.2 us (3%)
    all_to_all x1, waiting for transfers between devices, reduce_over_dp(): lax.all_to_all(split, 'chip', 0, 0, tiled=True).astype(jnp.float32)  38.1 us
    all_to_all x1, waiting for transfers between devices, gather_over(): return lax.all_to_all(rep, axis, 0, dim + 1, tiled=True)[0]  36.2 us
    all_to_all x1, starting transfers between devices, gather_over(): return lax.all_to_all(rep, axis, 0, dim + 1, tiled=True)[0]  16.5 us
    all_to_all x1, starting transfers between devices, reduce_over_dp(): lax.all_to_all(split, 'chip', 0, 0, tiled=True).astype(jnp.float32)  10.9 us
    all_to_all x1, blocking collectives, reduce_over_dp(): split = lax.all_to_all(split, 'core', 1, 1, tiled=True).sum(axis=1)  10.8 us
    all_to_all x1, blocking collectives, gather_over(): return lax.all_to_all(rep, axis, 0, dim + 1, tiled=True)[0]  9.93 us
    all_gather x1, waiting for transfers between devices, on_device(): w_full = lax.all_gather(w_local, 'seq', axis=1, tiled=True)  8.53 us
    all_to_all x1, starting transfers between devices, on_device(): lax.all_to_all(conv_parts, 'seq', 0, 0, tiled=True).astype(jnp.float32)  7.13 us
  transfers between devices with their start and end apart: 7, of which 6 were waited for; matrix products, arithmetic and copies ran while one was open for 7% of the time, Pallas kernels for 0%

profile of v11, /device:TPU:1, one launch (start us, length us, event | category | flops | bytes accessed | tf_op | source)
XLA Modules:
  0.0 186.2 jit_solution(6282750361972225226)
XLA Ops:
  7.2 0.0 all-gather.2.cloned.1.call-start
  7.2 1.0 copy.62
  8.2 0.0 copy-start.4
  8.2 0.0 copy-start.3
  8.3 1.7 pad_maximum_fusion.2
  10.0 0.0 all-gather.2.cloned.1.call-update
  10.0 0.7 pad_maximum_fusion.8
  10.8 1.2 broadcast_in_dim.19
  12.0 16.5 %all-to-all-start = ((bf16[32,128,2,64]{1,3,2,0:T(8,128)(2,1)}), bf16[32,128,2,64]{1,3,2,0:T(8,128)(2,1)S(1)}, u32[]{:S(2)}, u32[]{:S(2)}) async-start(bf16[32,128,2,64]{1,3,2,0:T(8,128)(2,1)} %broadcast_in_dim.19), calls=%async_computation | async-start | bytes 2097152 | tf_op jit(solution)/shard_map/all_to_all | solution.py:23
  28.5 0.0 reduce-scatter.2.cloned.1.call-start
  28.6 0.0 copy-done.4
  28.6 0.0 copy-done.3
  28.6 36.2 %all-to-all-done = bf16[32,128,2,64]{1,3,2,0:T(8,128)(2,1)S(1)} async-done(((bf16[32,128,2,64]{1,3,2,0:T(8,128)(2,1)}), bf16[32,128,2,64]{1,3,2,0:T(8,128)(2,1)S(1)}, u32[]{:S(2)}, u32[]{:S(2)}) %all-to-all-start) | async-done | bytes 1048608 | tf_op jit(solution)/shard_map/all_to_all | solution.py:23
  64.8 0.1 copy.63
  64.9 0.6 broadcast_in_dim.21
  65.5 9.9 %all_to_all.45 = bf16[2,128,2,32,1,64]{1,5,3,2,4,0:T(8,128)(2,1)S(1)} all-to-all(bf16[2,128,2,32,1,64]{1,5,3,2,4,0:T(8,128)(2,1)S(1)} %broadcast_in_dim.21), channel_id=1, replica_groups=mesh['chip'=32,'core'=2,'seq'=8] {'core'}, dimensions={0} | all-to-all | bytes 4194304 | tf_op jit(solution)/shard_map/all_to_all | solution.py:23
  75.5 0.2 copy.64
  75.6 8.5 %all-gather.2.cloned.1.call-done = bf16[3,4096,128]{2,1,0:T(8,128)(2,1)} async-done(((bf16[3,512,128]{2,1,0:T(8,128)(2,1)}), bf16[3,4096,128]{2,1,0:T(8,128)(2,1)}) %all-gather.2.cloned.1.call-update) | async-done | bytes 3145744 | tf_op jit(solution)/shard_map/all_gather | solution.py:47
  84.2 0.0 copy-start
  84.2 2.3 %fusion.4 = bf16[128,2,128]{2,0,1:T(8,128)(2,1)S(1)} fusion(bf16[3,4096,128]{2,1,0:T(8,128)(2,1)} %all-gather.2.cloned.1.call-done, bf16[128,2,4096]{0,2,1:T(8,128)(2,1)S(1)} %bitcast.108), kind=kOutput, calls=%fused_computation.9 | convolution fusion | flops 268468224 | bytes 3211264 | tf_op jit(solution)/shard_map/td,pde->tpe/dot_general | solution.py:57
  86.5 2.3 %collective-permute-start = (bf16[3,128]{1,0:T(4,128)(2,1)S(1)}, bf16[3,128]{1,0:T(4,128)(2,1)S(1)}, u32[]{:S(2)}, u32[]{:S(2)}) collective-permute-start(bf16[3,128]{1,0:T(4,128)(2,1)S(1)} %slice_bitcast_fusion.11), channel_id=1, source_target_pairs={{0,1},{1,2},{2,3},{3,4},{4,5},{5,6},{6,7},{8,9},{9,10},{10,11},{11... | collective-permute-start | bytes 2312 | tf_op jit(solution)/shard_map/ppermute | solution.py:13
  88.9 0.7 collective-permute-done
  89.5 0.0 copy-done
  89.6 0.5 fusion.24
  90.1 1.3 collective-permute-start.1
  91.4 0.1 fusion.33
  91.5 0.5 fusion.1
  92.0 2.7 %collective-permute-done.1 = bf16[3,128]{1,0:T(4,128)(2,1)S(1)} collective-permute-done((bf16[3,128]{1,0:T(4,128)(2,1)S(1)}, bf16[3,128]{1,0:T(4,128)(2,1)S(1)}, u32[]{:S(2)}, u32[]{:S(2)}) %collective-permute-start.1) | collective-permute-done | bytes 800 | tf_op jit(solution)/shard_map/ppermute | solution.py:13
  94.7 0.7 fusion
  95.4 2.0 %pad_maximum_fusion.1 = bf16[3,4096,128]{1,2,0:T(8,128)(2,1)} fusion(bf16[1,4096,128]{1,2,0:T(8,128)(2,1)S(1)} %fusion.1, bf16[2,4096,128]{1,2,0:T(8,128)(2,1)S(1)} %fusion), kind=kLoop, calls=%fused_computation.5 | loop fusion | flops 1572864 | bytes 6291456 | tf_op jit(solution)/shard_map/concatenate | solution.py:99
  97.4 0.0 slice-start
  97.4 0.0 reduce-scatter.2.cloned.1.call-update
  97.4 0.0 copy-start.1
  97.5 1.1 slice-done
  98.6 0.5 convolution_bitcast_fusion
  99.1 0.5 copy-done.1
  99.6 0.7 fusion.27
  100.3 0.6 pad_maximum_fusion
  100.9 0.6 copy.66
  101.5 10.8 %all_to_all.46 = f32[32,2,64,2,128]{4,2,0,3,1:T(8,128)} all-to-all(f32[32,2,64,2,128]{4,2,0,3,1:T(8,128)S(1)} %copy.66), channel_id=1, replica_groups=mesh['chip'=32,'core'=2,'seq'=8] {'core'}, dimensions={1} | all-to-all | bytes 8388608 | tf_op jit(solution)/shard_map/all_to_all | solution.py:36
  112.3 0.6 broadcast_in_dim.24
  112.9 7.1 %all-to-all-start.4 = ((bf16[8,15,128]{2,1,0:T(8,128)(2,1)}), bf16[8,15,128]{2,1,0:T(8,128)(2,1)S(1)}, u32[]{:S(2)}, u32[]{:S(2)}) async-start(bf16[8,15,128]{2,1,0:T(8,128)(2,1)} %broadcast_in_dim.24), calls=%async_computation.5 | async-start | bytes 65536 | tf_op jit(solution)/shard_map/all_to_all | solution.py:105
  120.0 2.7 %reduce_sum.72 = bf16[32,64,2,128]{3,1,0,2:T(8,128)(2,1)S(1)} reduce(f32[32,2,64,2,128]{4,2,0,3,1:T(8,128)} %all_to_all.46, f32[]{:T(128)} %constant.1.clone.1), dimensions={1}, to_apply=%region_0.0 | reduce | flops 524288 | bytes 5242884 | tf_op jit(solution)/shard_map/reduce_sum | solution.py:36
  122.8 1.1 copy.68
  123.9 1.7 all-to-all-done.4
  125.5 10.9 %all-to-all-start.3 = ((bf16[32,64,2,128]{3,1,2,0:T(8,128)(2,1)}), bf16[32,64,2,128]{3,1,2,0:T(8,128)(2,1)S(1)}, u32[]{:S(2)}, u32[]{:S(2)}) async-start(bf16[32,64,2,128]{3,1,2,0:T(8,128)(2,1)} %copy.68), calls=%async_computation.3 | async-start | bytes 2097152 | tf_op jit(solution)/shard_map/all_to_all | solution.py:38
  136.5 0.6 slice.120
  137.0 0.5 slice_bitcast_fusion.12
  137.6 38.1 %all-to-all-done.3 = bf16[32,64,2,128]{3,1,2,0:T(8,128)(2,1)S(1)} async-done(((bf16[32,64,2,128]{3,1,2,0:T(8,128)(2,1)}), bf16[32,64,2,128]{3,1,2,0:T(8,128)(2,1)S(1)}, u32[]{:S(2)}, u32[]{:S(2)}) %all-to-all-start.3) | async-done | bytes 1048608 | tf_op jit(solution)/shard_map/all_to_all | solution.py:38
  175.7 0.2 reduce
  175.8 0.6 slice_bitcast_fusion.9
  176.5 0.0 reduce-scatter.2.cloned.1.call-done
  176.5 0.0 copy-start.2
  176.5 1.1 slice.140
  177.5 1.0 copy.72
  178.5 0.0 copy-done.2
  178.5 0.1 convert_element_type.129
  178.6 0.7 slice_bitcast_fusion.6
  (11 shorter events, 0.1 us)
Async XLA Ops:
  7.2 77.0 %all-gather.2.cloned.1.call-start = ((), (), s32[]{:S(2)}) async-start(), calls=%async_computation.6 | async-start | bytes 3538944 | tf_op jit(solution)/shard_map/all_gather | solution.py:47
  8.2 20.3 %copy-start.4 = (bf16[128]{0:T(256)(128)(2,1)S(1)}, bf16[128]{0:T(256)(128)(2,1)}, u32[]{:S(2)}) copy-start(bf16[128]{0:T(256)(128)(2,1)} %param.9) | copy-start | bytes 772
  8.2 20.4 %copy-start.3 = (bf16[4,128]{1,0:T(4,128)(2,1)S(1)}, bf16[4,128]{1,0:T(4,128)(2,1)}, u32[]{:S(2)}) copy-start(bf16[4,128]{1,0:T(4,128)(2,1)} %param.8) | copy-start | bytes 3076
  12.0 52.8 %all-to-all-start = ((bf16[32,128,2,64]{1,3,2,0:T(8,128)(2,1)}), bf16[32,128,2,64]{1,3,2,0:T(8,128)(2,1)S(1)}, u32[]{:S(2)}, u32[]{:S(2)}) async-start(bf16[32,128,2,64]{1,3,2,0:T(8,128)(2,1)} %broadcast_in_dim.19), calls=%async_computation | async-start | bytes 2097152 | tf_op jit(solution)/shard_map/all_to_all | solution.py:23
  28.5 147.9 %reduce-scatter.2.cloned.1.call-start = ((), (), s32[]{:S(2)}) async-start(), calls=%async_computation.7 | async-start | bytes 3538944 | tf_op jit(solution)/shard_map/reduce_scatter | solution.py:100
  84.2 5.4 %copy-start = (bf16[3,4096,128]{2,1,0:T(8,128)(2,1)S(1)}, bf16[3,4096,128]{2,1,0:T(8,128)(2,1)}, u32[]{:S(2)}) copy-start(bf16[3,4096,128]{2,1,0:T(8,128)(2,1)} %all-gather.2.cloned.1.call-done) | copy-start | bytes 9437188
  86.5 3.0 %collective-permute-start = (bf16[3,128]{1,0:T(4,128)(2,1)S(1)}, bf16[3,128]{1,0:T(4,128)(2,1)S(1)}, u32[]{:S(2)}, u32[]{:S(2)}) collective-permute-start(bf16[3,128]{1,0:T(4,128)(2,1)S(1)} %slice_bitcast_fusion.11), channel_id=1, source_target_pairs={{0,1},{1,2},{2,3},{3,4},{4,5},{5,6},{6,7},{8,9},{9,10},{10,11},{11... | collective-permute-start | bytes 2312 | tf_op jit(solution)/shard_map/ppermute | solution.py:13
  90.1 4.6 %collective-permute-start.1 = (bf16[3,128]{1,0:T(4,128)(2,1)S(1)}, bf16[3,128]{1,0:T(4,128)(2,1)S(1)}, u32[]{:S(2)}, u32[]{:S(2)}) collective-permute-start(bf16[3,128]{1,0:T(4,128)(2,1)S(1)} %slice.133), channel_id=1, source_target_pairs={{1,0},{2,1},{3,2},{4,3},{5,4},{6,5},{7,6},{9,8},{10,9},{11,10},{12... | collective-permute-start | bytes 2312 | tf_op jit(solution)/shard_map/ppermute | solution.py:13
  97.4 1.2 slice-start
  97.4 2.2 %copy-start.1 = (bf16[3,4096,128]{2,1,0:T(8,128)(2,1)S(1)}, bf16[3,4096,128]{2,1,0:T(8,128)(2,1)}, u32[]{:S(2)}) copy-start(bf16[3,4096,128]{2,1,0:T(8,128)(2,1)} %all-gather.2.cloned.1.call-done) | copy-start | bytes 9437188
  112.9 12.6 %all-to-all-start.4 = ((bf16[8,15,128]{2,1,0:T(8,128)(2,1)}), bf16[8,15,128]{2,1,0:T(8,128)(2,1)S(1)}, u32[]{:S(2)}, u32[]{:S(2)}) async-start(bf16[8,15,128]{2,1,0:T(8,128)(2,1)} %broadcast_in_dim.24), calls=%async_computation.5 | async-start | bytes 65536 | tf_op jit(solution)/shard_map/all_to_all | solution.py:105
  125.5 50.2 %all-to-all-start.3 = ((bf16[32,64,2,128]{3,1,2,0:T(8,128)(2,1)}), bf16[32,64,2,128]{3,1,2,0:T(8,128)(2,1)S(1)}, u32[]{:S(2)}, u32[]{:S(2)}) async-start(bf16[32,64,2,128]{3,1,2,0:T(8,128)(2,1)} %copy.68), calls=%async_computation.3 | async-start | bytes 2097152 | tf_op jit(solution)/shard_map/all_to_all | solution.py:38
  176.5 2.1 %copy-start.2 = (bf16[3,512,128]{1,2,0:T(8,128)(2,1)S(1)}, bf16[3,512,128]{1,2,0:T(8,128)(2,1)}, u32[]{:S(2)}) copy-start(bf16[3,512,128]{1,2,0:T(8,128)(2,1)} %reduce-scatter.2.cloned.1.call-done) | copy-start | bytes 1179652
Sparse Core Ops, SparseCore 0:
  10.7 73.4 all-gather.1
  97.5 74.6 reduce-scatter.1

commit v12 on v11

--- a/solution.py
+++ b/solution.py
@@ -32,8 +32,9 @@
 
 
 def reduce_over_dp(part, n_chip, n_core):
-    split = part.reshape((n_chip, n_core, part.shape[0] // (n_chip * n_core)) + part.shape[1:])
-    split = lax.all_to_all(split, "core", 1, 1, tiled=True).sum(axis=1)
+    split = part.astype(jnp.bfloat16)
+    split = split.reshape((n_chip, n_core, part.shape[0] // (n_chip * n_core)) + part.shape[1:])
+    split = lax.all_to_all(split, "core", 1, 1, tiled=True).astype(jnp.float32).sum(axis=1)
     split = split.astype(jnp.bfloat16)
     return lax.all_to_all(split, "chip", 0, 0, tiled=True).astype(jnp.float32).sum(axis=0)
 

time: 187 us -> 185 us (0.989)
  blocking collectives: 20.7 us -> 18 us
  other arithmetic: 8.16 us -> 5.69 us
  waiting for transfers between devices: 87.9 us -> 90 us
    all_to_all x1, blocking collectives: 10.8 us -> 8.03 us  [reduce_over_dp(): lax.all_to_all(split, 'core', 1, 1, tiled=True).astype(jnp.float32)]
    reduce_sum x1, other arithmetic: 2.75 us -> 0.64 us  [reduce_over_dp(): lax.all_to_all(split, 'core', 1, 1, tiled=True).astype(jnp.float32)]
    all_to_all x1, waiting for transfers between devices: 1.65 us -> 3.61 us  [on_device(): lax.all_to_all(conv_parts, 'seq', 0, 0, tiled=True).astype(jnp.float32)]
  transfers between devices with their start and end apart: 7 -> 7, of which waited for: 6 -> 6; matrix products, arithmetic and copies ran while one was open for 7% -> 6% of each run, Pallas kernels for 0% -> 0%
where the time goes in v12:
time: 185 us; the launch traced here: 184 us
  waiting for transfers between devices  90 us (49%)
  starting transfers between devices  38.1 us (21%)
  blocking collectives  18 us (10%)
  between operations  14.3 us (8%)
  local copies, waits for them, and re-layouts  10.8 us (6%)
  matrix products  6.81 us (4%)
  other arithmetic  5.69 us (3%)
    all_to_all x1, waiting for transfers between devices, reduce_over_dp(): lax.all_to_all(split, 'chip', 0, 0, tiled=True).astype(jnp.float32)  38.2 us
    all_to_all x1, waiting for transfers between devices, gather_over(): return lax.all_to_all(rep, axis, 0, dim + 1, tiled=True)[0]  36.2 us
    all_to_all x1, starting transfers between devices, gather_over(): return lax.all_to_all(rep, axis, 0, dim + 1, tiled=True)[0]  16.5 us
    all_to_all x1, starting transfers between devices, reduce_over_dp(): lax.all_to_all(split, 'chip', 0, 0, tiled=True).astype(jnp.float32)  10.8 us
    all_to_all x1, blocking collectives, gather_over(): return lax.all_to_all(rep, axis, 0, dim + 1, tiled=True)[0]  9.93 us
    all_gather x1, waiting for transfers between devices, on_device(): w_full = lax.all_gather(w_local, 'seq', axis=1, tiled=True)  8.53 us
    all_to_all x1, blocking collectives, reduce_over_dp(): lax.all_to_all(split, 'core', 1, 1, tiled=True).astype(jnp.float32)  8.03 us
    all_to_all x1, starting transfers between devices, on_device(): lax.all_to_all(conv_parts, 'seq', 0, 0, tiled=True).astype(jnp.float32)  7.12 us
  transfers between devices with their start and end apart: 7, of which 6 were waited for; matrix products, arithmetic and copies ran while one was open for 6% of the time, Pallas kernels for 0%

profile of v12, /device:TPU:1, one launch (start us, length us, event | category | flops | bytes accessed | tf_op | source)
XLA Modules:
  0.0 183.6 jit_solution(6815564811677252783)
XLA Ops:
  7.2 0.0 all-gather.2.cloned.1.call-start
  7.2 1.0 copy.62
  8.2 0.0 copy-start.3
  8.2 0.0 copy-start.2
  8.3 1.7 pad_maximum_fusion.2
  10.0 0.0 all-gather.2.cloned.1.call-update
  10.0 0.7 pad_maximum_fusion.8
  10.8 1.2 broadcast_in_dim.19
  12.0 16.5 %all-to-all-start = ((bf16[32,128,2,64]{1,3,2,0:T(8,128)(2,1)}), bf16[32,128,2,64]{1,3,2,0:T(8,128)(2,1)S(1)}, u32[]{:S(2)}, u32[]{:S(2)}) async-start(bf16[32,128,2,64]{1,3,2,0:T(8,128)(2,1)} %broadcast_in_dim.19), calls=%async_computation | async-start | bytes 2097152 | tf_op jit(solution)/shard_map/all_to_all | solution.py:23
  28.5 0.0 reduce-scatter.2.cloned.1.call-start
  28.6 0.0 copy-done.3
  28.6 0.0 copy-done.2
  28.6 36.2 %all-to-all-done = bf16[32,128,2,64]{1,3,2,0:T(8,128)(2,1)S(1)} async-done(((bf16[32,128,2,64]{1,3,2,0:T(8,128)(2,1)}), bf16[32,128,2,64]{1,3,2,0:T(8,128)(2,1)S(1)}, u32[]{:S(2)}, u32[]{:S(2)}) %all-to-all-start) | async-done | bytes 1048608 | tf_op jit(solution)/shard_map/all_to_all | solution.py:23
  64.8 0.1 copy.63
  64.9 0.6 broadcast_in_dim.21
  65.5 9.9 %all_to_all.45 = bf16[2,128,2,32,1,64]{1,5,3,2,4,0:T(8,128)(2,1)S(1)} all-to-all(bf16[2,128,2,32,1,64]{1,5,3,2,4,0:T(8,128)(2,1)S(1)} %broadcast_in_dim.21), channel_id=1, replica_groups=mesh['chip'=32,'core'=2,'seq'=8] {'core'}, dimensions={0} | all-to-all | bytes 4194304 | tf_op jit(solution)/shard_map/all_to_all | solution.py:23
  75.5 0.2 copy.64
  75.6 8.5 %all-gather.2.cloned.1.call-done = bf16[3,4096,128]{2,1,0:T(8,128)(2,1)} async-done(((bf16[3,512,128]{2,1,0:T(8,128)(2,1)}), bf16[3,4096,128]{2,1,0:T(8,128)(2,1)}) %all-gather.2.cloned.1.call-update) | async-done | bytes 3145744 | tf_op jit(solution)/shard_map/all_gather | solution.py:48
  84.2 0.0 copy-start
  84.2 2.3 %fusion.6 = bf16[128,2,128]{2,0,1:T(8,128)(2,1)S(1)} fusion(bf16[3,4096,128]{2,1,0:T(8,128)(2,1)} %all-gather.2.cloned.1.call-done, bf16[128,2,4096]{0,2,1:T(8,128)(2,1)S(1)} %bitcast.110), kind=kOutput, calls=%fused_computation.12 | convolution fusion | flops 268468224 | bytes 3211264 | tf_op jit(solution)/shard_map/td,pde->tpe/dot_general | solution.py:58
  86.5 2.3 %collective-permute-start = (bf16[3,128]{1,0:T(4,128)(2,1)S(1)}, bf16[3,128]{1,0:T(4,128)(2,1)S(1)}, u32[]{:S(2)}, u32[]{:S(2)}) collective-permute-start(bf16[3,128]{1,0:T(4,128)(2,1)S(1)} %slice_bitcast_fusion.11), channel_id=1, source_target_pairs={{0,1},{1,2},{2,3},{3,4},{4,5},{5,6},{6,7},{8,9},{9,10},{10,11},{11... | collective-permute-start | bytes 2312 | tf_op jit(solution)/shard_map/ppermute | solution.py:13
  88.9 0.7 collective-permute-done
  89.5 0.0 copy-done
  89.6 0.5 fusion.26
  90.1 1.3 collective-permute-start.1
  91.4 0.1 fusion.34
  91.5 0.5 fusion.2
  92.0 2.7 %collective-permute-done.1 = bf16[3,128]{1,0:T(4,128)(2,1)S(1)} collective-permute-done((bf16[3,128]{1,0:T(4,128)(2,1)S(1)}, bf16[3,128]{1,0:T(4,128)(2,1)S(1)}, u32[]{:S(2)}, u32[]{:S(2)}) %collective-permute-start.1) | collective-permute-done | bytes 800 | tf_op jit(solution)/shard_map/ppermute | solution.py:13
  94.7 0.7 fusion
  95.4 2.0 %pad_maximum_fusion = bf16[3,4096,128]{1,2,0:T(8,128)(2,1)} fusion(bf16[1,4096,128]{1,2,0:T(8,128)(2,1)S(1)} %fusion.2, bf16[2,4096,128]{1,2,0:T(8,128)(2,1)S(1)} %fusion), kind=kLoop, calls=%fused_computation.6 | loop fusion | flops 1572864 | bytes 6291456 | tf_op jit(solution)/shard_map/concatenate | solution.py:100
  97.4 0.0 slice-start
  97.4 0.0 reduce-scatter.2.cloned.1.call-update
  97.5 1.1 slice-done
  98.6 0.4 fusion.5
  99.1 2.3 %fusion.1 = bf16[4096,128]{1,0:T(8,128)(2,1)S(1)} fusion(bf16[3,4096,128]{2,1,0:T(8,128)(2,1)} %all-gather.2.cloned.1.call-done, bf16[128,1,128]{2,0,1:T(8,128)(2,1)S(1)} %fusion.34, bf16[128,1,128]{2,0,1:T(8,128)(2,1)S(1)} %fusion.35), kind=kOutput, calls=%fused_computation.3 | convolution fusion | flops 269090816 | bytes 4259840 | tf_op jit(solution)/shard_map/tpe,pde->dt/dot_general | solution.py:94
  101.4 0.2 pad_maximum_fusion.1
  101.6 0.2 copy.66
  101.8 8.0 %all_to_all.46 = bf16[32,2,64,2,128]{4,2,0,3,1:T(8,128)(2,1)S(1)} all-to-all(bf16[32,2,64,2,128]{4,2,0,3,1:T(8,128)(2,1)S(1)} %copy.66), channel_id=1, replica_groups=mesh['chip'=32,'core'=2,'seq'=8] {'core'}, dimensions={1} | all-to-all | bytes 4194304 | tf_op jit(solution)/shard_map/all_to_all | solution.py:37
  109.8 0.6 broadcast_in_dim.24
  110.5 7.1 %all-to-all-start.4 = ((bf16[8,15,128]{2,1,0:T(8,128)(2,1)}), bf16[8,15,128]{2,1,0:T(8,128)(2,1)S(1)}, u32[]{:S(2)}, u32[]{:S(2)}) async-start(bf16[8,15,128]{2,1,0:T(8,128)(2,1)} %broadcast_in_dim.24), calls=%async_computation.5 | async-start | bytes 65536 | tf_op jit(solution)/shard_map/all_to_all | solution.py:106
  117.6 0.6 reduce_sum.75
  118.2 1.1 copy.68
  119.3 3.6 %all-to-all-done.4 = bf16[8,15,128]{2,1,0:T(8,128)(2,1)S(1)} async-done(((bf16[8,15,128]{2,1,0:T(8,128)(2,1)}), bf16[8,15,128]{2,1,0:T(8,128)(2,1)S(1)}, u32[]{:S(2)}, u32[]{:S(2)}) %all-to-all-start.4) | async-done | bytes 30752 | tf_op jit(solution)/shard_map/all_to_all | solution.py:106
  122.9 10.8 %all-to-all-start.3 = ((bf16[32,64,2,128]{3,1,2,0:T(8,128)(2,1)}), bf16[32,64,2,128]{3,1,2,0:T(8,128)(2,1)S(1)}, u32[]{:S(2)}, u32[]{:S(2)}) async-start(bf16[32,64,2,128]{3,1,2,0:T(8,128)(2,1)} %copy.68), calls=%async_computation.3 | async-start | bytes 2097152 | tf_op jit(solution)/shard_map/all_to_all | solution.py:39
  133.8 0.6 slice.120
  134.4 0.5 slice_bitcast_fusion.12
  134.9 38.2 %all-to-all-done.3 = bf16[32,64,2,128]{3,1,2,0:T(8,128)(2,1)S(1)} async-done(((bf16[32,64,2,128]{3,1,2,0:T(8,128)(2,1)}), bf16[32,64,2,128]{3,1,2,0:T(8,128)(2,1)S(1)}, u32[]{:S(2)}, u32[]{:S(2)}) %all-to-all-start.3) | async-done | bytes 1048608 | tf_op jit(solution)/shard_map/all_to_all | solution.py:39
  173.1 0.2 reduce.1
  173.3 0.6 slice_bitcast_fusion.9
  173.9 0.0 reduce-scatter.2.cloned.1.call-done
  173.9 0.0 copy-start.1
  173.9 1.1 slice.140
  175.0 1.0 copy.72
  176.0 0.0 copy-done.1
  176.0 0.1 convert_element_type.129
  176.1 0.7 slice_bitcast_fusion.6
  (11 shorter events, 0.1 us)
Async XLA Ops:
  7.2 77.0 %all-gather.2.cloned.1.call-start = ((), (), s32[]{:S(2)}) async-start(), calls=%async_computation.6 | async-start | bytes 3538944 | tf_op jit(solution)/shard_map/all_gather | solution.py:48
  8.2 20.3 %copy-start.3 = (bf16[128]{0:T(256)(128)(2,1)S(1)}, bf16[128]{0:T(256)(128)(2,1)}, u32[]{:S(2)}) copy-start(bf16[128]{0:T(256)(128)(2,1)} %param.9) | copy-start | bytes 772
  8.2 20.4 %copy-start.2 = (bf16[4,128]{1,0:T(4,128)(2,1)S(1)}, bf16[4,128]{1,0:T(4,128)(2,1)}, u32[]{:S(2)}) copy-start(bf16[4,128]{1,0:T(4,128)(2,1)} %param.8) | copy-start | bytes 3076
  12.0 52.8 %all-to-all-start = ((bf16[32,128,2,64]{1,3,2,0:T(8,128)(2,1)}), bf16[32,128,2,64]{1,3,2,0:T(8,128)(2,1)S(1)}, u32[]{:S(2)}, u32[]{:S(2)}) async-start(bf16[32,128,2,64]{1,3,2,0:T(8,128)(2,1)} %broadcast_in_dim.19), calls=%async_computation | async-start | bytes 2097152 | tf_op jit(solution)/shard_map/all_to_all | solution.py:23
  28.5 145.4 %reduce-scatter.2.cloned.1.call-start = ((), (), s32[]{:S(2)}) async-start(), calls=%async_computation.7 | async-start | bytes 3538944 | tf_op jit(solution)/shard_map/reduce_scatter | solution.py:101
  84.2 5.4 %copy-start = (bf16[3,4096,128]{2,1,0:T(8,128)(2,1)S(1)}, bf16[3,4096,128]{2,1,0:T(8,128)(2,1)}, u32[]{:S(2)}) copy-start(bf16[3,4096,128]{2,1,0:T(8,128)(2,1)} %all-gather.2.cloned.1.call-done) | copy-start | bytes 9437188
  86.5 3.0 %collective-permute-start = (bf16[3,128]{1,0:T(4,128)(2,1)S(1)}, bf16[3,128]{1,0:T(4,128)(2,1)S(1)}, u32[]{:S(2)}, u32[]{:S(2)}) collective-permute-start(bf16[3,128]{1,0:T(4,128)(2,1)S(1)} %slice_bitcast_fusion.11), channel_id=1, source_target_pairs={{0,1},{1,2},{2,3},{3,4},{4,5},{5,6},{6,7},{8,9},{9,10},{10,11},{11... | collective-permute-start | bytes 2312 | tf_op jit(solution)/shard_map/ppermute | solution.py:13
  90.1 4.6 %collective-permute-start.1 = (bf16[3,128]{1,0:T(4,128)(2,1)S(1)}, bf16[3,128]{1,0:T(4,128)(2,1)S(1)}, u32[]{:S(2)}, u32[]{:S(2)}) collective-permute-start(bf16[3,128]{1,0:T(4,128)(2,1)S(1)} %slice.133), channel_id=1, source_target_pairs={{1,0},{2,1},{3,2},{4,3},{5,4},{6,5},{7,6},{9,8},{10,9},{11,10},{12... | collective-permute-start | bytes 2312 | tf_op jit(solution)/shard_map/ppermute | solution.py:13
  97.4 1.2 slice-start
  110.5 12.5 %all-to-all-start.4 = ((bf16[8,15,128]{2,1,0:T(8,128)(2,1)}), bf16[8,15,128]{2,1,0:T(8,128)(2,1)S(1)}, u32[]{:S(2)}, u32[]{:S(2)}) async-start(bf16[8,15,128]{2,1,0:T(8,128)(2,1)} %broadcast_in_dim.24), calls=%async_computation.5 | async-start | bytes 65536 | tf_op jit(solution)/shard_map/all_to_all | solution.py:106
  122.9 50.2 %all-to-all-start.3 = ((bf16[32,64,2,128]{3,1,2,0:T(8,128)(2,1)}), bf16[32,64,2,128]{3,1,2,0:T(8,128)(2,1)S(1)}, u32[]{:S(2)}, u32[]{:S(2)}) async-start(bf16[32,64,2,128]{3,1,2,0:T(8,128)(2,1)} %copy.68), calls=%async_computation.3 | async-start | bytes 2097152 | tf_op jit(solution)/shard_map/all_to_all | solution.py:39
  173.9 2.1 %copy-start.1 = (bf16[3,512,128]{1,2,0:T(8,128)(2,1)S(1)}, bf16[3,512,128]{1,2,0:T(8,128)(2,1)}, u32[]{:S(2)}) copy-start(bf16[3,512,128]{1,2,0:T(8,128)(2,1)} %reduce-scatter.2.cloned.1.call-done) | copy-start | bytes 1179652
Sparse Core Ops, SparseCore 0:
  10.7 73.4 all-gather.1
  97.6 76.1 reduce-scatter.1

commit v13 on v12

--- a/solution.py
+++ b/solution.py
@@ -48,34 +48,48 @@
     w_full = lax.all_gather(w_local, "seq", axis=1, tiled=True)
     in_full = w_full[:2]
     out_full_t = w_full[2]
-    acts = gather_over(jnp.stack([tokens, grad_out], axis=1), "chip", n_chip, 2)
+    taps = conv_weight.shape[0]
+    rim_rows = taps - 1
+    tok_rows = tokens.shape[0]
+    ext_tok = jnp.concatenate(
+        [
+            from_behind(tokens[tok_rows - rim_rows :], "seq", 1),
+            tokens,
+            from_behind(tokens[:rim_rows], "seq", -1),
+        ],
+        axis=0,
+    )
+    ext_go = jnp.concatenate(
+        [jnp.zeros_like(grad_out[:rim_rows]), grad_out, from_behind(grad_out[:rim_rows], "seq", -1)],
+        axis=0,
+    )
+    acts = gather_over(jnp.stack([ext_tok, ext_go], axis=1), "chip", n_chip, 2)
     acts = gather_over(acts.reshape(acts.shape[:2] + (n_chip, 1, -1)), "core", n_core, 3)
     acts = acts.reshape(acts.shape[:2] + (-1,))
-    whole = acts[:, 0]
-    upstream = acts[:, 1]
-    tok_rows = whole.shape[0]
-    taps = conv_weight.shape[0]
-    mixed = jnp.einsum("td,pde->tpe", whole, in_full, preferred_element_type=jnp.float32).astype(
+    whole = acts[rim_rows : rim_rows + tok_rows, 0]
+    upstream_ext = acts[rim_rows:, 1]
+    upstream = upstream_ext[:tok_rows]
+    mixed = jnp.einsum("td,pde->tpe", acts[:, 0], in_full, preferred_element_type=jnp.float32).astype(
         jnp.bfloat16
     )
-    inner = mixed[:, 0, :]
-    gate_in = mixed[:, 1, :]
-    rim = from_behind(inner[tok_rows - (taps - 1) :], "seq", 1)
-    padded = jnp.concatenate([rim, inner], axis=0)
-    conv = jnp.broadcast_to(conv_bias.astype(jnp.float32)[None, :], inner.shape)
+    inner_ext = mixed[:, 0, :]
+    gate_in = mixed[rim_rows:, 1, :]
+    n_out = tok_rows + rim_rows
+    conv = jnp.broadcast_to(conv_bias.astype(jnp.float32)[None, :], (n_out, inner_ext.shape[1]))
     for lag in range(taps):
-        conv = conv + conv_weight[lag].astype(jnp.float32)[None, :] * padded[
-            lag : lag + tok_rows
+        conv = conv + conv_weight[lag].astype(jnp.float32)[None, :] * inner_ext[
+            lag : lag + n_out
         ].astype(jnp.float32)
     act, act_slope = silu_parts(conv)
     gate, gate_slope = silu_parts(gate_in.astype(jnp.float32))
-    hidden = (act * gate).astype(jnp.bfloat16)
+    hidden = (act[:tok_rows] * gate[:tok_rows]).astype(jnp.bfloat16)
     out_part = jnp.einsum("te,de->dt", hidden, out_full_t, preferred_element_type=jnp.float32)
-    back = jnp.einsum("td,de->te", upstream, out_full_t, preferred_element_type=jnp.float32)
-    grad_conv = (back * gate * act_slope).astype(jnp.bfloat16)
-    grad_gate = (back * act * gate_slope).astype(jnp.bfloat16)
-    ahead_rim = from_behind(grad_conv[: taps - 1], "seq", -1)
-    ahead = jnp.concatenate([grad_conv, ahead_rim], axis=0)
+    back = jnp.einsum("td,de->te", upstream_ext, out_full_t, preferred_element_type=jnp.float32)
+    ahead = (back * gate * act_slope).astype(jnp.bfloat16)
+    grad_conv = ahead[:tok_rows]
+    grad_gate = (back[:tok_rows] * act[:tok_rows] * gate_slope[:tok_rows]).astype(jnp.bfloat16)
+    padded = inner_ext[:n_out]
+    inner = inner_ext[rim_rows : rim_rows + tok_rows]
     grad_inner = jnp.zeros(inner.shape, jnp.float32)
     for lag in range(taps):
         shift_start = taps - 1 - lag

time: 185 us -> 229 us (1.24)
  waiting for transfers between devices: 90 us -> 118 us
  local copies, waits for them, and re-layouts: 10.8 us -> 31.7 us
  blocking collectives: 18 us -> 9.8 us
    all_to_all x1, waiting for transfers between devices: 36.2 us -> 71.2 us  [gather_over(): return lax.all_to_all(rep, axis, 0, dim + 1, tiled=True)[0]]
    all_to_all x1, local copies, waits for them, and re-layouts: 0.17 us -> 11.9 us  [gather_over(): return lax.all_to_all(rep, axis, 0, dim + 1, tiled=True)[0]]
    all_gather x1, waiting for transfers between devices: 8.53 us -> 0.01 us  [on_device(): w_full = lax.all_gather(w_local, 'seq', axis=1, tiled=True)]
    all_to_all x1 -> x0, blocking collectives: 8.03 us -> none  [reduce_over_dp(): lax.all_to_all(split, 'core', 1, 1, tiled=True).astype(jnp.float32)]
    another operation x0 -> x1, local copies, waits for them, and re-layouts: none -> 6.36 us  [on_device(): acts = acts.reshape(acts.shape[:2] + (-1,))]
    all_to_all x0 -> x1, starting transfers between devices: none -> 4.12 us  [reduce_over_dp(): lax.all_to_all(split, 'core', 1, 1, tiled=True).astype(jnp.float32)]
    all_to_all x1, starting transfers between devices: 7.12 us -> 3.78 us  [on_device(): lax.all_to_all(conv_parts, 'seq', 0, 0, tiled=True).astype(jnp.float32)]
    ppermute x2 -> x3, starting transfers between devices: 3.61 us -> 6.52 us  [from_behind(): return lax.ppermute(block, axis, route)]
  transfers between devices with their start and end apart: 7 -> 9, of which waited for: 6 -> 6; matrix products, arithmetic and copies ran while one was open for 6% -> 13% of each run, Pallas kernels for 0% -> 0%
where the time goes in v13:
time: 229 us; the launch traced here: 228 us
  waiting for transfers between devices  118 us (52%)
  starting transfers between devices  40.1 us (18%)
  local copies, waits for them, and re-layouts  31.7 us (14%)
  between operations  14.3 us (6%)
  blocking collectives  9.8 us (4%)
  matrix products  6.78 us (3%)
  other arithmetic  6.56 us (3%)
    all_to_all x1, waiting for transfers between devices, gather_over(): return lax.all_to_all(rep, axis, 0, dim + 1, tiled=True)[0]  71.2 us
    all_to_all x1, waiting for transfers between devices, reduce_over_dp(): lax.all_to_all(split, 'chip', 0, 0, tiled=True).astype(jnp.float32)  37.7 us
    all_to_all x1, starting transfers between devices, gather_over(): return lax.all_to_all(rep, axis, 0, dim + 1, tiled=True)[0]  15.8 us
    all_to_all x1, local copies, waits for them, and re-layouts, gather_over(): return lax.all_to_all(rep, axis, 0, dim + 1, tiled=True)[0]  11.9 us
    all_to_all x1, starting transfers between devices, reduce_over_dp(): lax.all_to_all(split, 'chip', 0, 0, tiled=True).astype(jnp.float32)  9.84 us
    all_to_all x1, blocking collectives, gather_over(): return lax.all_to_all(rep, axis, 0, dim + 1, tiled=True)[0]  9.8 us
    ppermute x3, starting transfers between devices, from_behind(): return lax.ppermute(block, axis, route)  6.52 us
    another operation x1, local copies, waits for them, and re-layouts, on_device(): acts = acts.reshape(acts.shape[:2] + (-1,))  6.36 us
  transfers between devices with their start and end apart: 9, of which 6 were waited for; matrix products, arithmetic and copies ran while one was open for 13% of the time, Pallas kernels for 0%

profile of v13, /device:TPU:1, one launch (start us, length us, event | category | flops | bytes accessed | tf_op | source)
XLA Modules:
  0.0 227.7 jit_solution(13933357316966035611)
XLA Ops:
  7.2 0.0 all-gather.2.cloned.1.call-start
  7.2 1.0 copy.58
  8.2 1.7 pad_maximum_fusion.2
  10.0 0.0 all-gather.2.cloned.1.call-update
  10.0 0.9 fusion.36
  10.9 3.9 %collective-permute-start = (bf16[3,64]{0,1:T(8,128)(2,1)S(1)}, bf16[3,64]{0,1:T(8,128)(2,1)S(1)}, u32[]{:S(2)}, u32[]{:S(2)}) collective-permute-start(bf16[3,64]{0,1:T(8,128)(2,1)S(1)} %get-tuple-element.62), channel_id=1, source_target_pairs={{0,1},{1,2},{2,3},{3,4},{4,5},{5,6},{6,7},{8,9},{9,10},{10,11},{11... | collective-permute-start | bytes 1160 | tf_op jit(solution)/shard_map/ppermute | solution.py:13
  14.8 1.3 collective-permute-start.1
  16.1 1.3 collective-permute-start.2
  17.4 0.0 collective-permute-done
  17.4 1.8 collective-permute-done.1
  19.3 0.8 maximum_bitcast_fusion
  20.1 1.3 collective-permute-done.2
  21.4 0.8 maximum_bitcast_fusion.1
  22.3 1.6 broadcast_in_dim.22
  23.8 0.0 copy-start.4
  23.8 0.0 copy-start.3
  23.9 15.8 %all-to-all-start = ((bf16[32,134,2,64]{1,3,2,0:T(8,128)(2,1)}), bf16[32,134,2,64]{1,3,2,0:T(8,128)(2,1)S(1)}, u32[]{:S(2)}, u32[]{:S(2)}) async-start(bf16[32,134,2,64]{1,3,2,0:T(8,128)(2,1)} %broadcast_in_dim.22), calls=%async_computation | async-start | bytes 4194304 | tf_op jit(solution)/shard_map/all_to_all | solution.py:23
  39.7 0.0 reduce-scatter.2.cloned.1.call-start
  39.7 0.0 copy-done.4
  39.8 0.0 copy-done.3
  39.8 71.2 %all-to-all-done = bf16[32,134,2,64]{1,3,2,0:T(8,128)(2,1)S(1)} async-done(((bf16[32,134,2,64]{1,3,2,0:T(8,128)(2,1)}), bf16[32,134,2,64]{1,3,2,0:T(8,128)(2,1)S(1)}, u32[]{:S(2)}, u32[]{:S(2)}) %all-to-all-start) | async-done | bytes 1097760 | tf_op jit(solution)/shard_map/all_to_all | solution.py:23
  111.0 0.1 copy.59
  111.1 0.5 broadcast_in_dim.24
  111.7 9.8 %all_to_all.45 = bf16[2,134,2,32,1,64]{1,5,4,3,2,0:T(8,128)(2,1)} all-to-all(bf16[2,134,2,32,1,64]{1,5,4,3,2,0:T(8,128)(2,1)S(1)} %broadcast_in_dim.24), channel_id=1, replica_groups=mesh['chip'=32,'core'=2,'seq'=8] {'core'}, dimensions={0} | all-to-all | bytes 4390912 | tf_op jit(solution)/shard_map/all_to_all | solution.py:23
  121.5 11.9 %copy.60 = bf16[1,134,2,32,2,1,64]{6,4,3,1,2,5,0:T(2,128)(2,1)} copy(bf16[1,134,2,32,2,1,64]{1,6,3,2,4,5,0:T(8,128)(2,1)} %bitcast.151) | data formatting | bytes 4390912 | tf_op jit(solution)/shard_map/all_to_all | solution.py:23
  133.4 6.4 %reshape_squeeze.3 = bf16[134,2,4096]{2,0,1:T(8,128)(2,1)} reshape(bf16[1,134,2,32,2,1,64]{6,4,3,1,2,5,0:T(2,128)(2,1)} %copy.60) | data formatting | bytes 4390912 | tf_op jit(solution)/shard_map/reshape;squeeze | solution.py:68
  139.8 0.0 all-gather.2.cloned.1.call-done
  139.8 0.0 copy-start
  139.8 2.5 %fusion.6 = bf16[134,2,128]{2,0,1:T(8,128)(2,1)S(1)} fusion(bf16[3,4096,128]{2,1,0:T(8,128)(2,1)} %all-gather.2.cloned.1.call-done, bf16[134,2,4096]{2,0,1:T(8,128)(2,1)} %reshape_squeeze.3), kind=kOutput, calls=%fused_computation.12 | convolution fusion | flops 281052672 | bytes 3279872 | tf_op jit(solution)/shard_map/td,pde->tpe/dot_general | solution.py:72
  142.4 0.3 copy-done
  142.6 0.0 copy-start.1
  142.6 1.9 multiply_convert_fusion
  144.5 0.1 fusion.20
  144.7 0.0 copy-done.1
  144.7 0.5 fusion.2
  145.2 0.7 fusion
  145.9 1.9 pad_maximum_fusion
  147.9 0.0 reduce-scatter.2.cloned.1.call-update
  147.9 0.0 slice-start
  147.9 1.2 slice-done
  149.1 0.4 fusion.5
  149.5 0.7 fusion.1
  150.2 0.2 pad_maximum_fusion.1
  150.4 1.5 copy.61
  152.0 4.1 %all-to-all-start.2 = ((bf16[32,2,64,2,128]{4,2,0,3,1:T(8,128)(2,1)}), bf16[32,2,64,2,128]{4,2,0,3,1:T(8,128)(2,1)S(1)}, u32[]{:S(2)}, u32[]{:S(2)}) async-start(bf16[32,2,64,2,128]{4,2,0,3,1:T(8,128)(2,1)} %copy.61), calls=%async_computation.2 | async-start | bytes 4194304 | tf_op jit(solution)/shard_map/all_to_all | solution.py:37
  156.1 2.5 %all-to-all-done.2 = bf16[32,2,64,2,128]{4,2,0,3,1:T(8,128)(2,1)S(1)} async-done(((bf16[32,2,64,2,128]{4,2,0,3,1:T(8,128)(2,1)}), bf16[32,2,64,2,128]{4,2,0,3,1:T(8,128)(2,1)S(1)}, u32[]{:S(2)}, u32[]{:S(2)}) %all-to-all-start.2) | async-done | bytes 2097184 | tf_op jit(solution)/shard_map/all_to_all | solution.py:37
  158.6 0.6 broadcast_in_dim.54
  159.2 3.8 %all-to-all-start.4 = ((bf16[8,15,128]{2,1,0:T(8,128)(2,1)}), bf16[8,15,128]{2,1,0:T(8,128)(2,1)S(1)}, u32[]{:S(2)}, u32[]{:S(2)}) async-start(bf16[8,15,128]{2,1,0:T(8,128)(2,1)} %broadcast_in_dim.54), calls=%async_computation.5 | async-start | bytes 65536 | tf_op jit(solution)/shard_map/all_to_all | solution.py:120
  163.0 0.6 reduce_sum.75
  163.6 1.1 copy.63
  164.7 3.8 %all-to-all-done.4 = bf16[8,15,128]{2,1,0:T(8,128)(2,1)S(1)} async-done(((bf16[8,15,128]{2,1,0:T(8,128)(2,1)}), bf16[8,15,128]{2,1,0:T(8,128)(2,1)S(1)}, u32[]{:S(2)}, u32[]{:S(2)}) %all-to-all-start.4) | async-done | bytes 30752 | tf_op jit(solution)/shard_map/all_to_all | solution.py:120
  168.5 9.8 %all-to-all-start.3 = ((bf16[32,64,2,128]{3,1,2,0:T(8,128)(2,1)}), bf16[32,64,2,128]{3,1,2,0:T(8,128)(2,1)S(1)}, u32[]{:S(2)}, u32[]{:S(2)}) async-start(bf16[32,64,2,128]{3,1,2,0:T(8,128)(2,1)} %copy.63), calls=%async_computation.3 | async-start | bytes 2097152 | tf_op jit(solution)/shard_map/all_to_all | solution.py:39
  178.4 0.6 slice.185
  178.9 0.5 slice_bitcast_fusion.20
  179.5 37.7 %all-to-all-done.3 = bf16[32,64,2,128]{3,1,2,0:T(8,128)(2,1)S(1)} async-done(((bf16[32,64,2,128]{3,1,2,0:T(8,128)(2,1)}), bf16[32,64,2,128]{3,1,2,0:T(8,128)(2,1)S(1)}, u32[]{:S(2)}, u32[]{:S(2)}) %all-to-all-start.3) | async-done | bytes 1048608 | tf_op jit(solution)/shard_map/all_to_all | solution.py:39
  217.1 0.2 reduce.1
  217.3 0.6 slice_bitcast_fusion.18
  217.9 0.0 reduce-scatter.2.cloned.1.call-done
  217.9 0.0 copy-start.2
  217.9 1.1 slice.210
  219.0 1.0 copy.67
  220.0 0.0 copy-done.2
  220.0 0.1 convert_element_type.165
  220.1 0.7 slice_bitcast_fusion.8
  (13 shorter events, 0.2 us)
Async XLA Ops:
  7.2 132.6 %all-gather.2.cloned.1.call-start = ((), (), s32[]{:S(2)}) async-start(), calls=%async_computation.6 | async-start | bytes 3538944 | tf_op jit(solution)/shard_map/all_gather | solution.py:48
  10.9 6.6 %collective-permute-start = (bf16[3,64]{0,1:T(8,128)(2,1)S(1)}, bf16[3,64]{0,1:T(8,128)(2,1)S(1)}, u32[]{:S(2)}, u32[]{:S(2)}) collective-permute-start(bf16[3,64]{0,1:T(8,128)(2,1)S(1)} %get-tuple-element.62), channel_id=1, source_target_pairs={{0,1},{1,2},{2,3},{3,4},{4,5},{5,6},{6,7},{8,9},{9,10},{10,11},{11... | collective-permute-start | bytes 1160 | tf_op jit(solution)/shard_map/ppermute | solution.py:13
  14.8 4.5 %collective-permute-start.1 = (bf16[3,64]{0,1:T(8,128)(2,1)S(1)}, bf16[3,64]{0,1:T(8,128)(2,1)S(1)}, u32[]{:S(2)}, u32[]{:S(2)}) collective-permute-start(bf16[3,64]{0,1:T(8,128)(2,1)S(1)} %get-tuple-element.63), channel_id=1, source_target_pairs={{1,0},{2,1},{3,2},{4,3},{5,4},{6,5},{7,6},{9,8},{10,9},{11,10},{12... | collective-permute-start | bytes 1160 | tf_op jit(solution)/shard_map/ppermute | solution.py:13
  16.1 5.3 %collective-permute-start.2 = (bf16[3,64]{0,1:T(8,128)(2,1)}, bf16[3,64]{0,1:T(8,128)(2,1)S(1)}, u32[]{:S(2)}, u32[]{:S(2)}) collective-permute-start(bf16[3,64]{0,1:T(8,128)(2,1)} %bitcast.156), channel_id=1, source_target_pairs={{1,0},{2,1},{3,2},{4,3},{5,4},{6,5},{7,6},{9,8},{10,9},{11,10},{12... | collective-permute-start | bytes 1160 | tf_op jit(solution)/shard_map/ppermute | solution.py:13
  23.8 15.9 %copy-start.4 = (bf16[128]{0:T(256)(128)(2,1)S(1)}, bf16[128]{0:T(256)(128)(2,1)}, u32[]{:S(2)}) copy-start(bf16[128]{0:T(256)(128)(2,1)} %param.9) | copy-start | bytes 772
  23.8 15.9 %copy-start.3 = (bf16[4,128]{1,0:T(4,128)(2,1)S(1)}, bf16[4,128]{1,0:T(4,128)(2,1)}, u32[]{:S(2)}) copy-start(bf16[4,128]{1,0:T(4,128)(2,1)} %param.8) | copy-start | bytes 3076
  23.9 87.1 %all-to-all-start = ((bf16[32,134,2,64]{1,3,2,0:T(8,128)(2,1)}), bf16[32,134,2,64]{1,3,2,0:T(8,128)(2,1)S(1)}, u32[]{:S(2)}, u32[]{:S(2)}) async-start(bf16[32,134,2,64]{1,3,2,0:T(8,128)(2,1)} %broadcast_in_dim.22), calls=%async_computation | async-start | bytes 4194304 | tf_op jit(solution)/shard_map/all_to_all | solution.py:23
  39.7 178.2 %reduce-scatter.2.cloned.1.call-start = ((), (), s32[]{:S(2)}) async-start(), calls=%async_computation.7 | async-start | bytes 3538944 | tf_op jit(solution)/shard_map/reduce_scatter | solution.py:115
  139.8 2.9 %copy-start = (bf16[3,4096,128]{2,1,0:T(8,128)(2,1)S(1)}, bf16[3,4096,128]{2,1,0:T(8,128)(2,1)}, u32[]{:S(2)}) copy-start(bf16[3,4096,128]{2,1,0:T(8,128)(2,1)} %all-gather.2.cloned.1.call-done) | copy-start | bytes 9437188
  142.6 2.1 copy-start.1
  147.9 1.2 slice-start
  152.0 6.6 %all-to-all-start.2 = ((bf16[32,2,64,2,128]{4,2,0,3,1:T(8,128)(2,1)}), bf16[32,2,64,2,128]{4,2,0,3,1:T(8,128)(2,1)S(1)}, u32[]{:S(2)}, u32[]{:S(2)}) async-start(bf16[32,2,64,2,128]{4,2,0,3,1:T(8,128)(2,1)} %copy.61), calls=%async_computation.2 | async-start | bytes 4194304 | tf_op jit(solution)/shard_map/all_to_all | solution.py:37
  159.2 9.3 %all-to-all-start.4 = ((bf16[8,15,128]{2,1,0:T(8,128)(2,1)}), bf16[8,15,128]{2,1,0:T(8,128)(2,1)S(1)}, u32[]{:S(2)}, u32[]{:S(2)}) async-start(bf16[8,15,128]{2,1,0:T(8,128)(2,1)} %broadcast_in_dim.54), calls=%async_computation.5 | async-start | bytes 65536 | tf_op jit(solution)/shard_map/all_to_all | solution.py:120
  168.5 48.7 %all-to-all-start.3 = ((bf16[32,64,2,128]{3,1,2,0:T(8,128)(2,1)}), bf16[32,64,2,128]{3,1,2,0:T(8,128)(2,1)S(1)}, u32[]{:S(2)}, u32[]{:S(2)}) async-start(bf16[32,64,2,128]{3,1,2,0:T(8,128)(2,1)} %copy.63), calls=%async_computation.3 | async-start | bytes 2097152 | tf_op jit(solution)/shard_map/all_to_all | solution.py:39
  217.9 2.1 copy-start.2
Sparse Core Ops, SparseCore 0:
  10.7 95.4 all-gather.1
  148.0 69.6 reduce-scatter.1

commit v14 on v13

--- a/solution.py
+++ b/solution.py
@@ -50,31 +50,33 @@
     out_full_t = w_full[2]
     taps = conv_weight.shape[0]
     rim_rows = taps - 1
+    halo = 8
+    base = halo - rim_rows
     tok_rows = tokens.shape[0]
     ext_tok = jnp.concatenate(
         [
-            from_behind(tokens[tok_rows - rim_rows :], "seq", 1),
+            from_behind(tokens[tok_rows - halo :], "seq", 1),
             tokens,
-            from_behind(tokens[:rim_rows], "seq", -1),
+            from_behind(tokens[:halo], "seq", -1),
         ],
         axis=0,
     )
     ext_go = jnp.concatenate(
-        [jnp.zeros_like(grad_out[:rim_rows]), grad_out, from_behind(grad_out[:rim_rows], "seq", -1)],
+        [jnp.zeros_like(grad_out[:halo]), grad_out, from_behind(grad_out[:halo], "seq", -1)],
         axis=0,
     )
     acts = gather_over(jnp.stack([ext_tok, ext_go], axis=1), "chip", n_chip, 2)
     acts = gather_over(acts.reshape(acts.shape[:2] + (n_chip, 1, -1)), "core", n_core, 3)
     acts = acts.reshape(acts.shape[:2] + (-1,))
-    whole = acts[rim_rows : rim_rows + tok_rows, 0]
-    upstream_ext = acts[rim_rows:, 1]
+    n_out = tok_rows + rim_rows
+    whole = acts[halo : halo + tok_rows, 0]
+    upstream_ext = acts[halo : halo + n_out, 1]
     upstream = upstream_ext[:tok_rows]
     mixed = jnp.einsum("td,pde->tpe", acts[:, 0], in_full, preferred_element_type=jnp.float32).astype(
         jnp.bfloat16
     )
-    inner_ext = mixed[:, 0, :]
-    gate_in = mixed[rim_rows:, 1, :]
-    n_out = tok_rows + rim_rows
+    inner_ext = mixed[base:, 0, :]
+    gate_in = mixed[halo : halo + n_out, 1, :]
     conv = jnp.broadcast_to(conv_bias.astype(jnp.float32)[None, :], (n_out, inner_ext.shape[1]))
     for lag in range(taps):
         conv = conv + conv_weight[lag].astype(jnp.float32)[None, :] * inner_ext[

time: 229 us -> 228 us (level)
  no operation moved by 1% of the time
where the time goes in v14:
time: 228 us; the launch traced here: 226 us
  waiting for transfers between devices  119 us (52%)
  starting transfers between devices  40.2 us (18%)
  local copies, waits for them, and re-layouts  31.6 us (14%)
  between operations  14.3 us (6%)
  blocking collectives  9.82 us (4%)
  other arithmetic  6.56 us (3%)
  matrix products  5.05 us (2%)
    all_to_all x1, waiting for transfers between devices, gather_over(): return lax.all_to_all(rep, axis, 0, dim + 1, tiled=True)[0]  71.2 us
    all_to_all x1, waiting for transfers between devices, reduce_over_dp(): lax.all_to_all(split, 'chip', 0, 0, tiled=True).astype(jnp.float32)  38.1 us
    all_to_all x1, starting transfers between devices, gather_over(): return lax.all_to_all(rep, axis, 0, dim + 1, tiled=True)[0]  15.8 us
    all_to_all x1, local copies, waits for them, and re-layouts, gather_over(): return lax.all_to_all(rep, axis, 0, dim + 1, tiled=True)[0]  11.6 us
    all_to_all x1, starting transfers between devices, reduce_over_dp(): lax.all_to_all(split, 'chip', 0, 0, tiled=True).astype(jnp.float32)  9.91 us
    all_to_all x1, blocking collectives, gather_over(): return lax.all_to_all(rep, axis, 0, dim + 1, tiled=True)[0]  9.82 us
    ppermute x3, starting transfers between devices, from_behind(): return lax.ppermute(block, axis, route)  6.52 us
    another operation x1, local copies, waits for them, and re-layouts, on_device(): acts = acts.reshape(acts.shape[:2] + (-1,))  6.09 us
  transfers between devices with their start and end apart: 9, of which 6 were waited for; matrix products, arithmetic and copies ran while one was open for 13% of the time, Pallas kernels for 0%

profile of v14, /device:TPU:1, one launch (start us, length us, event | category | flops | bytes accessed | tf_op | source)
XLA Modules:
  0.0 226.4 jit_solution(3609975239542139341)
XLA Ops:
  7.2 0.0 all-gather.2.cloned.1.call-start
  7.2 1.0 copy.58
  8.2 1.7 pad_maximum_fusion.2
  10.0 0.0 all-gather.2.cloned.1.call-update
  10.0 0.9 fusion.36
  10.9 3.9 %collective-permute-start = (bf16[8,64]{0,1:T(8,128)(2,1)S(1)}, bf16[8,64]{0,1:T(8,128)(2,1)S(1)}, u32[]{:S(2)}, u32[]{:S(2)}) collective-permute-start(bf16[8,64]{0,1:T(8,128)(2,1)S(1)} %get-tuple-element.62), channel_id=1, source_target_pairs={{0,1},{1,2},{2,3},{3,4},{4,5},{5,6},{6,7},{8,9},{9,10},{10,11},{11... | collective-permute-start | bytes 3080 | tf_op jit(solution)/shard_map/ppermute | solution.py:13
  14.8 1.3 collective-permute-start.1
  16.1 1.3 collective-permute-start.2
  17.4 0.0 collective-permute-done
  17.4 1.8 collective-permute-done.1
  19.3 0.8 maximum_bitcast_fusion
  20.1 1.3 collective-permute-done.2
  21.4 0.8 maximum_bitcast_fusion.1
  22.3 1.6 broadcast_in_dim.22
  23.8 0.0 copy-start.4
  23.8 0.0 copy-start.3
  23.9 15.8 %all-to-all-start = ((bf16[32,144,2,64]{1,3,2,0:T(8,128)(2,1)}), bf16[32,144,2,64]{1,3,2,0:T(8,128)(2,1)S(1)}, u32[]{:S(2)}, u32[]{:S(2)}) async-start(bf16[32,144,2,64]{1,3,2,0:T(8,128)(2,1)} %broadcast_in_dim.22), calls=%async_computation | async-start | bytes 4194304 | tf_op jit(solution)/shard_map/all_to_all | solution.py:23
  39.7 0.0 reduce-scatter.2.cloned.1.call-start
  39.7 0.0 copy-done.4
  39.8 0.0 copy-done.3
  39.8 71.2 %all-to-all-done = bf16[32,144,2,64]{1,3,2,0:T(8,128)(2,1)S(1)} async-done(((bf16[32,144,2,64]{1,3,2,0:T(8,128)(2,1)}), bf16[32,144,2,64]{1,3,2,0:T(8,128)(2,1)S(1)}, u32[]{:S(2)}, u32[]{:S(2)}) %all-to-all-start) | async-done | bytes 1179680 | tf_op jit(solution)/shard_map/all_to_all | solution.py:23
  111.0 0.1 copy.59
  111.1 0.5 broadcast_in_dim.24
  111.7 9.8 %all_to_all.45 = bf16[2,144,2,32,1,64]{1,5,4,3,2,0:T(8,128)(2,1)} all-to-all(bf16[2,144,2,32,1,64]{1,5,4,3,2,0:T(8,128)(2,1)S(1)} %broadcast_in_dim.24), channel_id=1, replica_groups=mesh['chip'=32,'core'=2,'seq'=8] {'core'}, dimensions={0} | all-to-all | bytes 4718592 | tf_op jit(solution)/shard_map/all_to_all | solution.py:23
  121.5 11.6 %copy.60 = bf16[1,144,2,32,2,1,64]{6,4,3,1,2,5,0:T(2,128)(2,1)} copy(bf16[1,144,2,32,2,1,64]{1,6,3,2,4,5,0:T(8,128)(2,1)} %bitcast.153) | data formatting | bytes 4718592 | tf_op jit(solution)/shard_map/all_to_all | solution.py:23
  133.1 6.1 %reshape_squeeze.3 = bf16[144,2,4096]{2,0,1:T(8,128)(2,1)S(1)} reshape(bf16[1,144,2,32,2,1,64]{6,4,3,1,2,5,0:T(2,128)(2,1)} %copy.60) | data formatting | bytes 4718592 | tf_op jit(solution)/shard_map/reshape;squeeze | solution.py:70
  139.2 0.0 all-gather.2.cloned.1.call-done
  139.2 0.0 copy-start
  139.2 2.2 fusion.6
  141.5 0.3 copy-done
  141.8 0.5 multiply_convert_fusion
  142.2 0.1 fusion.20
  142.4 0.5 fusion.2
  142.9 0.7 fusion
  143.6 1.9 pad_maximum_fusion
  145.5 0.0 slice-start
  145.5 0.0 reduce-scatter.2.cloned.1.call-update
  145.6 0.0 copy-start.1
  145.6 1.2 slice-done
  146.8 0.4 fusion.5
  147.2 0.6 copy-done.1
  147.8 0.7 fusion.1
  148.5 0.2 pad_maximum_fusion.1
  148.7 1.5 copy.61
  150.2 4.1 %all-to-all-start.2 = ((bf16[32,2,64,2,128]{4,2,0,3,1:T(8,128)(2,1)}), bf16[32,2,64,2,128]{4,2,0,3,1:T(8,128)(2,1)S(1)}, u32[]{:S(2)}, u32[]{:S(2)}) async-start(bf16[32,2,64,2,128]{4,2,0,3,1:T(8,128)(2,1)} %copy.61), calls=%async_computation.2 | async-start | bytes 4194304 | tf_op jit(solution)/shard_map/all_to_all | solution.py:37
  154.4 2.5 %all-to-all-done.2 = bf16[32,2,64,2,128]{4,2,0,3,1:T(8,128)(2,1)S(1)} async-done(((bf16[32,2,64,2,128]{4,2,0,3,1:T(8,128)(2,1)}), bf16[32,2,64,2,128]{4,2,0,3,1:T(8,128)(2,1)S(1)}, u32[]{:S(2)}, u32[]{:S(2)}) %all-to-all-start.2) | async-done | bytes 2097184 | tf_op jit(solution)/shard_map/all_to_all | solution.py:37
  156.8 0.6 broadcast_in_dim.54
  157.4 3.8 %all-to-all-start.4 = ((bf16[8,15,128]{2,1,0:T(8,128)(2,1)}), bf16[8,15,128]{2,1,0:T(8,128)(2,1)S(1)}, u32[]{:S(2)}, u32[]{:S(2)}) async-start(bf16[8,15,128]{2,1,0:T(8,128)(2,1)} %broadcast_in_dim.54), calls=%async_computation.5 | async-start | bytes 65536 | tf_op jit(solution)/shard_map/all_to_all | solution.py:122
  161.2 0.6 reduce_sum.75
  161.8 1.1 copy.63
  162.9 3.8 %all-to-all-done.4 = bf16[8,15,128]{2,1,0:T(8,128)(2,1)S(1)} async-done(((bf16[8,15,128]{2,1,0:T(8,128)(2,1)}), bf16[8,15,128]{2,1,0:T(8,128)(2,1)S(1)}, u32[]{:S(2)}, u32[]{:S(2)}) %all-to-all-start.4) | async-done | bytes 30752 | tf_op jit(solution)/shard_map/all_to_all | solution.py:122
  166.7 9.9 %all-to-all-start.3 = ((bf16[32,64,2,128]{3,1,2,0:T(8,128)(2,1)}), bf16[32,64,2,128]{3,1,2,0:T(8,128)(2,1)S(1)}, u32[]{:S(2)}, u32[]{:S(2)}) async-start(bf16[32,64,2,128]{3,1,2,0:T(8,128)(2,1)} %copy.63), calls=%async_computation.3 | async-start | bytes 2097152 | tf_op jit(solution)/shard_map/all_to_all | solution.py:39
  176.7 0.6 slice.185
  177.2 0.5 slice_bitcast_fusion.22
  177.7 38.1 %all-to-all-done.3 = bf16[32,64,2,128]{3,1,2,0:T(8,128)(2,1)S(1)} async-done(((bf16[32,64,2,128]{3,1,2,0:T(8,128)(2,1)}), bf16[32,64,2,128]{3,1,2,0:T(8,128)(2,1)S(1)}, u32[]{:S(2)}, u32[]{:S(2)}) %all-to-all-start.3) | async-done | bytes 1048608 | tf_op jit(solution)/shard_map/all_to_all | solution.py:39
  215.9 0.2 reduce.1
  216.0 0.6 slice_bitcast_fusion.20
  216.7 0.0 reduce-scatter.2.cloned.1.call-done
  216.7 0.0 copy-start.2
  216.7 1.1 slice.210
  217.7 1.0 copy.67
  218.7 0.0 copy-done.2
  218.7 0.1 convert_element_type.165
  218.8 0.7 slice_bitcast_fusion.10
  (13 shorter events, 0.2 us)
Async XLA Ops:
  7.2 132.1 %all-gather.2.cloned.1.call-start = ((), (), s32[]{:S(2)}) async-start(), calls=%async_computation.6 | async-start | bytes 3538944 | tf_op jit(solution)/shard_map/all_gather | solution.py:48
  10.9 6.6 %collective-permute-start = (bf16[8,64]{0,1:T(8,128)(2,1)S(1)}, bf16[8,64]{0,1:T(8,128)(2,1)S(1)}, u32[]{:S(2)}, u32[]{:S(2)}) collective-permute-start(bf16[8,64]{0,1:T(8,128)(2,1)S(1)} %get-tuple-element.62), channel_id=1, source_target_pairs={{0,1},{1,2},{2,3},{3,4},{4,5},{5,6},{6,7},{8,9},{9,10},{10,11},{11... | collective-permute-start | bytes 3080 | tf_op jit(solution)/shard_map/ppermute | solution.py:13
  14.8 4.5 %collective-permute-start.1 = (bf16[8,64]{0,1:T(8,128)(2,1)S(1)}, bf16[8,64]{0,1:T(8,128)(2,1)S(1)}, u32[]{:S(2)}, u32[]{:S(2)}) collective-permute-start(bf16[8,64]{0,1:T(8,128)(2,1)S(1)} %get-tuple-element.63), channel_id=1, source_target_pairs={{1,0},{2,1},{3,2},{4,3},{5,4},{6,5},{7,6},{9,8},{10,9},{11,10},{12... | collective-permute-start | bytes 3080 | tf_op jit(solution)/shard_map/ppermute | solution.py:13
  16.1 5.3 %collective-permute-start.2 = (bf16[8,64]{0,1:T(8,128)(2,1)}, bf16[8,64]{0,1:T(8,128)(2,1)S(1)}, u32[]{:S(2)}, u32[]{:S(2)}) collective-permute-start(bf16[8,64]{0,1:T(8,128)(2,1)} %bitcast.158), channel_id=1, source_target_pairs={{1,0},{2,1},{3,2},{4,3},{5,4},{6,5},{7,6},{9,8},{10,9},{11,10},{12... | collective-permute-start | bytes 3080 | tf_op jit(solution)/shard_map/ppermute | solution.py:13
  23.8 15.9 %copy-start.4 = (bf16[128]{0:T(256)(128)(2,1)S(1)}, bf16[128]{0:T(256)(128)(2,1)}, u32[]{:S(2)}) copy-start(bf16[128]{0:T(256)(128)(2,1)} %param.9) | copy-start | bytes 772
  23.8 15.9 %copy-start.3 = (bf16[4,128]{1,0:T(4,128)(2,1)S(1)}, bf16[4,128]{1,0:T(4,128)(2,1)}, u32[]{:S(2)}) copy-start(bf16[4,128]{1,0:T(4,128)(2,1)} %param.8) | copy-start | bytes 3076
  23.9 87.1 %all-to-all-start = ((bf16[32,144,2,64]{1,3,2,0:T(8,128)(2,1)}), bf16[32,144,2,64]{1,3,2,0:T(8,128)(2,1)S(1)}, u32[]{:S(2)}, u32[]{:S(2)}) async-start(bf16[32,144,2,64]{1,3,2,0:T(8,128)(2,1)} %broadcast_in_dim.22), calls=%async_computation | async-start | bytes 4194304 | tf_op jit(solution)/shard_map/all_to_all | solution.py:23
  39.7 177.0 %reduce-scatter.2.cloned.1.call-start = ((), (), s32[]{:S(2)}) async-start(), calls=%async_computation.7 | async-start | bytes 3538944 | tf_op jit(solution)/shard_map/reduce_scatter | solution.py:117
  139.2 2.5 %copy-start = (bf16[3,4096,128]{2,1,0:T(8,128)(2,1)S(1)}, bf16[3,4096,128]{2,1,0:T(8,128)(2,1)}, u32[]{:S(2)}) copy-start(bf16[3,4096,128]{2,1,0:T(8,128)(2,1)} %all-gather.2.cloned.1.call-done) | copy-start | bytes 9437188
  145.5 1.2 slice-start
  145.6 2.2 copy-start.1
  150.2 6.6 %all-to-all-start.2 = ((bf16[32,2,64,2,128]{4,2,0,3,1:T(8,128)(2,1)}), bf16[32,2,64,2,128]{4,2,0,3,1:T(8,128)(2,1)S(1)}, u32[]{:S(2)}, u32[]{:S(2)}) async-start(bf16[32,2,64,2,128]{4,2,0,3,1:T(8,128)(2,1)} %copy.61), calls=%async_computation.2 | async-start | bytes 4194304 | tf_op jit(solution)/shard_map/all_to_all | solution.py:37
  157.4 9.3 %all-to-all-start.4 = ((bf16[8,15,128]{2,1,0:T(8,128)(2,1)}), bf16[8,15,128]{2,1,0:T(8,128)(2,1)S(1)}, u32[]{:S(2)}, u32[]{:S(2)}) async-start(bf16[8,15,128]{2,1,0:T(8,128)(2,1)} %broadcast_in_dim.54), calls=%async_computation.5 | async-start | bytes 65536 | tf_op jit(solution)/shard_map/all_to_all | solution.py:122
  166.7 49.2 %all-to-all-start.3 = ((bf16[32,64,2,128]{3,1,2,0:T(8,128)(2,1)}), bf16[32,64,2,128]{3,1,2,0:T(8,128)(2,1)S(1)}, u32[]{:S(2)}, u32[]{:S(2)}) async-start(bf16[32,64,2,128]{3,1,2,0:T(8,128)(2,1)} %copy.63), calls=%async_computation.3 | async-start | bytes 2097152 | tf_op jit(solution)/shard_map/all_to_all | solution.py:39
  216.7 2.1 copy-start.2
Sparse Core Ops, SparseCore 0:
  10.7 95.4 all-gather.1
  145.7 68.8 reduce-scatter.1

commit v15 on v12

--- a/solution.py
+++ b/solution.py
@@ -60,7 +60,10 @@
     )
     inner = mixed[:, 0, :]
     gate_in = mixed[:, 1, :]
-    rim = from_behind(inner[tok_rows - (taps - 1) :], "seq", 1)
+    tail = jnp.einsum(
+        "td,de->te", whole[tok_rows - (taps - 1) :], in_full[0], preferred_element_type=jnp.float32
+    ).astype(jnp.bfloat16)
+    rim = from_behind(tail, "seq", 1)
     padded = jnp.concatenate([rim, inner], axis=0)
     conv = jnp.broadcast_to(conv_bias.astype(jnp.float32)[None, :], inner.shape)
     for lag in range(taps):
@@ -74,7 +77,11 @@
     back = jnp.einsum("td,de->te", upstream, out_full_t, preferred_element_type=jnp.float32)
     grad_conv = (back * gate * act_slope).astype(jnp.bfloat16)
     grad_gate = (back * act * gate_slope).astype(jnp.bfloat16)
-    ahead_rim = from_behind(grad_conv[: taps - 1], "seq", -1)
+    head_back = jnp.einsum(
+        "td,de->te", upstream[: taps - 1], out_full_t, preferred_element_type=jnp.float32
+    )
+    head = (head_back * gate[: taps - 1] * act_slope[: taps - 1]).astype(jnp.bfloat16)
+    ahead_rim = from_behind(head, "seq", -1)
     ahead = jnp.concatenate([grad_conv, ahead_rim], axis=0)
     grad_inner = jnp.zeros(inner.shape, jnp.float32)
     for lag in range(taps):

time: 185 us -> 186 us (level)
  matrix products: 6.81 us -> 9.27 us
    dot_general x0 -> x2, matrix products: none -> 2.61 us  [the longest x1 2.18 us: on_device(): jnp.einsum('td,de->te', whole[tok_rows - (taps - 1):], in_full[0], prefer...]
  transfers between devices with their start and end apart: 7 -> 7, of which waited for: 6 -> 5; matrix products, arithmetic and copies ran while one was open for 6% -> 7% of each run, Pallas kernels for 0% -> 0%
where the time goes in v15:
time: 186 us; the launch traced here: 185 us
  waiting for transfers between devices  89.1 us (48%)
  starting transfers between devices  38 us (20%)
  blocking collectives  17.4 us (9%)
  between operations  14.3 us (8%)
  local copies, waits for them, and re-layouts  10.8 us (6%)
  matrix products  9.27 us (5%)
  other arithmetic  5.71 us (3%)
    all_to_all x1, waiting for transfers between devices, reduce_over_dp(): lax.all_to_all(split, 'chip', 0, 0, tiled=True).astype(jnp.float32)  38.2 us
    all_to_all x1, waiting for transfers between devices, gather_over(): return lax.all_to_all(rep, axis, 0, dim + 1, tiled=True)[0]  36.2 us
    all_to_all x1, starting transfers between devices, gather_over(): return lax.all_to_all(rep, axis, 0, dim + 1, tiled=True)[0]  16.5 us
    all_to_all x1, starting transfers between devices, reduce_over_dp(): lax.all_to_all(split, 'chip', 0, 0, tiled=True).astype(jnp.float32)  10.9 us
    all_to_all x1, blocking collectives, gather_over(): return lax.all_to_all(rep, axis, 0, dim + 1, tiled=True)[0]  9.93 us
    all_gather x1, waiting for transfers between devices, on_device(): w_full = lax.all_gather(w_local, 'seq', axis=1, tiled=True)  8.53 us
    all_to_all x1, blocking collectives, reduce_over_dp(): lax.all_to_all(split, 'core', 1, 1, tiled=True).astype(jnp.float32)  7.46 us
    all_to_all x1, starting transfers between devices, on_device(): lax.all_to_all(conv_parts, 'seq', 0, 0, tiled=True).astype(jnp.float32)  6.64 us
  transfers between devices with their start and end apart: 7, of which 5 were waited for; matrix products, arithmetic and copies ran while one was open for 7% of the time, Pallas kernels for 0%

profile of v15, /device:TPU:1, one launch (start us, length us, event | category | flops | bytes accessed | tf_op | source)
XLA Modules:
  0.0 184.5 jit_solution(14932046950664624298)
XLA Ops:
  7.2 0.0 all-gather.2.cloned.1.call-start
  7.2 1.0 copy.62
  8.2 0.0 copy-start.3
  8.2 0.0 copy-start.2
  8.3 1.7 pad_maximum_fusion.2
  10.0 0.0 all-gather.2.cloned.1.call-update
  10.0 0.7 pad_maximum_fusion.8
  10.8 1.2 broadcast_in_dim.19
  12.0 16.5 %all-to-all-start = ((bf16[32,128,2,64]{1,3,2,0:T(8,128)(2,1)}), bf16[32,128,2,64]{1,3,2,0:T(8,128)(2,1)S(1)}, u32[]{:S(2)}, u32[]{:S(2)}) async-start(bf16[32,128,2,64]{1,3,2,0:T(8,128)(2,1)} %broadcast_in_dim.19), calls=%async_computation | async-start | bytes 2097152 | tf_op jit(solution)/shard_map/all_to_all | solution.py:23
  28.5 0.0 reduce-scatter.2.cloned.1.call-start
  28.6 0.0 copy-done.3
  28.6 0.0 copy-done.2
  28.6 36.2 %all-to-all-done = bf16[32,128,2,64]{1,3,2,0:T(8,128)(2,1)S(1)} async-done(((bf16[32,128,2,64]{1,3,2,0:T(8,128)(2,1)}), bf16[32,128,2,64]{1,3,2,0:T(8,128)(2,1)S(1)}, u32[]{:S(2)}, u32[]{:S(2)}) %all-to-all-start) | async-done | bytes 1048608 | tf_op jit(solution)/shard_map/all_to_all | solution.py:23
  64.8 0.1 copy.63
  64.9 0.6 broadcast_in_dim.21
  65.5 9.9 %all_to_all.45 = bf16[2,128,2,32,1,64]{1,5,3,2,4,0:T(8,128)(2,1)S(1)} all-to-all(bf16[2,128,2,32,1,64]{1,5,3,2,4,0:T(8,128)(2,1)S(1)} %broadcast_in_dim.21), channel_id=1, replica_groups=mesh['chip'=32,'core'=2,'seq'=8] {'core'}, dimensions={0} | all-to-all | bytes 4194304 | tf_op jit(solution)/shard_map/all_to_all | solution.py:23
  75.5 0.2 copy.64
  75.6 8.5 %all-gather.2.cloned.1.call-done = bf16[3,4096,128]{2,1,0:T(8,128)(2,1)} async-done(((bf16[3,512,128]{2,1,0:T(8,128)(2,1)}), bf16[3,4096,128]{2,1,0:T(8,128)(2,1)}) %all-gather.2.cloned.1.call-update) | async-done | bytes 3145744 | tf_op jit(solution)/shard_map/all_gather | solution.py:48
  84.2 2.2 %convolution_convert_fusion.3 = bf16[3,128]{1,0:T(4,128)(2,1)S(1)} fusion(bf16[3,4096,128]{2,1,0:T(8,128)(2,1)} %all-gather.2.cloned.1.call-done, bf16[128,2,4096]{0,2,1:T(8,128)(2,1)S(1)} %bitcast.118), kind=kOutput, calls=%fused_computation.16 | convolution fusion | flops 3146112 | bytes 2097920 | tf_op jit(solution)/shard_map/td,de->te/dot_general | solution.py:63
  86.4 0.0 copy-start
  86.4 2.6 %collective-permute-start = (bf16[3,128]{1,0:T(4,128)(2,1)S(1)}, bf16[3,128]{1,0:T(4,128)(2,1)S(1)}, u32[]{:S(2)}, u32[]{:S(2)}) collective-permute-start(bf16[3,128]{1,0:T(4,128)(2,1)S(1)} %convolution_convert_fusion.3), channel_id=1, source_target_pairs={{0,1},{1,2},{2,3},{3,4},{4,5},{5,6},{6,7},{8,9},{9,10},{10,11},{11... | collective-permute-start | bytes 2312 | tf_op jit(solution)/shard_map/ppermute | solution.py:13
  88.9 2.2 %fusion.6 = bf16[128,2,128]{2,0,1:T(8,128)(2,1)S(1)} fusion(bf16[3,4096,128]{2,1,0:T(8,128)(2,1)} %all-gather.2.cloned.1.call-done, bf16[128,2,4096]{0,2,1:T(8,128)(2,1)S(1)} %bitcast.119), kind=kOutput, calls=%fused_computation.12 | convolution fusion | flops 268468224 | bytes 3211264 | tf_op jit(solution)/shard_map/td,pde->tpe/dot_general | solution.py:58
  91.1 0.0 collective-permute-done
  91.1 0.0 copy-done
  91.2 0.5 fusion.29
  91.7 0.1 add_multiply_fusion
  91.8 0.4 fusion.10
  92.2 1.3 collective-permute-start.1
  93.5 0.5 fusion.2
  94.0 2.5 %collective-permute-done.1 = bf16[3,128]{1,0:T(4,128)(2,1)S(1)} collective-permute-done((bf16[3,128]{1,0:T(4,128)(2,1)S(1)}, bf16[3,128]{1,0:T(4,128)(2,1)S(1)}, u32[]{:S(2)}, u32[]{:S(2)}) %collective-permute-start.1) | collective-permute-done | bytes 800 | tf_op jit(solution)/shard_map/ppermute | solution.py:13
  96.6 0.7 fusion
  97.3 2.0 %pad_maximum_fusion = bf16[3,4096,128]{1,2,0:T(8,128)(2,1)} fusion(bf16[1,4096,128]{1,2,0:T(8,128)(2,1)S(1)} %fusion.2, bf16[2,4096,128]{1,2,0:T(8,128)(2,1)S(1)} %fusion), kind=kLoop, calls=%fused_computation.6 | loop fusion | flops 1572864 | bytes 6291456 | tf_op jit(solution)/shard_map/concatenate | solution.py:107
  99.3 0.0 slice-start
  99.3 0.0 reduce-scatter.2.cloned.1.call-update
  99.3 1.1 slice-done
  100.5 0.5 fusion.5
  101.0 2.3 %fusion.1 = bf16[4096,128]{1,0:T(8,128)(2,1)S(1)} fusion(bf16[3,4096,128]{2,1,0:T(8,128)(2,1)} %all-gather.2.cloned.1.call-done, bf16[128,1,128]{2,0,1:T(8,128)(2,1)S(1)} %get-tuple-element.57, bf16[128,1,128]{2,0,1:T(8,128)(2,1)S(1)} %fusion.38), kind=kOutput, calls=%fused_computation.3 | convolution fusion | flops 269090816 | bytes 4259840 | tf_op jit(solution)/shard_map/tpe,pde->dt/dot_general | solution.py:101
  103.2 0.2 pad_maximum_fusion.1
  103.4 0.2 copy.66
  103.7 7.5 %all_to_all.46 = bf16[32,2,64,2,128]{4,2,0,3,1:T(8,128)(2,1)S(1)} all-to-all(bf16[32,2,64,2,128]{4,2,0,3,1:T(8,128)(2,1)S(1)} %copy.66), channel_id=1, replica_groups=mesh['chip'=32,'core'=2,'seq'=8] {'core'}, dimensions={1} | all-to-all | bytes 4194304 | tf_op jit(solution)/shard_map/all_to_all | solution.py:37
  111.1 0.6 broadcast_in_dim.24
  111.8 6.6 %all-to-all-start.4 = ((bf16[8,15,128]{2,1,0:T(8,128)(2,1)}), bf16[8,15,128]{2,1,0:T(8,128)(2,1)S(1)}, u32[]{:S(2)}, u32[]{:S(2)}) async-start(bf16[8,15,128]{2,1,0:T(8,128)(2,1)} %broadcast_in_dim.24), calls=%async_computation.5 | async-start | bytes 65536 | tf_op jit(solution)/shard_map/all_to_all | solution.py:113
  118.4 0.6 reduce_sum.75
  119.0 1.1 copy.68
  120.1 3.6 %all-to-all-done.4 = bf16[8,15,128]{2,1,0:T(8,128)(2,1)S(1)} async-done(((bf16[8,15,128]{2,1,0:T(8,128)(2,1)}), bf16[8,15,128]{2,1,0:T(8,128)(2,1)S(1)}, u32[]{:S(2)}, u32[]{:S(2)}) %all-to-all-start.4) | async-done | bytes 30752 | tf_op jit(solution)/shard_map/all_to_all | solution.py:113
  123.7 10.9 %all-to-all-start.3 = ((bf16[32,64,2,128]{3,1,2,0:T(8,128)(2,1)}), bf16[32,64,2,128]{3,1,2,0:T(8,128)(2,1)S(1)}, u32[]{:S(2)}, u32[]{:S(2)}) async-start(bf16[32,64,2,128]{3,1,2,0:T(8,128)(2,1)} %copy.68), calls=%async_computation.3 | async-start | bytes 2097152 | tf_op jit(solution)/shard_map/all_to_all | solution.py:39
  134.7 0.6 slice.138
  135.2 0.5 slice_bitcast_fusion.17
  135.8 38.2 %all-to-all-done.3 = bf16[32,64,2,128]{3,1,2,0:T(8,128)(2,1)S(1)} async-done(((bf16[32,64,2,128]{3,1,2,0:T(8,128)(2,1)}), bf16[32,64,2,128]{3,1,2,0:T(8,128)(2,1)S(1)}, u32[]{:S(2)}, u32[]{:S(2)}) %all-to-all-start.3) | async-done | bytes 1048608 | tf_op jit(solution)/shard_map/all_to_all | solution.py:39
  174.0 0.2 reduce.1
  174.2 0.6 slice_bitcast_fusion.15
  174.8 0.0 reduce-scatter.2.cloned.1.call-done
  174.8 0.0 copy-start.1
  174.8 1.1 slice.161
  175.9 1.0 copy.72
  176.9 0.0 copy-done.1
  176.9 0.1 convert_element_type.137
  176.9 0.7 slice_bitcast_fusion.12
  (9 shorter events, 0.1 us)
Async XLA Ops:
  7.2 77.0 %all-gather.2.cloned.1.call-start = ((), (), s32[]{:S(2)}) async-start(), calls=%async_computation.6 | async-start | bytes 3538944 | tf_op jit(solution)/shard_map/all_gather | solution.py:48
  8.2 20.3 %copy-start.3 = (bf16[128]{0:T(256)(128)(2,1)S(1)}, bf16[128]{0:T(256)(128)(2,1)}, u32[]{:S(2)}) copy-start(bf16[128]{0:T(256)(128)(2,1)} %param.9) | copy-start | bytes 772
  8.2 20.4 %copy-start.2 = (bf16[4,128]{1,0:T(4,128)(2,1)S(1)}, bf16[4,128]{1,0:T(4,128)(2,1)}, u32[]{:S(2)}) copy-start(bf16[4,128]{1,0:T(4,128)(2,1)} %param.8) | copy-start | bytes 3076
  12.0 52.8 %all-to-all-start = ((bf16[32,128,2,64]{1,3,2,0:T(8,128)(2,1)}), bf16[32,128,2,64]{1,3,2,0:T(8,128)(2,1)S(1)}, u32[]{:S(2)}, u32[]{:S(2)}) async-start(bf16[32,128,2,64]{1,3,2,0:T(8,128)(2,1)} %broadcast_in_dim.19), calls=%async_computation | async-start | bytes 2097152 | tf_op jit(solution)/shard_map/all_to_all | solution.py:23
  28.5 146.2 %reduce-scatter.2.cloned.1.call-start = ((), (), s32[]{:S(2)}) async-start(), calls=%async_computation.7 | async-start | bytes 3538944 | tf_op jit(solution)/shard_map/reduce_scatter | solution.py:108
  86.4 4.8 %copy-start = (bf16[3,4096,128]{2,1,0:T(8,128)(2,1)S(1)}, bf16[3,4096,128]{2,1,0:T(8,128)(2,1)}, u32[]{:S(2)}) copy-start(bf16[3,4096,128]{2,1,0:T(8,128)(2,1)} %all-gather.2.cloned.1.call-done) | copy-start | bytes 9437188
  86.4 4.8 %collective-permute-start = (bf16[3,128]{1,0:T(4,128)(2,1)S(1)}, bf16[3,128]{1,0:T(4,128)(2,1)S(1)}, u32[]{:S(2)}, u32[]{:S(2)}) collective-permute-start(bf16[3,128]{1,0:T(4,128)(2,1)S(1)} %convolution_convert_fusion.3), channel_id=1, source_target_pairs={{0,1},{1,2},{2,3},{3,4},{4,5},{5,6},{6,7},{8,9},{9,10},{10,11},{11... | collective-permute-start | bytes 2312 | tf_op jit(solution)/shard_map/ppermute | solution.py:13
  92.2 4.3 %collective-permute-start.1 = (bf16[3,128]{1,0:T(4,128)(2,1)S(1)}, bf16[3,128]{1,0:T(4,128)(2,1)S(1)}, u32[]{:S(2)}, u32[]{:S(2)}) collective-permute-start(bf16[3,128]{1,0:T(4,128)(2,1)S(1)} %fusion.10), channel_id=1, source_target_pairs={{1,0},{2,1},{3,2},{4,3},{5,4},{6,5},{7,6},{9,8},{10,9},{11,10},{12... | collective-permute-start | bytes 2312 | tf_op jit(solution)/shard_map/ppermute | solution.py:13
  99.3 1.2 slice-start
  111.8 12.0 %all-to-all-start.4 = ((bf16[8,15,128]{2,1,0:T(8,128)(2,1)}), bf16[8,15,128]{2,1,0:T(8,128)(2,1)S(1)}, u32[]{:S(2)}, u32[]{:S(2)}) async-start(bf16[8,15,128]{2,1,0:T(8,128)(2,1)} %broadcast_in_dim.24), calls=%async_computation.5 | async-start | bytes 65536 | tf_op jit(solution)/shard_map/all_to_all | solution.py:113
  123.7 50.3 %all-to-all-start.3 = ((bf16[32,64,2,128]{3,1,2,0:T(8,128)(2,1)}), bf16[32,64,2,128]{3,1,2,0:T(8,128)(2,1)S(1)}, u32[]{:S(2)}, u32[]{:S(2)}) async-start(bf16[32,64,2,128]{3,1,2,0:T(8,128)(2,1)} %copy.68), calls=%async_computation.3 | async-start | bytes 2097152 | tf_op jit(solution)/shard_map/all_to_all | solution.py:39
  174.8 2.1 %copy-start.1 = (bf16[3,512,128]{1,2,0:T(8,128)(2,1)S(1)}, bf16[3,512,128]{1,2,0:T(8,128)(2,1)}, u32[]{:S(2)}) copy-start(bf16[3,512,128]{1,2,0:T(8,128)(2,1)} %reduce-scatter.2.cloned.1.call-done) | copy-start | bytes 1179652
Sparse Core Ops, SparseCore 0:
  10.7 73.4 all-gather.1
  99.4 75.2 reduce-scatter.1
